TPU v7x, 256 devices: a whole 4x4x8 slice. The times are simulated.
256 devices in a mesh: row: 4 (over y), col: 16 (over z_hi, x, core), dep: 4 (over z_lo).
Axes of the slice: x: 4, y: 4, z: 8 (z_hi: 2, z_lo: 4; z = z_hi * 4 + z_lo), core: 2. Of those that a mesh axis runs over, the one named last changes fastest.
Arguments:
- grad_out: bfloat16 [4, 512, 12288], P('row', 'dep', 'col'), may hold values from -7 to 7
- out_weight: bfloat16 [8192, 12288], P('row', 'col'), may hold values from -0.09375 to 0.09375
- query_rows: bfloat16 [2048, 8192], P('dep', ('row', 'col')), may hold values from -6 to 6
- key_rows: bfloat16 [2048, 8192], P('dep', ('row', 'col')), may hold values from -6 to 6
- value_rows: bfloat16 [2048, 8192], P('dep', ('row', 'col')), may hold values from -7 to 7
- seg_lengths: int32 [8], replicated, may hold values from 1 to 1536, 2048 in all
Outputs:
- grad_weight: float32 [8192, 12288], P('row', 'col')
- grad_query: bfloat16 [2048, 8192], P('dep', ('row', 'col'))
- grad_key: bfloat16 [2048, 8192], P('dep', ('row', 'col'))
- grad_value: bfloat16 [2048, 8192], P('dep', ('row', 'col'))
All inputs are finite; a program needn't handle non-finite values.
Results may differ from a plain program's by a relative error of at most 0.029.
Values may be sent and summed in bfloat16 or wider, within the bound.
No kernel may reach another device: no remote copies, remote signals or barrier semaphores. Data moves between devices by JAX's collectives and lax.ppermute only.
A program may use at most 128 MiB of HBM per device.

v0:
```python
import math

import jax
import jax.numpy as jnp
from jax import lax
from jax.sharding import Mesh
from jax.sharding import PartitionSpec as P

NEG_FILL = -1e30
COL = ("zh", "x", "core")
DEP = "zl"


def segment_count(positions, seg_ends):
    return jnp.sum((positions[:, None] >= seg_ends[None, :]).astype(jnp.int32), axis=1)


def shift(x, axis, n, s):
    return lax.ppermute(x, axis, [(i, (i + s) % n) for i in range(n)])


def shift_open(x, axis, n, s):
    return lax.ppermute(x, axis, [(i, i + s) for i in range(n) if 0 <= i + s < n])


def roll_rows(x, amount, axis):
    size = x.shape[axis]
    doubled = jnp.concatenate([x, x], axis=axis)
    return lax.dynamic_slice_in_dim(doubled, (size - amount) % size, size, axis=axis)


def rolled_gather(x, axis, n, stack_axis=0):
    parts = [x] + [shift(x, axis, n, -s) for s in range(1, n)]
    return jnp.stack(parts, axis=stack_axis)


def pp_reduce_scatter(x, axis, n, dim):
    me = lax.axis_index(axis)
    acc = lax.dynamic_index_in_dim(x, me, dim, keepdims=False).astype(jnp.float32)
    for s in range(1, n):
        send = lax.dynamic_index_in_dim(x, (me + s) % n, dim, keepdims=False)
        acc = acc + shift(send, axis, n, s).astype(jnp.float32)
    return acc


def pp_reduce_scatter_cols(x, axis, n):
    me = lax.axis_index(axis)
    width = x.shape[1] // n
    acc = lax.dynamic_slice_in_dim(x, me * width, width, axis=1).astype(jnp.float32)
    for s in range(1, n):
        send = lax.dynamic_slice_in_dim(x, ((me + s) % n) * width, width, axis=1)
        acc = acc + shift(send, axis, n, s).astype(jnp.float32)
    return acc


def make_shards(n_zh, n_x, n_core, n_row, n_dep):
    def shards(grad_out, out_weight, query_rows, key_rows, value_rows, seg_lengths):
        n_tok, feat = grad_out.shape[1], grad_out.shape[2]
        tok_depth = n_row * n_tok
        head_dim = query_rows.shape[1]
        inv_root = 1.0 / math.sqrt(head_dim)
        me_r = lax.axis_index("row")
        me_d = lax.axis_index(DEP)
        local = grad_out[0]
        grad_rows = rolled_gather(local, "row", n_row).reshape(tok_depth, feat)

        kv = jnp.concatenate([key_rows, value_rows], axis=1)
        packed = jnp.concatenate([kv, local.reshape(-1, 2 * head_dim)], axis=0)
        packed_all = rolled_gather(packed, DEP, n_dep)
        kv_all = packed_all[:, :tok_depth].reshape(n_dep * tok_depth, 2 * head_dim)
        keys_all, values_all = kv_all[:, :head_dim], kv_all[:, head_dim:]
        by_depth = roll_rows(packed_all[:, tok_depth:].reshape(n_dep, n_tok, feat), me_d, 0)

        src_depth = (me_d + jnp.arange(n_dep, dtype=jnp.int32)) % n_dep
        key_pos = (
            (src_depth * tok_depth)[:, None] + jnp.arange(tok_depth, dtype=jnp.int32)[None, :]
        ).reshape(-1)
        seg_ends = jnp.cumsum(seg_lengths)
        key_seg = segment_count(key_pos, seg_ends)
        query_pos = me_d * tok_depth + jnp.arange(tok_depth, dtype=jnp.int32)
        query_seg = segment_count(query_pos, seg_ends)
        allowed = (query_seg[:, None] == key_seg[None, :]) & (
            key_pos[None, :] <= query_pos[:, None]
        )
        scores = (
            jnp.einsum("qh,kh->qk", query_rows, keys_all, preferred_element_type=jnp.float32)
            * inv_root
        )
        masked = jnp.where(allowed, scores, NEG_FILL)
        row_max = jnp.max(masked, axis=1, keepdims=True)
        exponent = jnp.where(allowed, jnp.exp(masked - row_max), 0.0)
        row_sum = jnp.sum(exponent, axis=1, keepdims=True)
        prob_full = exponent / row_sum
        prob_half = prob_full.astype(jnp.bfloat16)
        context = jnp.dot(prob_half, values_all, preferred_element_type=jnp.float32).astype(
            jnp.bfloat16
        )

        rows_all = rolled_gather(by_depth, "row", n_row, stack_axis=1)
        context = roll_rows(context, -me_r * n_tok, 0)

        weight_perm = jnp.transpose(
            out_weight.reshape(n_zh, n_x, n_core, head_dim, feat), (2, 1, 0, 3, 4)
        ).reshape(-1, feat)
        partial = jnp.einsum(
            "tf,hf->th", grad_rows, weight_perm, preferred_element_type=jnp.float32
        ).astype(jnp.bfloat16)
        partial = pp_reduce_scatter_cols(partial, "core", n_core).astype(jnp.bfloat16)
        context, partial = lax.optimization_barrier((context, partial))
        ctx_all = lax.all_gather(context[None], ("zh", DEP, "x", "core"), axis=0, tiled=True)
        ctx_all = ctx_all.reshape(n_zh, n_dep, n_x, n_core, tok_depth, head_dim)
        partial = pp_reduce_scatter_cols(partial, "x", n_x).astype(jnp.bfloat16)
        partial = pp_reduce_scatter_cols(partial, "zh", n_zh).astype(jnp.bfloat16)
        context_grad = roll_rows(partial, me_r * n_tok, 0)

        grad_prob = jnp.dot(context_grad, values_all.T, preferred_element_type=jnp.float32)
        delta_row = jnp.sum(prob_full * grad_prob, axis=1, keepdims=True)
        grad_score = (prob_full * (grad_prob - delta_row)).astype(jnp.bfloat16)
        grad_query = (
            jnp.dot(grad_score, keys_all, preferred_element_type=jnp.float32) * inv_root
        ).astype(jnp.bfloat16)
        key_partial = (
            jnp.einsum("qk,qh->kh", grad_score, query_rows, preferred_element_type=jnp.float32)
            * inv_root
        ).astype(jnp.bfloat16)
        value_partial = jnp.einsum(
            "qk,qh->kh", prob_half, context_grad, preferred_element_type=jnp.float32
        ).astype(jnp.bfloat16)
        kv_partial = jnp.concatenate([key_partial, value_partial], axis=1).reshape(
            n_dep, tok_depth, 2 * head_dim
        )
        kv_grad = kv_partial[0].astype(jnp.float32)
        for s in range(1, n_dep):
            kv_grad = kv_grad + shift_open(kv_partial[s], DEP, n_dep, s - n_dep).astype(
                jnp.float32
            )
        kv_grad = kv_grad.astype(jnp.bfloat16)
        grad_key, grad_value = kv_grad[:, :head_dim], kv_grad[:, head_dim:]

        grad_weight = None
        for depth in range(n_dep):
            piece = jnp.einsum(
                "zxcth,tf->zxchf",
                ctx_all[:, depth],
                rows_all[depth].reshape(tok_depth, feat),
                preferred_element_type=jnp.float32,
            )
            grad_weight = piece if grad_weight is None else grad_weight + piece
            if depth < n_dep - 1:
                grad_weight = lax.optimization_barrier(grad_weight)
        grad_weight = grad_weight.reshape(n_zh * n_x * n_core * head_dim, feat)
        return (grad_weight, grad_query, grad_key, grad_value)

    return shards


def solution(mesh):
    n_row, n_col, n_dep = mesh.shape["row"], mesh.shape["col"], mesh.shape["dep"]
    n_zh, n_core = 2, 2
    n_x = n_col // (n_zh * n_core)
    fine = Mesh(
        mesh.devices.reshape(n_row, n_zh, n_x, n_core, n_dep), ("row",) + COL + (DEP,)
    )
    in_specs = (
        P("row", DEP, COL),
        P("row", COL),
        P(DEP, ("row",) + COL),
        P(DEP, ("row",) + COL),
        P(DEP, ("row",) + COL),
        P(),
    )
    out_specs = (
        P("row", COL),
        P(DEP, ("row",) + COL),
        P(DEP, ("row",) + COL),
        P(DEP, ("row",) + COL),
    )
    return jax.shard_map(
        make_shards(n_zh, n_x, n_core, n_row, n_dep),
        mesh=fine,
        in_specs=in_specs,
        out_specs=out_specs,
        check_vma=False,
    )
```

profile of v0, /device:TPU:1, one launch (start us, length us, event | category | flops | bytes accessed | tf_op | source)
XLA Modules:
  0.0 189.5 jit_solution(15365920941142318406)
XLA Ops:
  7.2 2.2 %collective-permute-start.5 = (bf16[128,768]{1,0:T(8,128)(2,1)}, bf16[128,768]{1,0:T(8,128)(2,1)S(1)}, u32[]{:S(2)}, u32[]{:S(2)}) collective-permute-start(bf16[128,768]{1,0:T(8,128)(2,1)} %bitcast.110), channel_id=1, source_target_pairs={{0,64},{64,128},{128,192},{192,0},{1,65},{65,129},{129,193},{193,1... | collective-permute-start | bytes 589832 | tf_op jit(solution)/shard_map/ppermute | solution.py:19
  9.4 2.6 %collective-permute-start.4 = (bf16[128,768]{1,0:T(8,128)(2,1)}, bf16[128,768]{1,0:T(8,128)(2,1)S(1)}, u32[]{:S(2)}, u32[]{:S(2)}) collective-permute-start(bf16[128,768]{1,0:T(8,128)(2,1)} %bitcast.111), channel_id=1, source_target_pairs={{0,128},{64,192},{128,0},{192,64},{1,129},{65,193},{129,1},{193,65... | collective-permute-start | bytes 589832 | tf_op jit(solution)/shard_map/ppermute | solution.py:19
  14.2 1.8 fusion.24
  16.0 3.0 %collective-permute-start.1 = (bf16[896,256]{1,0:T(8,128)(2,1)}, bf16[896,256]{1,0:T(8,128)(2,1)S(1)}, u32[]{:S(2)}, u32[]{:S(2)}) collective-permute-start(bf16[896,256]{1,0:T(8,128)(2,1)} %get-tuple-element.35), channel_id=1, source_target_pairs={{0,2},{1,3},{2,0},{3,1},{4,6},{5,7},{6,4},{7,5},{8,10},{9,11},{10,... | collective-permute-start | bytes 1376264 | tf_op jit(solution)/shard_map/ppermute | solution.py:19
  21.3 3.8 %copy.41 = bf16[2,4,2,128,768]{4,3,2,1,0:T(8,128)(2,1)} copy(bf16[2,4,2,128,768]{4,3,0,1,2:T(8,128)(2,1)} %bitcast.102) | data formatting | bytes 6291456 | tf_op jit(solution)/shard_map/transpose | solution.py:102
  27.4 3.7 %convolution_convert_fusion = bf16[512,2048]{1,0:T(8,128)(2,1)S(1)} fusion(bf16[512,768]{1,0:T(8,128)(2,1)S(1)} %bitcast.113, bf16[2048,768]{1,0:T(8,128)(2,1)} %bitcast.103), kind=kOutput, calls=%fused_computation.7 | convolution fusion | flops 1611661312 | bytes 6029312 | tf_op jit(solution)/shard_map/tf,hf->th/dot_general | solution.py:105
  31.2 2.3 %collective-permute-start.6 = (bf16[512,1024]{1,0:T(8,128)(2,1)S(1)}, bf16[512,1024]{1,0:T(8,128)(2,1)}, u32[]{:S(2)}, u32[]{:S(2)}) collective-permute-start(bf16[512,1024]{1,0:T(8,128)(2,1)S(1)} %constant_dynamic-slice_fusion.4), channel_id=1, source_target_pairs={{0,4},{4,0},{1,5},{5,1},{2,6},{6,2},{3,7},{7,3},{8,12},{12,8},{9,1... | collective-permute-start | bytes 3145736 | tf_op jit(solution)/shard_map/ppermute | solution.py:19
  33.5 5.1 %collective-permute-done.1 = bf16[896,256]{1,0:T(8,128)(2,1)S(1)} collective-permute-done((bf16[896,256]{1,0:T(8,128)(2,1)}, bf16[896,256]{1,0:T(8,128)(2,1)S(1)}, u32[]{:S(2)}, u32[]{:S(2)}) %collective-permute-start.1) | collective-permute-done | bytes 458784 | tf_op jit(solution)/shard_map/ppermute | solution.py:19
  38.6 11.0 %collective-permute-done.2 = bf16[896,256]{1,0:T(8,128)(2,1)S(1)} collective-permute-done((bf16[896,256]{1,0:T(8,128)(2,1)}, bf16[896,256]{1,0:T(8,128)(2,1)S(1)}, u32[]{:S(2)}, u32[]{:S(2)}) %collective-permute-start.2) | collective-permute-done | bytes 458784 | tf_op jit(solution)/shard_map/ppermute | solution.py:19
  51.9 1.8 fusion.3
  53.6 1.9 %fusion.2 = f32[512,2048]{0,1:T(8,128)S(1)} fusion(f32[2048,512]{1,0:T(8,128)S(1)} %get-tuple-element.39, f32[512]{0:T(512)S(1)} %fusion.3, f32[512]{0:T(512)S(1)} %get-tuple-element.38, s32[512]{0:T(512)S(1)} %copy-done.14, s32[512]{0:T(512)S(1)} %convert_reduce_fusion.1, s32[2048]{0:T(1024)S(1)} %bitcast.117, s32[2048]{0:T(1024)S(1)} %convert_reduce_fusion), kind=kLoop, calls=%fused_computation.14 | loop fusion | flops 8388608 | bytes 8413184 | tf_op jit(solution)/shard_map/div | solution.py:93
  55.6 2.0 %copy-done.2 = f32[512,2048]{0,1:T(8,128)} copy-done((f32[512,2048]{0,1:T(8,128)}, f32[512,2048]{0,1:T(8,128)S(1)}, u32[]{:S(2)}) %copy-start.2) | copy-done | bytes 4194328
  59.6 1.9 %add_convert_fusion = bf16[512,1024]{1,0:T(8,128)(2,1)S(1)} fusion(bf16[512,1024]{1,0:T(8,128)(2,1)} %collective-permute-done.6, bf16[512,2048]{1,0:T(8,128)(2,1)} %copy-done.8, s32[]{:T(128)S(6)} %select_n.90), kind=kLoop, calls=%fused_computation.21 | loop fusion | flops 2097152 | bytes 3145732 | tf_op jit(solution)/shard_map/convert_element_type | solution.py:108
  61.6 2.0 %pad_maximum_fusion.2 = bf16[4,384,256]{2,1,0:T(8,128)(2,1)} fusion(bf16[1,896,256]{2,1,0:T(8,128)(2,1)} %bitcast.109, bf16[1,896,256]{2,1,0:T(8,128)(2,1)S(1)} %bitcast.105, bf16[1,896,256]{2,1,0:T(8,128)(2,1)} %bitcast.107, bf16[1,896,256]{2,1,0:T(8,128)(2,1)S(1)} %get-tuple-element.34), kind=kLoop, calls=%fused_computation.37 | loop fusion | flops 3145728 | bytes 2621440 | tf_op jit(solution)/shard_map/slice | solution.py:72
  63.6 1.5 reshape.121
  66.6 1.9 collective-permute-start.8
  70.2 1.5 collective-permute-start.12
  71.6 11.6 %collective-permute-done.7 = bf16[4,128,768]{2,1,0:T(8,128)(2,1)} collective-permute-done((bf16[4,128,768]{2,1,0:T(8,128)(2,1)}, bf16[4,128,768]{2,1,0:T(8,128)(2,1)}, u32[]{:S(2)}, u32[]{:S(2)}) %collective-permute-start.7) | collective-permute-done | bytes 786464 | tf_op jit(solution)/shard_map/ppermute | solution.py:19
  83.2 2.7 %collective-permute-start.11 = (bf16[512,256]{1,0:T(8,128)(2,1)S(1)}, bf16[512,256]{1,0:T(8,128)(2,1)S(1)}, u32[]{:S(2)}, u32[]{:S(2)}) collective-permute-start(bf16[512,256]{1,0:T(8,128)(2,1)S(1)} %get-tuple-element.33), channel_id=1, source_target_pairs={{0,16},{8,24},{16,0},{24,8},{1,17},{9,25},{17,1},{25,9},{2,18},{10... | collective-permute-start | bytes 786440 | tf_op jit(solution)/shard_map/ppermute | solution.py:19
  85.9 18.8 %collective-permute-done.9 = bf16[4,128,768]{2,1,0:T(8,128)(2,1)} collective-permute-done((bf16[4,128,768]{2,1,0:T(8,128)(2,1)}, bf16[4,128,768]{2,1,0:T(8,128)(2,1)}, u32[]{:S(2)}, u32[]{:S(2)}) %collective-permute-start.9) | collective-permute-done | bytes 786464 | tf_op jit(solution)/shard_map/ppermute | solution.py:19
  104.7 1.8 pad_maximum_fusion
  106.8 5.2 %collective-permute-start.13 = (bf16[512,128]{1,0:T(8,128)(2,1)S(1)}, bf16[512,128]{1,0:T(8,128)(2,1)S(1)}, u32[]{:S(2)}, u32[]{:S(2)}) collective-permute-start(bf16[512,128]{1,0:T(8,128)(2,1)S(1)} %constant_dynamic-slice_fusion), channel_id=1, source_target_pairs={{0,32},{32,0},{1,33},{33,1},{2,34},{34,2},{3,35},{35,3},{4,36},{36... | collective-permute-start | bytes 393224 | tf_op jit(solution)/shard_map/ppermute | solution.py:19
  113.1 2.2 %collective-permute-done.13 = bf16[512,128]{1,0:T(8,128)(2,1)S(1)} collective-permute-done((bf16[512,128]{1,0:T(8,128)(2,1)S(1)}, bf16[512,128]{1,0:T(8,128)(2,1)S(1)}, u32[]{:S(2)}, u32[]{:S(2)}) %collective-permute-start.13) | collective-permute-done | bytes 131104 | tf_op jit(solution)/shard_map/ppermute | solution.py:19
  117.6 2.2 %multiply_convert_fusion = bf16[512,2048]{0,1:T(8,128)(2,1)S(1)} fusion(f32[512,2048]{0,1:T(8,128)S(1)} %get-tuple-element.41, f32[512]{0:T(512)S(1)} %get-tuple-element.40, f32[512]{0:T(512)S(1)} %copy-done.21, f32[512]{0:T(512)S(1)} %copy-done.19, f32[2048,512]{1,0:T(8,128)S(1)} %copy-done.5, s32[512]{0:T(512)S(1)} %copy-done.15, s32[2048]{0:T(1024)S(1)} %bitcast.118, ...), kind=kLoop, calls=%fused_computation.1 | loop fusion | flops 11534336 | bytes 10512384 | tf_op jit(solution)/shard_map/convert_element_type | solution.py:118
  124.5 1.5 collective-permute-start.15
  127.4 12.8 %collective-permute-done.14 = bf16[512,256]{0,1:T(8,128)(2,1)S(1)} collective-permute-done((bf16[512,256]{0,1:T(8,128)(2,1)S(1)}, bf16[512,256]{0,1:T(8,128)(2,1)S(1)}, u32[]{:S(2)}, u32[]{:S(2)}) %collective-permute-start.14) | collective-permute-done | bytes 262176 | tf_op jit(solution)/shard_map/ppermute | solution.py:23
  140.2 11.2 %collective-permute-done.16 = bf16[512,256]{0,1:T(8,128)(2,1)S(1)} collective-permute-done((bf16[512,256]{0,1:T(8,128)(2,1)S(1)}, bf16[512,256]{0,1:T(8,128)(2,1)S(1)}, u32[]{:S(2)}, u32[]{:S(2)}) %collective-permute-start.16) | collective-permute-done | bytes 262176 | tf_op jit(solution)/shard_map/ppermute | solution.py:23
  151.4 17.1 %collective-permute-done.15 = bf16[512,256]{0,1:T(8,128)(2,1)S(1)} collective-permute-done((bf16[512,256]{0,1:T(8,128)(2,1)S(1)}, bf16[512,256]{0,1:T(8,128)(2,1)S(1)}, u32[]{:S(2)}, u32[]{:S(2)}) %collective-permute-start.15) | collective-permute-done | bytes 262176 | tf_op jit(solution)/shard_map/ppermute | solution.py:23
  170.3 3.6 %fusion.4 = f32[2,4,2,128,768]{4,3,2,1,0:T(8,128)S(1)} fusion(bf16[512,768,1,1,1]{1,0,4,3,2:T(8,128)(2,1)S(1)} %bitcast.101, bf16[2,4,4,2,512,128]{5,4,3,2,1,0:T(8,128)(2,1)} %bitcast.89), kind=kOutput, calls=%fused_computation.20 | convolution fusion | flops 1610612736 | bytes 9175040 | tf_op jit(solution)/shard_map/zxcth,tf->zxchf/dot_general | solution.py:142
  174.4 1.8 convolution_add_fusion.2
  176.3 1.8 convolution_add_fusion.1
  178.1 4.5 %convolution_add_fusion = f32[2,4,2,128,768]{4,3,2,1,0:T(8,128)} fusion(f32[2,4,2,128,768]{4,3,2,1,0:T(8,128)S(1)} %convolution_add_fusion.1, bf16[512,768,1,1,1]{1,0,4,3,2:T(8,128)(2,1)S(1)} %bitcast.98, bf16[2,4,4,2,512,128]{5,4,3,2,1,0:T(8,128)(2,1)S(1)} %bitcast.92), kind=kOutput, calls=%fused_computation.8 | convolution fusion | flops 1612185600 | bytes 15466496 | tf_op jit(solution)/shard_map/zxcth,tf->zxchf/dot_general | solution.py:142
  (94 shorter events, 26.0 us)
Async XLA Ops:
  7.2 43.6 %copy-start = (bf16[512,128]{1,0:T(8,128)(2,1)S(1)}, bf16[512,128]{1,0:T(8,128)(2,1)}, u32[]{:S(2)}) copy-start(bf16[512,128]{1,0:T(8,128)(2,1)} %param.8) | copy-start | bytes 393220
  7.2 19.2 %copy-start.11 = (bf16[1,128,768]{2,1,0:T(8,128)(2,1)S(1)}, bf16[1,128,768]{2,1,0:T(8,128)(2,1)}, u32[]{:S(2)}) copy-start(bf16[1,128,768]{2,1,0:T(8,128)(2,1)} %param.6) | copy-start | bytes 589828
  7.2 163.1 %all-gather.3.cloned.1.call-start = ((), (), s32[]{:S(2)}) async-start(), calls=%async_computation | async-start | bytes 8519680 | tf_op jit(solution)/shard_map/all_gather | solution.py:110
  7.2 18.0 %collective-permute-start.5 = (bf16[128,768]{1,0:T(8,128)(2,1)}, bf16[128,768]{1,0:T(8,128)(2,1)S(1)}, u32[]{:S(2)}, u32[]{:S(2)}) collective-permute-start(bf16[128,768]{1,0:T(8,128)(2,1)} %bitcast.110), channel_id=1, source_target_pairs={{0,64},{64,128},{128,192},{192,0},{1,65},{65,129},{129,193},{193,1... | collective-permute-start | bytes 589832 | tf_op jit(solution)/shard_map/ppermute | solution.py:19
  9.4 16.2 %collective-permute-start.4 = (bf16[128,768]{1,0:T(8,128)(2,1)}, bf16[128,768]{1,0:T(8,128)(2,1)S(1)}, u32[]{:S(2)}, u32[]{:S(2)}) collective-permute-start(bf16[128,768]{1,0:T(8,128)(2,1)} %bitcast.111), channel_id=1, source_target_pairs={{0,128},{64,192},{128,0},{192,64},{1,129},{65,193},{129,1},{193,65... | collective-permute-start | bytes 589832 | tf_op jit(solution)/shard_map/ppermute | solution.py:19
  12.1 13.6 %collective-permute-start.3 = (bf16[128,768]{1,0:T(8,128)(2,1)}, bf16[128,768]{1,0:T(8,128)(2,1)S(1)}, u32[]{:S(2)}, u32[]{:S(2)}) collective-permute-start(bf16[128,768]{1,0:T(8,128)(2,1)} %bitcast.112), channel_id=1, source_target_pairs={{0,192},{64,0},{128,64},{192,128},{1,193},{65,1},{129,65},{193,129... | collective-permute-start | bytes 589832 | tf_op jit(solution)/shard_map/ppermute | solution.py:19
  16.0 22.6 %collective-permute-start.1 = (bf16[896,256]{1,0:T(8,128)(2,1)}, bf16[896,256]{1,0:T(8,128)(2,1)S(1)}, u32[]{:S(2)}, u32[]{:S(2)}) collective-permute-start(bf16[896,256]{1,0:T(8,128)(2,1)} %get-tuple-element.35), channel_id=1, source_target_pairs={{0,2},{1,3},{2,0},{3,1},{4,6},{5,7},{6,4},{7,5},{8,10},{9,11},{10,... | collective-permute-start | bytes 1376264 | tf_op jit(solution)/shard_map/ppermute | solution.py:19
  19.0 19.6 %collective-permute-start = (bf16[896,256]{1,0:T(8,128)(2,1)}, bf16[896,256]{1,0:T(8,128)(2,1)S(1)}, u32[]{:S(2)}, u32[]{:S(2)}) collective-permute-start(bf16[896,256]{1,0:T(8,128)(2,1)} %get-tuple-element.35), channel_id=1, source_target_pairs={{0,3},{1,0},{2,1},{3,2},{4,7},{5,4},{6,5},{7,6},{8,11},{9,8},{10,9... | collective-permute-start | bytes 1376264 | tf_op jit(solution)/shard_map/ppermute | solution.py:19
  21.2 4.5 %copy-start.13 = (s32[512]{0:T(512)}, s32[512]{0:T(512)S(1)}, u32[]{:S(2)}) copy-start(s32[512]{0:T(512)S(1)} %iota_add_fusion) | copy-start | bytes 6148
  25.2 28.4 %copy-start.16 = (s32[512]{0:T(512)}, s32[512]{0:T(512)S(1)}, u32[]{:S(2)}) copy-start(s32[512]{0:T(512)S(1)} %convert_reduce_fusion.1) | copy-start | bytes 6148
  25.3 24.4 %collective-permute-start.2 = (bf16[896,256]{1,0:T(8,128)(2,1)}, bf16[896,256]{1,0:T(8,128)(2,1)S(1)}, u32[]{:S(2)}, u32[]{:S(2)}) collective-permute-start(bf16[896,256]{1,0:T(8,128)(2,1)} %get-tuple-element.35), channel_id=1, source_target_pairs={{0,1},{1,2},{2,3},{3,0},{4,5},{5,6},{6,7},{7,4},{8,9},{9,10},{10,1... | collective-permute-start | bytes 1376264 | tf_op jit(solution)/shard_map/ppermute | solution.py:19
  31.1 20.7 %copy-start.8 = (bf16[512,2048]{1,0:T(8,128)(2,1)}, bf16[512,2048]{1,0:T(8,128)(2,1)S(1)}, u32[]{:S(2)}) copy-start(bf16[512,2048]{1,0:T(8,128)(2,1)S(1)} %convolution_convert_fusion) | copy-start | bytes 6291460
  31.1 19.6 %copy-start.14 = (s32[512]{0:T(512)S(1)}, s32[512]{0:T(512)}, u32[]{:S(2)}) copy-start(s32[512]{0:T(512)} %copy-done.13) | copy-start | bytes 6148
  31.2 28.4 %collective-permute-start.6 = (bf16[512,1024]{1,0:T(8,128)(2,1)S(1)}, bf16[512,1024]{1,0:T(8,128)(2,1)}, u32[]{:S(2)}, u32[]{:S(2)}) collective-permute-start(bf16[512,1024]{1,0:T(8,128)(2,1)S(1)} %constant_dynamic-slice_fusion.4), channel_id=1, source_target_pairs={{0,4},{4,0},{1,5},{5,1},{2,6},{6,2},{3,7},{7,3},{8,12},{12,8},{9,1... | collective-permute-start | bytes 3145736 | tf_op jit(solution)/shard_map/ppermute | solution.py:19
  38.6 11.0 %copy-start.9 = (bf16[896,256]{1,0:T(8,128)(2,1)}, bf16[896,256]{1,0:T(8,128)(2,1)S(1)}, u32[]{:S(2)}) copy-start(bf16[896,256]{1,0:T(8,128)(2,1)S(1)} %collective-permute-done) | copy-start | bytes 1376260
  51.8 3.8 %copy-start.4 = (f32[2048,512]{1,0:T(8,128)}, f32[2048,512]{1,0:T(8,128)S(1)}, u32[]{:S(2)}) copy-start(f32[2048,512]{1,0:T(8,128)S(1)} %get-tuple-element.39) | copy-start | bytes 12582916
  51.8 3.8 %copy-start.18 = (f32[512]{0:T(512)}, f32[512]{0:T(512)S(1)}, u32[]{:S(2)}) copy-start(f32[512]{0:T(512)S(1)} %get-tuple-element.38) | copy-start | bytes 6148
  66.3 16.9 %collective-permute-start.7 = (bf16[4,128,768]{2,1,0:T(8,128)(2,1)}, bf16[4,128,768]{2,1,0:T(8,128)(2,1)}, u32[]{:S(2)}, u32[]{:S(2)}) collective-permute-start(bf16[4,128,768]{2,1,0:T(8,128)(2,1)} %fusion.8), channel_id=1, source_target_pairs={{0,192},{64,0},{128,64},{192,128},{1,193},{65,1},{129,65},{193,129... | collective-permute-start | bytes 2359304 | tf_op jit(solution)/shard_map/ppermute | solution.py:19
  66.6 19.3 %collective-permute-start.8 = (bf16[4,128,768]{2,1,0:T(8,128)(2,1)}, bf16[4,128,768]{2,1,0:T(8,128)(2,1)}, u32[]{:S(2)}, u32[]{:S(2)}) collective-permute-start(bf16[4,128,768]{2,1,0:T(8,128)(2,1)} %fusion.8), channel_id=1, source_target_pairs={{0,128},{64,192},{128,0},{192,64},{1,129},{65,193},{129,1},{193,65... | collective-permute-start | bytes 2359304 | tf_op jit(solution)/shard_map/ppermute | solution.py:19
  68.5 36.3 %collective-permute-start.9 = (bf16[4,128,768]{2,1,0:T(8,128)(2,1)}, bf16[4,128,768]{2,1,0:T(8,128)(2,1)}, u32[]{:S(2)}, u32[]{:S(2)}) collective-permute-start(bf16[4,128,768]{2,1,0:T(8,128)(2,1)} %fusion.8), channel_id=1, source_target_pairs={{0,64},{64,128},{128,192},{192,0},{1,65},{65,129},{129,193},{193,1... | collective-permute-start | bytes 2359304 | tf_op jit(solution)/shard_map/ppermute | solution.py:19
  68.9 37.7 %collective-permute-start.10 = (bf16[512,256]{1,0:T(8,128)(2,1)S(1)}, bf16[512,256]{1,0:T(8,128)(2,1)S(1)}, u32[]{:S(2)}, u32[]{:S(2)}) collective-permute-start(bf16[512,256]{1,0:T(8,128)(2,1)S(1)} %get-tuple-element.31), channel_id=1, source_target_pairs={{0,8},{8,16},{16,24},{24,0},{1,9},{9,17},{17,25},{25,1},{2,10},{10... | collective-permute-start | bytes 786440 | tf_op jit(solution)/shard_map/ppermute | solution.py:19
  70.2 36.4 %collective-permute-start.12 = (bf16[512,256]{1,0:T(8,128)(2,1)S(1)}, bf16[512,256]{1,0:T(8,128)(2,1)S(1)}, u32[]{:S(2)}, u32[]{:S(2)}) collective-permute-start(bf16[512,256]{1,0:T(8,128)(2,1)S(1)} %get-tuple-element.32), channel_id=1, source_target_pairs={{0,24},{8,0},{16,8},{24,16},{1,25},{9,1},{17,9},{25,17},{2,26},{10... | collective-permute-start | bytes 786440 | tf_op jit(solution)/shard_map/ppermute | solution.py:19
  83.2 23.4 %collective-permute-start.11 = (bf16[512,256]{1,0:T(8,128)(2,1)S(1)}, bf16[512,256]{1,0:T(8,128)(2,1)S(1)}, u32[]{:S(2)}, u32[]{:S(2)}) collective-permute-start(bf16[512,256]{1,0:T(8,128)(2,1)S(1)} %get-tuple-element.33), channel_id=1, source_target_pairs={{0,16},{8,24},{16,0},{24,8},{1,17},{9,25},{17,1},{25,9},{2,18},{10... | collective-permute-start | bytes 786440 | tf_op jit(solution)/shard_map/ppermute | solution.py:19
  106.6 8.8 %copy-start.3 = (f32[512,2048]{0,1:T(8,128)S(1)}, f32[512,2048]{0,1:T(8,128)}, u32[]{:S(2)}) copy-start(f32[512,2048]{0,1:T(8,128)} %copy-done.2) | copy-start | bytes 12582916
  106.8 8.6 %collective-permute-start.13 = (bf16[512,128]{1,0:T(8,128)(2,1)S(1)}, bf16[512,128]{1,0:T(8,128)(2,1)S(1)}, u32[]{:S(2)}, u32[]{:S(2)}) collective-permute-start(bf16[512,128]{1,0:T(8,128)(2,1)S(1)} %constant_dynamic-slice_fusion), channel_id=1, source_target_pairs={{0,32},{32,0},{1,33},{33,1},{2,34},{34,2},{3,35},{35,3},{4,36},{36... | collective-permute-start | bytes 393224 | tf_op jit(solution)/shard_map/ppermute | solution.py:19
  115.4 2.2 %copy-start.5 = (f32[2048,512]{1,0:T(8,128)S(1)}, f32[2048,512]{1,0:T(8,128)}, u32[]{:S(2)}) copy-start(f32[2048,512]{1,0:T(8,128)} %copy-done.4) | copy-start | bytes 12582916
  121.9 18.3 %collective-permute-start.14 = (bf16[512,256]{0,1:T(8,128)(2,1)S(1)}, bf16[512,256]{0,1:T(8,128)(2,1)S(1)}, u32[]{:S(2)}, u32[]{:S(2)}) collective-permute-start(bf16[512,256]{0,1:T(8,128)(2,1)S(1)} %get-tuple-element.28), channel_id=1, source_target_pairs={{3,0},{7,4},{11,8},{15,12},{19,16},{23,20},{27,24},{31,28},{35,32}... | collective-permute-start | bytes 786440 | tf_op jit(solution)/shard_map/ppermute | solution.py:23
  123.2 28.2 %collective-permute-start.16 = (bf16[512,256]{0,1:T(8,128)(2,1)S(1)}, bf16[512,256]{0,1:T(8,128)(2,1)S(1)}, u32[]{:S(2)}, u32[]{:S(2)}) collective-permute-start(bf16[512,256]{0,1:T(8,128)(2,1)S(1)} %get-tuple-element.29), channel_id=1, source_target_pairs={{1,0},{2,1},{3,2},{5,4},{6,5},{7,6},{9,8},{10,9},{11,10},{13,12},{... | collective-permute-start | bytes 786440 | tf_op jit(solution)/shard_map/ppermute | solution.py:23
  124.5 44.1 %collective-permute-start.15 = (bf16[512,256]{0,1:T(8,128)(2,1)S(1)}, bf16[512,256]{0,1:T(8,128)(2,1)S(1)}, u32[]{:S(2)}, u32[]{:S(2)}) collective-permute-start(bf16[512,256]{0,1:T(8,128)(2,1)S(1)} %get-tuple-element.30), channel_id=1, source_target_pairs={{2,0},{3,1},{6,4},{7,5},{10,8},{11,9},{14,12},{15,13},{18,16},{19,... | collective-permute-start | bytes 786440 | tf_op jit(solution)/shard_map/ppermute | solution.py:23
  170.3 4.0 %copy-start.6 = (bf16[32768,128]{1,0:T(8,128)(2,1)S(1)}, bf16[32768,128]{1,0:T(8,128)(2,1)}, u32[]{:S(2)}) copy-start(bf16[32768,128]{1,0:T(8,128)(2,1)} %all-gather.3.cloned.1.call-done) | copy-start | bytes 25165828
  170.3 4.1 %copy-start.7 = (bf16[1,4,128,768]{3,2,1,0:T(8,128)(2,1)S(1)}, bf16[1,4,128,768]{3,2,1,0:T(8,128)(2,1)}, u32[]{:S(2)}) copy-start(bf16[1,4,128,768]{3,2,1,0:T(8,128)(2,1)} %get-tuple-element.26) | copy-start | bytes 2359300
  178.1 4.6 %copy-start.1 = (bf16[512,128]{1,0:T(8,128)(2,1)S(1)}, bf16[512,128]{1,0:T(8,128)(2,1)}, u32[]{:S(2)}) copy-start(bf16[512,128]{1,0:T(8,128)(2,1)} %param.8) | copy-start | bytes 393220
  (8 other events, 14.1 us)
Sparse Core Ops, SparseCore 0:
  61.7 107.3 all-gather.2
where the time goes:
time: 190 us
  waiting for transfers between devices  90 us (47%)
  starting transfers between devices  29.8 us (16%)
  matrix products  22 us (12%)
  other arithmetic  18.9 us (10%)
  between operations  14.5 us (8%)
  local copies, waits for them, and re-layouts  14.4 us (8%)
    ppermute x14, waiting for transfers between devices, shift(): return lax.ppermute(x, axis, [(i, (i + s) % n) for i in range(n)])  48.8 us
    ppermute x3, waiting for transfers between devices, shift_open(): lax.ppermute(x, axis, [(i, i + s) for i in range(n) if 0 <= i + s < n])  41.1 us
    ppermute x14, starting transfers between devices, shift(): return lax.ppermute(x, axis, [(i, (i + s) % n) for i in range(n)])  25.7 us
    dot_general x4, matrix products, shards(): jnp.einsum('zxcth,tf->zxchf', ctx_all[:, depth], rows_all[depth].reshape(...  11.8 us
    unnamed x47, local copies, waits for them, and re-layouts  6.54 us
    another operation x5, other arithmetic, rolled_gather(): return jnp.stack(parts, axis=stack_axis)  5.16 us
    ppermute x3, starting transfers between devices, shift_open(): lax.ppermute(x, axis, [(i, i + s) for i in range(n) if 0 <= i + s < n])  4.1 us
    transpose x1, local copies, waits for them, and re-layouts, shards(): jnp.transpose(out_weight.reshape(n_zh, n_x, n_core, head_dim, feat), (2,...  3.83 us
  transfers between devices with their start and end apart: 18, of which 8 were waited for; matrix products, arithmetic and copies ran while one was open for 19% of the time, Pallas kernels for 0%

commit v1 on v0

--- a/solution.py
+++ b/solution.py
@@ -7,6 +7,7 @@
 from jax.sharding import PartitionSpec as P
 
 NEG_FILL = -1e30
+FAR = 1 << 30
 COL = ("zh", "x", "core")
 DEP = "zl"
 
@@ -65,15 +66,16 @@
         grad_rows = rolled_gather(local, "row", n_row).reshape(tok_depth, feat)
 
         kv = jnp.concatenate([key_rows, value_rows], axis=1)
-        packed = jnp.concatenate([kv, local.reshape(-1, 2 * head_dim)], axis=0)
-        packed_all = rolled_gather(packed, DEP, n_dep)
-        kv_all = packed_all[:, :tok_depth].reshape(n_dep * tok_depth, 2 * head_dim)
+        kv_all = jnp.stack(
+            [kv] + [shift_open(kv, DEP, n_dep, t) for t in range(1, n_dep)], axis=0
+        ).reshape(n_dep * tok_depth, 2 * head_dim)
         keys_all, values_all = kv_all[:, :head_dim], kv_all[:, head_dim:]
-        by_depth = roll_rows(packed_all[:, tok_depth:].reshape(n_dep, n_tok, feat), me_d, 0)
+        by_depth = roll_rows(rolled_gather(local, DEP, n_dep), me_d, 0)
 
-        src_depth = (me_d + jnp.arange(n_dep, dtype=jnp.int32)) % n_dep
+        src_depth = me_d - jnp.arange(n_dep, dtype=jnp.int32)
         key_pos = (
-            (src_depth * tok_depth)[:, None] + jnp.arange(tok_depth, dtype=jnp.int32)[None, :]
+            jnp.where(src_depth >= 0, src_depth * tok_depth, FAR)[:, None]
+            + jnp.arange(tok_depth, dtype=jnp.int32)[None, :]
         ).reshape(-1)
         seg_ends = jnp.cumsum(seg_lengths)
         key_seg = segment_count(key_pos, seg_ends)
@@ -131,9 +133,7 @@
         )
         kv_grad = kv_partial[0].astype(jnp.float32)
         for s in range(1, n_dep):
-            kv_grad = kv_grad + shift_open(kv_partial[s], DEP, n_dep, s - n_dep).astype(
-                jnp.float32
-            )
+            kv_grad = kv_grad + shift_open(kv_partial[s], DEP, n_dep, -s).astype(jnp.float32)
         kv_grad = kv_grad.astype(jnp.bfloat16)
         grad_key, grad_value = kv_grad[:, :head_dim], kv_grad[:, head_dim:]
 

time: 190 us -> 187 us (0.984)
  starting transfers between devices: 29.8 us -> 47.7 us
  waiting for transfers between devices: 90 us -> 74 us
  other arithmetic: 18.9 us -> 13.1 us
    ppermute x3 -> x6, waiting for transfers between devices: 41.1 us -> 19.1 us  [shift_open(): lax.ppermute(x, axis, [(i, i + s) for i in range(n) if 0 <= i + s < n])]
    ppermute x3 -> x6, starting transfers between devices: 4.1 us -> 14.6 us  [shift_open(): lax.ppermute(x, axis, [(i, i + s) for i in range(n) if 0 <= i + s < n])]
    ppermute x14, starting transfers between devices: 25.7 us -> 33.1 us  [shift(): return lax.ppermute(x, axis, [(i, (i + s) % n) for i in range(n)])]
    ppermute x14, waiting for transfers between devices: 48.8 us -> 54.9 us  [shift(): return lax.ppermute(x, axis, [(i, (i + s) % n) for i in range(n)])]
    another operation x5 -> x2, other arithmetic: 5.16 us -> 1.67 us  [rolled_gather(): return jnp.stack(parts, axis=stack_axis)]
    slice x1 -> x0, other arithmetic: 2.01 us -> none  [shards(): packed_all[:, tok_depth:].reshape(n_dep, n_tok, feat)]
    unnamed x47 -> x51, local copies, waits for them, and re-layouts: 6.54 us -> 7.34 us
  transfers between devices with their start and end apart: 18 -> 21, of which waited for: 8 -> 8; matrix products, arithmetic and copies ran while one was open for 19% -> 17% of each run, Pallas kernels for 0% -> 0%
where the time goes in v1:
time: 187 us
  waiting for transfers between devices  74 us (40%)
  starting transfers between devices  47.7 us (26%)
  matrix products  22 us (12%)
  local copies, waits for them, and re-layouts  15.7 us (8%)
  between operations  14.6 us (8%)
  other arithmetic  13.1 us (7%)
    ppermute x14, waiting for transfers between devices, shift(): return lax.ppermute(x, axis, [(i, (i + s) % n) for i in range(n)])  54.9 us
    ppermute x14, starting transfers between devices, shift(): return lax.ppermute(x, axis, [(i, (i + s) % n) for i in range(n)])  33.1 us
    ppermute x6, waiting for transfers between devices, shift_open(): lax.ppermute(x, axis, [(i, i + s) for i in range(n) if 0 <= i + s < n])  19.1 us
    ppermute x6, starting transfers between devices, shift_open(): lax.ppermute(x, axis, [(i, i + s) for i in range(n) if 0 <= i + s < n])  14.6 us
    dot_general x4, matrix products, shards(): jnp.einsum('zxcth,tf->zxchf', ctx_all[:, depth], rows_all[depth].reshape(...  11.8 us
    unnamed x51, local copies, waits for them, and re-layouts  7.34 us
    transpose x1, local copies, waits for them, and re-layouts, shards(): jnp.transpose(out_weight.reshape(n_zh, n_x, n_core, head_dim, feat), (2,...  3.83 us
  transfers between devices with their start and end apart: 21, of which 8 were waited for; matrix products, arithmetic and copies ran while one was open for 17% of the time, Pallas kernels for 0%

profile of v1, /device:TPU:1, one launch (start us, length us, event | category | flops | bytes accessed | tf_op | source)
XLA Modules:
  0.0 187.0 jit_solution(14630378323412586293)
XLA Ops:
  7.2 2.2 %collective-permute-start.5 = (bf16[128,768]{1,0:T(8,128)(2,1)}, bf16[128,768]{1,0:T(8,128)(2,1)S(1)}, u32[]{:S(2)}, u32[]{:S(2)}) collective-permute-start(bf16[128,768]{1,0:T(8,128)(2,1)} %bitcast.108), channel_id=1, source_target_pairs={{0,64},{64,128},{128,192},{192,0},{1,65},{65,129},{129,193},{193,1... | collective-permute-start | bytes 589832 | tf_op jit(solution)/shard_map/ppermute | solution.py:20
  9.4 2.6 %collective-permute-start.4 = (bf16[128,768]{1,0:T(8,128)(2,1)}, bf16[128,768]{1,0:T(8,128)(2,1)S(1)}, u32[]{:S(2)}, u32[]{:S(2)}) collective-permute-start(bf16[128,768]{1,0:T(8,128)(2,1)} %bitcast.109), channel_id=1, source_target_pairs={{0,128},{64,192},{128,0},{192,64},{1,129},{65,193},{129,1},{193,65... | collective-permute-start | bytes 589832 | tf_op jit(solution)/shard_map/ppermute | solution.py:20
  15.0 7.0 %collective-permute-start.2 = (bf16[512,256]{1,0:T(8,128)(2,1)S(1)}, bf16[512,256]{1,0:T(8,128)(2,1)}, u32[]{:S(2)}, u32[]{:S(2)}) collective-permute-start(bf16[512,256]{1,0:T(8,128)(2,1)S(1)} %constant_dynamic-update-slice_fusion), channel_id=1, source_target_pairs={{0,3},{4,7},{8,11},{12,15},{16,19},{20,23},{24,27},{28,31},{32,35}... | collective-permute-start | bytes 786440 | tf_op jit(solution)/shard_map/ppermute | solution.py:24
  22.0 2.0 %collective-permute-start.1 = (bf16[512,256]{1,0:T(8,128)(2,1)S(1)}, bf16[512,256]{1,0:T(8,128)(2,1)}, u32[]{:S(2)}, u32[]{:S(2)}) collective-permute-start(bf16[512,256]{1,0:T(8,128)(2,1)S(1)} %constant_dynamic-update-slice_fusion), channel_id=1, source_target_pairs={{0,2},{1,3},{4,6},{5,7},{8,10},{9,11},{12,14},{13,15},{16,18},{17,... | collective-permute-start | bytes 786440 | tf_op jit(solution)/shard_map/ppermute | solution.py:24
  24.9 3.8 %copy.35 = bf16[2,4,2,128,768]{4,3,2,1,0:T(8,128)(2,1)} copy(bf16[2,4,2,128,768]{4,3,0,1,2:T(8,128)(2,1)} %bitcast.106) | data formatting | bytes 6291456 | tf_op jit(solution)/shard_map/transpose | solution.py:104
  28.9 1.5 collective-permute-start
  30.6 3.7 %convolution_convert_fusion = bf16[512,2048]{1,0:T(8,128)(2,1)S(1)} fusion(bf16[512,768]{1,0:T(8,128)(2,1)S(1)} %bitcast.115, bf16[2048,768]{1,0:T(8,128)(2,1)} %bitcast.107), kind=kOutput, calls=%fused_computation.7 | convolution fusion | flops 1611661312 | bytes 6029312 | tf_op jit(solution)/shard_map/tf,hf->th/dot_general | solution.py:107
  34.4 2.2 %collective-permute-start.6 = (bf16[512,1024]{1,0:T(8,128)(2,1)S(1)}, bf16[512,1024]{1,0:T(8,128)(2,1)S(1)}, u32[]{:S(2)}, u32[]{:S(2)}) collective-permute-start(bf16[512,1024]{1,0:T(8,128)(2,1)S(1)} %constant_dynamic-slice_fusion.5), channel_id=1, source_target_pairs={{0,4},{4,0},{1,5},{5,1},{2,6},{6,2},{3,7},{7,3},{8,12},{12,8},{9,1... | collective-permute-start | bytes 3145736 | tf_op jit(solution)/shard_map/ppermute | solution.py:20
  39.0 1.8 fusion.3
  40.8 1.9 %fusion.2 = f32[512,2048]{0,1:T(8,128)S(1)} fusion(f32[2048,512]{1,0:T(8,128)S(1)} %get-tuple-element.37, f32[512]{0:T(512)S(1)} %fusion.3, f32[512]{0:T(512)S(1)} %get-tuple-element.36, s32[512]{0:T(512)S(1)} %iota_add_fusion, s32[512]{0:T(512)S(1)} %convert_reduce_fusion.1, s32[2048]{0:T(1024)S(1)} %bitcast.121, s32[2048]{0:T(1024)S(1)} %convert_reduce_fusion), kind=kLoop, calls=%fused_computation.14 | loop fusion | flops 8388608 | bytes 8413184 | tf_op jit(solution)/shard_map/div | solution.py:95
  42.8 2.0 %copy-done.2 = f32[512,2048]{0,1:T(8,128)} copy-done((f32[512,2048]{0,1:T(8,128)}, f32[512,2048]{0,1:T(8,128)S(1)}, u32[]{:S(2)}) %copy-start.2) | copy-done | bytes 4194328
  46.7 1.6 add_convert_fusion
  48.4 6.1 %collective-permute-start.7 = (bf16[128,768]{1,0:T(8,128)(2,1)S(1)}, bf16[128,768]{1,0:T(8,128)(2,1)S(1)}, u32[]{:S(2)}, u32[]{:S(2)}) collective-permute-start(bf16[128,768]{1,0:T(8,128)(2,1)S(1)} %bitcast.111), channel_id=1, source_target_pairs={{0,3},{1,0},{2,1},{3,2},{4,7},{5,4},{6,5},{7,6},{8,11},{9,8},{10,9... | collective-permute-start | bytes 589832 | tf_op jit(solution)/shard_map/ppermute | solution.py:20
  54.5 2.8 %collective-permute-start.9 = (bf16[128,768]{1,0:T(8,128)(2,1)S(1)}, bf16[128,768]{1,0:T(8,128)(2,1)S(1)}, u32[]{:S(2)}, u32[]{:S(2)}) collective-permute-start(bf16[128,768]{1,0:T(8,128)(2,1)S(1)} %bitcast.112), channel_id=1, source_target_pairs={{0,1},{1,2},{2,3},{3,0},{4,5},{5,6},{6,7},{7,4},{8,9},{9,10},{10,1... | collective-permute-start | bytes 589832 | tf_op jit(solution)/shard_map/ppermute | solution.py:20
  57.3 3.3 %collective-permute-start.8 = (bf16[128,768]{1,0:T(8,128)(2,1)S(1)}, bf16[128,768]{1,0:T(8,128)(2,1)S(1)}, u32[]{:S(2)}, u32[]{:S(2)}) collective-permute-start(bf16[128,768]{1,0:T(8,128)(2,1)S(1)} %bitcast.113), channel_id=1, source_target_pairs={{0,2},{1,3},{2,0},{3,1},{4,6},{5,7},{6,4},{7,5},{8,10},{9,11},{10,... | collective-permute-start | bytes 589832 | tf_op jit(solution)/shard_map/ppermute | solution.py:20
  62.1 16.0 %collective-permute-done.8 = bf16[128,768]{1,0:T(8,128)(2,1)S(1)} collective-permute-done((bf16[128,768]{1,0:T(8,128)(2,1)S(1)}, bf16[128,768]{1,0:T(8,128)(2,1)S(1)}, u32[]{:S(2)}, u32[]{:S(2)}) %collective-permute-start.8) | collective-permute-done | bytes 196640 | tf_op jit(solution)/shard_map/ppermute | solution.py:20
  80.3 2.8 %collective-permute-start.10 = (bf16[4,128,768]{2,1,0:T(8,128)(2,1)}, bf16[4,128,768]{2,1,0:T(8,128)(2,1)}, u32[]{:S(2)}, u32[]{:S(2)}) collective-permute-start(bf16[4,128,768]{2,1,0:T(8,128)(2,1)} %constant_dynamic-slice_fusion.4), channel_id=1, source_target_pairs={{0,192},{64,0},{128,64},{192,128},{1,193},{65,1},{129,65},{193,129... | collective-permute-start | bytes 2359304 | tf_op jit(solution)/shard_map/ppermute | solution.py:20
  87.1 12.7 %collective-permute-done.11 = bf16[4,128,768]{2,1,0:T(8,128)(2,1)S(1)} collective-permute-done((bf16[4,128,768]{2,1,0:T(8,128)(2,1)}, bf16[4,128,768]{2,1,0:T(8,128)(2,1)S(1)}, u32[]{:S(2)}, u32[]{:S(2)}) %collective-permute-start.11) | collective-permute-done | bytes 786464 | tf_op jit(solution)/shard_map/ppermute | solution.py:20
  99.8 2.7 %collective-permute-start.14 = (bf16[512,256]{1,0:T(8,128)(2,1)S(1)}, bf16[512,256]{1,0:T(8,128)(2,1)S(1)}, u32[]{:S(2)}, u32[]{:S(2)}) collective-permute-start(bf16[512,256]{1,0:T(8,128)(2,1)S(1)} %get-tuple-element.33), channel_id=1, source_target_pairs={{0,16},{8,24},{16,0},{24,8},{1,17},{9,25},{17,1},{25,9},{2,18},{10... | collective-permute-start | bytes 786440 | tf_op jit(solution)/shard_map/ppermute | solution.py:20
  102.6 12.2 %collective-permute-done.10 = bf16[4,128,768]{2,1,0:T(8,128)(2,1)} collective-permute-done((bf16[4,128,768]{2,1,0:T(8,128)(2,1)}, bf16[4,128,768]{2,1,0:T(8,128)(2,1)}, u32[]{:S(2)}, u32[]{:S(2)}) %collective-permute-start.10) | collective-permute-done | bytes 786464 | tf_op jit(solution)/shard_map/ppermute | solution.py:20
  114.8 3.6 %collective-permute-done.12 = bf16[4,128,768]{2,1,0:T(8,128)(2,1)} collective-permute-done((bf16[4,128,768]{2,1,0:T(8,128)(2,1)}, bf16[4,128,768]{2,1,0:T(8,128)(2,1)}, u32[]{:S(2)}, u32[]{:S(2)}) %collective-permute-start.12) | collective-permute-done | bytes 786464 | tf_op jit(solution)/shard_map/ppermute | solution.py:20
  118.4 1.6 pad_maximum_fusion
  120.2 4.6 %collective-permute-start.16 = (bf16[512,128]{1,0:T(8,128)(2,1)S(1)}, bf16[512,128]{1,0:T(8,128)(2,1)S(1)}, u32[]{:S(2)}, u32[]{:S(2)}) collective-permute-start(bf16[512,128]{1,0:T(8,128)(2,1)S(1)} %constant_dynamic-slice_fusion), channel_id=1, source_target_pairs={{0,32},{32,0},{1,33},{33,1},{2,34},{34,2},{3,35},{35,3},{4,36},{36... | collective-permute-start | bytes 393224 | tf_op jit(solution)/shard_map/ppermute | solution.py:20
  125.9 8.9 %collective-permute-done.16 = bf16[512,128]{1,0:T(8,128)(2,1)S(1)} collective-permute-done((bf16[512,128]{1,0:T(8,128)(2,1)S(1)}, bf16[512,128]{1,0:T(8,128)(2,1)S(1)}, u32[]{:S(2)}, u32[]{:S(2)}) %collective-permute-start.16) | collective-permute-done | bytes 131104 | tf_op jit(solution)/shard_map/ppermute | solution.py:20
  137.2 2.2 %multiply_convert_fusion = bf16[512,2048]{0,1:T(8,128)(2,1)S(1)} fusion(f32[512,2048]{0,1:T(8,128)S(1)} %get-tuple-element.39, f32[512]{0:T(512)S(1)} %get-tuple-element.38, f32[512]{0:T(512)S(1)} %copy-done.19, f32[512]{0:T(512)S(1)} %copy-done.17, f32[2048,512]{1,0:T(8,128)S(1)} %copy-done.5, s32[512]{0:T(512)S(1)} %copy-done.13, s32[2048]{0:T(1024)S(1)} %bitcast.122, ...), kind=kLoop, calls=%fused_computation.1 | loop fusion | flops 11534336 | bytes 10512384 | tf_op jit(solution)/shard_map/convert_element_type | solution.py:120
  144.1 1.5 collective-permute-start.18
  147.0 7.1 %collective-permute-done.17 = bf16[512,256]{0,1:T(8,128)(2,1)S(1)} collective-permute-done((bf16[512,256]{0,1:T(8,128)(2,1)S(1)}, bf16[512,256]{0,1:T(8,128)(2,1)S(1)}, u32[]{:S(2)}, u32[]{:S(2)}) %collective-permute-start.17) | collective-permute-done | bytes 262176 | tf_op jit(solution)/shard_map/ppermute | solution.py:24
  154.2 11.9 %collective-permute-done.18 = bf16[512,256]{0,1:T(8,128)(2,1)S(1)} collective-permute-done((bf16[512,256]{0,1:T(8,128)(2,1)S(1)}, bf16[512,256]{0,1:T(8,128)(2,1)S(1)}, u32[]{:S(2)}, u32[]{:S(2)}) %collective-permute-start.18) | collective-permute-done | bytes 262176 | tf_op jit(solution)/shard_map/ppermute | solution.py:24
  167.8 3.6 %fusion.4 = f32[2,4,2,128,768]{4,3,2,1,0:T(8,128)S(1)} fusion(bf16[512,768,1,1,1]{1,0,4,3,2:T(8,128)(2,1)S(1)} %bitcast.105, bf16[2,4,4,2,512,128]{5,4,3,2,1,0:T(8,128)(2,1)} %bitcast.93), kind=kOutput, calls=%fused_computation.20 | convolution fusion | flops 1610612736 | bytes 9175040 | tf_op jit(solution)/shard_map/zxcth,tf->zxchf/dot_general | solution.py:142
  171.9 1.8 convolution_add_fusion.2
  173.8 1.8 convolution_add_fusion.1
  175.6 4.5 %convolution_add_fusion = f32[2,4,2,128,768]{4,3,2,1,0:T(8,128)} fusion(f32[2,4,2,128,768]{4,3,2,1,0:T(8,128)S(1)} %convolution_add_fusion.1, bf16[512,768,1,1,1]{1,0,4,3,2:T(8,128)(2,1)S(1)} %bitcast.102, bf16[2,4,4,2,512,128]{5,4,3,2,1,0:T(8,128)(2,1)S(1)} %bitcast.96), kind=kOutput, calls=%fused_computation.8 | convolution fusion | flops 1612185600 | bytes 15466496 | tf_op jit(solution)/shard_map/zxcth,tf->zxchf/dot_general | solution.py:142
  (101 shorter events, 28.3 us)
Async XLA Ops:
  7.2 30.7 %copy-start = (bf16[512,128]{1,0:T(8,128)(2,1)S(1)}, bf16[512,128]{1,0:T(8,128)(2,1)}, u32[]{:S(2)}) copy-start(bf16[512,128]{1,0:T(8,128)(2,1)} %param.8) | copy-start | bytes 393220
  7.2 23.3 %copy-start.10 = (bf16[1,128,768]{2,1,0:T(8,128)(2,1)S(1)}, bf16[1,128,768]{2,1,0:T(8,128)(2,1)}, u32[]{:S(2)}) copy-start(bf16[1,128,768]{2,1,0:T(8,128)(2,1)} %param.6) | copy-start | bytes 589828
  7.2 160.6 %all-gather.3.cloned.1.call-start = ((), (), s32[]{:S(2)}) async-start(), calls=%async_computation | async-start | bytes 8519680 | tf_op jit(solution)/shard_map/all_gather | solution.py:112
  7.2 21.7 %collective-permute-start.5 = (bf16[128,768]{1,0:T(8,128)(2,1)}, bf16[128,768]{1,0:T(8,128)(2,1)S(1)}, u32[]{:S(2)}, u32[]{:S(2)}) collective-permute-start(bf16[128,768]{1,0:T(8,128)(2,1)} %bitcast.108), channel_id=1, source_target_pairs={{0,64},{64,128},{128,192},{192,0},{1,65},{65,129},{129,193},{193,1... | collective-permute-start | bytes 589832 | tf_op jit(solution)/shard_map/ppermute | solution.py:20
  9.4 21.0 %collective-permute-start.4 = (bf16[128,768]{1,0:T(8,128)(2,1)}, bf16[128,768]{1,0:T(8,128)(2,1)S(1)}, u32[]{:S(2)}, u32[]{:S(2)}) collective-permute-start(bf16[128,768]{1,0:T(8,128)(2,1)} %bitcast.109), channel_id=1, source_target_pairs={{0,128},{64,192},{128,0},{192,64},{1,129},{65,193},{129,1},{193,65... | collective-permute-start | bytes 589832 | tf_op jit(solution)/shard_map/ppermute | solution.py:20
  12.1 18.4 %collective-permute-start.3 = (bf16[128,768]{1,0:T(8,128)(2,1)}, bf16[128,768]{1,0:T(8,128)(2,1)S(1)}, u32[]{:S(2)}, u32[]{:S(2)}) collective-permute-start(bf16[128,768]{1,0:T(8,128)(2,1)} %bitcast.110), channel_id=1, source_target_pairs={{0,192},{64,0},{128,64},{192,128},{1,193},{65,1},{129,65},{193,129... | collective-permute-start | bytes 589832 | tf_op jit(solution)/shard_map/ppermute | solution.py:20
  15.0 19.3 %copy-start.11 = (bf16[512,256]{1,0:T(8,128)(2,1)}, bf16[512,256]{1,0:T(8,128)(2,1)S(1)}, u32[]{:S(2)}) copy-start(bf16[512,256]{1,0:T(8,128)(2,1)S(1)} %constant_dynamic-update-slice_fusion) | copy-start | bytes 786436
  15.0 21.6 %collective-permute-start.2 = (bf16[512,256]{1,0:T(8,128)(2,1)S(1)}, bf16[512,256]{1,0:T(8,128)(2,1)}, u32[]{:S(2)}, u32[]{:S(2)}) collective-permute-start(bf16[512,256]{1,0:T(8,128)(2,1)S(1)} %constant_dynamic-update-slice_fusion), channel_id=1, source_target_pairs={{0,3},{4,7},{8,11},{12,15},{16,19},{20,23},{24,27},{28,31},{32,35}... | collective-permute-start | bytes 786440 | tf_op jit(solution)/shard_map/ppermute | solution.py:24
  22.0 14.6 %collective-permute-start.1 = (bf16[512,256]{1,0:T(8,128)(2,1)S(1)}, bf16[512,256]{1,0:T(8,128)(2,1)}, u32[]{:S(2)}, u32[]{:S(2)}) collective-permute-start(bf16[512,256]{1,0:T(8,128)(2,1)S(1)} %constant_dynamic-update-slice_fusion), channel_id=1, source_target_pairs={{0,2},{1,3},{4,6},{5,7},{8,10},{9,11},{12,14},{13,15},{16,18},{17,... | collective-permute-start | bytes 786440 | tf_op jit(solution)/shard_map/ppermute | solution.py:24
  24.8 15.9 %copy-start.12 = (s32[512]{0:T(512)}, s32[512]{0:T(512)S(1)}, u32[]{:S(2)}) copy-start(s32[512]{0:T(512)S(1)} %iota_add_fusion) | copy-start | bytes 6148
  28.8 11.9 %copy-start.14 = (s32[512]{0:T(512)}, s32[512]{0:T(512)S(1)}, u32[]{:S(2)}) copy-start(s32[512]{0:T(512)S(1)} %convert_reduce_fusion.1) | copy-start | bytes 6148
  28.9 7.7 %collective-permute-start = (bf16[512,256]{1,0:T(8,128)(2,1)S(1)}, bf16[512,256]{1,0:T(8,128)(2,1)S(1)}, u32[]{:S(2)}, u32[]{:S(2)}) collective-permute-start(bf16[512,256]{1,0:T(8,128)(2,1)S(1)} %constant_dynamic-update-slice_fusion), channel_id=1, source_target_pairs={{0,1},{1,2},{2,3},{4,5},{5,6},{6,7},{8,9},{9,10},{10,11},{12,13},{... | collective-permute-start | bytes 786440 | tf_op jit(solution)/shard_map/ppermute | solution.py:24
  34.3 4.6 %copy-start.8 = (bf16[512,2048]{1,0:T(8,128)(2,1)}, bf16[512,2048]{1,0:T(8,128)(2,1)S(1)}, u32[]{:S(2)}) copy-start(bf16[512,2048]{1,0:T(8,128)(2,1)S(1)} %convolution_convert_fusion) | copy-start | bytes 6291460
  34.4 12.3 %collective-permute-start.6 = (bf16[512,1024]{1,0:T(8,128)(2,1)S(1)}, bf16[512,1024]{1,0:T(8,128)(2,1)S(1)}, u32[]{:S(2)}, u32[]{:S(2)}) collective-permute-start(bf16[512,1024]{1,0:T(8,128)(2,1)S(1)} %constant_dynamic-slice_fusion.5), channel_id=1, source_target_pairs={{0,4},{4,0},{1,5},{5,1},{2,6},{6,2},{3,7},{7,3},{8,12},{12,8},{9,1... | collective-permute-start | bytes 3145736 | tf_op jit(solution)/shard_map/ppermute | solution.py:20
  39.0 3.8 %copy-start.4 = (f32[2048,512]{1,0:T(8,128)}, f32[2048,512]{1,0:T(8,128)S(1)}, u32[]{:S(2)}) copy-start(f32[2048,512]{1,0:T(8,128)S(1)} %get-tuple-element.37) | copy-start | bytes 12582916
  48.4 13.7 %collective-permute-start.7 = (bf16[128,768]{1,0:T(8,128)(2,1)S(1)}, bf16[128,768]{1,0:T(8,128)(2,1)S(1)}, u32[]{:S(2)}, u32[]{:S(2)}) collective-permute-start(bf16[128,768]{1,0:T(8,128)(2,1)S(1)} %bitcast.111), channel_id=1, source_target_pairs={{0,3},{1,0},{2,1},{3,2},{4,7},{5,4},{6,5},{7,6},{8,11},{9,8},{10,9... | collective-permute-start | bytes 589832 | tf_op jit(solution)/shard_map/ppermute | solution.py:20
  54.5 23.5 %collective-permute-start.9 = (bf16[128,768]{1,0:T(8,128)(2,1)S(1)}, bf16[128,768]{1,0:T(8,128)(2,1)S(1)}, u32[]{:S(2)}, u32[]{:S(2)}) collective-permute-start(bf16[128,768]{1,0:T(8,128)(2,1)S(1)} %bitcast.112), channel_id=1, source_target_pairs={{0,1},{1,2},{2,3},{3,0},{4,5},{5,6},{6,7},{7,4},{8,9},{9,10},{10,1... | collective-permute-start | bytes 589832 | tf_op jit(solution)/shard_map/ppermute | solution.py:20
  57.3 20.7 %collective-permute-start.8 = (bf16[128,768]{1,0:T(8,128)(2,1)S(1)}, bf16[128,768]{1,0:T(8,128)(2,1)S(1)}, u32[]{:S(2)}, u32[]{:S(2)}) collective-permute-start(bf16[128,768]{1,0:T(8,128)(2,1)S(1)} %bitcast.113), channel_id=1, source_target_pairs={{0,2},{1,3},{2,0},{3,1},{4,6},{5,7},{6,4},{7,5},{8,10},{9,11},{10,... | collective-permute-start | bytes 589832 | tf_op jit(solution)/shard_map/ppermute | solution.py:20
  80.3 19.6 %collective-permute-start.11 = (bf16[4,128,768]{2,1,0:T(8,128)(2,1)}, bf16[4,128,768]{2,1,0:T(8,128)(2,1)S(1)}, u32[]{:S(2)}, u32[]{:S(2)}) collective-permute-start(bf16[4,128,768]{2,1,0:T(8,128)(2,1)} %constant_dynamic-slice_fusion.4), channel_id=1, source_target_pairs={{0,128},{64,192},{128,0},{192,64},{1,129},{65,193},{129,1},{193,65... | collective-permute-start | bytes 2359304 | tf_op jit(solution)/shard_map/ppermute | solution.py:20
  80.3 34.5 %collective-permute-start.10 = (bf16[4,128,768]{2,1,0:T(8,128)(2,1)}, bf16[4,128,768]{2,1,0:T(8,128)(2,1)}, u32[]{:S(2)}, u32[]{:S(2)}) collective-permute-start(bf16[4,128,768]{2,1,0:T(8,128)(2,1)} %constant_dynamic-slice_fusion.4), channel_id=1, source_target_pairs={{0,192},{64,0},{128,64},{192,128},{1,193},{65,1},{129,65},{193,129... | collective-permute-start | bytes 2359304 | tf_op jit(solution)/shard_map/ppermute | solution.py:20
  83.0 35.4 %collective-permute-start.12 = (bf16[4,128,768]{2,1,0:T(8,128)(2,1)}, bf16[4,128,768]{2,1,0:T(8,128)(2,1)}, u32[]{:S(2)}, u32[]{:S(2)}) collective-permute-start(bf16[4,128,768]{2,1,0:T(8,128)(2,1)} %constant_dynamic-slice_fusion.4), channel_id=1, source_target_pairs={{0,64},{64,128},{128,192},{192,0},{1,65},{65,129},{129,193},{193,1... | collective-permute-start | bytes 2359304 | tf_op jit(solution)/shard_map/ppermute | solution.py:20
  84.4 35.6 %collective-permute-start.13 = (bf16[512,256]{1,0:T(8,128)(2,1)S(1)}, bf16[512,256]{1,0:T(8,128)(2,1)S(1)}, u32[]{:S(2)}, u32[]{:S(2)}) collective-permute-start(bf16[512,256]{1,0:T(8,128)(2,1)S(1)} %get-tuple-element.31), channel_id=1, source_target_pairs={{0,8},{8,16},{16,24},{24,0},{1,9},{9,17},{17,25},{25,1},{2,10},{10... | collective-permute-start | bytes 786440 | tf_op jit(solution)/shard_map/ppermute | solution.py:20
  85.7 34.3 %collective-permute-start.15 = (bf16[512,256]{1,0:T(8,128)(2,1)S(1)}, bf16[512,256]{1,0:T(8,128)(2,1)S(1)}, u32[]{:S(2)}, u32[]{:S(2)}) collective-permute-start(bf16[512,256]{1,0:T(8,128)(2,1)S(1)} %get-tuple-element.32), channel_id=1, source_target_pairs={{0,24},{8,0},{16,8},{24,16},{1,25},{9,1},{17,9},{25,17},{2,26},{10... | collective-permute-start | bytes 786440 | tf_op jit(solution)/shard_map/ppermute | solution.py:20
  99.8 20.2 %collective-permute-start.14 = (bf16[512,256]{1,0:T(8,128)(2,1)S(1)}, bf16[512,256]{1,0:T(8,128)(2,1)S(1)}, u32[]{:S(2)}, u32[]{:S(2)}) collective-permute-start(bf16[512,256]{1,0:T(8,128)(2,1)S(1)} %get-tuple-element.33), channel_id=1, source_target_pairs={{0,16},{8,24},{16,0},{24,8},{1,17},{9,25},{17,1},{25,9},{2,18},{10... | collective-permute-start | bytes 786440 | tf_op jit(solution)/shard_map/ppermute | solution.py:20
  120.0 14.9 %copy-start.3 = (f32[512,2048]{0,1:T(8,128)S(1)}, f32[512,2048]{0,1:T(8,128)}, u32[]{:S(2)}) copy-start(f32[512,2048]{0,1:T(8,128)} %copy-done.2) | copy-start | bytes 12582916
  120.2 14.7 %collective-permute-start.16 = (bf16[512,128]{1,0:T(8,128)(2,1)S(1)}, bf16[512,128]{1,0:T(8,128)(2,1)S(1)}, u32[]{:S(2)}, u32[]{:S(2)}) collective-permute-start(bf16[512,128]{1,0:T(8,128)(2,1)S(1)} %constant_dynamic-slice_fusion), channel_id=1, source_target_pairs={{0,32},{32,0},{1,33},{33,1},{2,34},{34,2},{3,35},{35,3},{4,36},{36... | collective-permute-start | bytes 393224 | tf_op jit(solution)/shard_map/ppermute | solution.py:20
  141.5 12.7 %collective-permute-start.17 = (bf16[512,256]{0,1:T(8,128)(2,1)S(1)}, bf16[512,256]{0,1:T(8,128)(2,1)S(1)}, u32[]{:S(2)}, u32[]{:S(2)}) collective-permute-start(bf16[512,256]{0,1:T(8,128)(2,1)S(1)} %get-tuple-element.28), channel_id=1, source_target_pairs={{1,0},{2,1},{3,2},{5,4},{6,5},{7,6},{9,8},{10,9},{11,10},{13,12},{... | collective-permute-start | bytes 786440 | tf_op jit(solution)/shard_map/ppermute | solution.py:24
  142.8 11.4 %collective-permute-start.19 = (bf16[512,256]{0,1:T(8,128)(2,1)S(1)}, bf16[512,256]{0,1:T(8,128)(2,1)S(1)}, u32[]{:S(2)}, u32[]{:S(2)}) collective-permute-start(bf16[512,256]{0,1:T(8,128)(2,1)S(1)} %get-tuple-element.29), channel_id=1, source_target_pairs={{3,0},{7,4},{11,8},{15,12},{19,16},{23,20},{27,24},{31,28},{35,32}... | collective-permute-start | bytes 786440 | tf_op jit(solution)/shard_map/ppermute | solution.py:24
  144.1 22.0 %collective-permute-start.18 = (bf16[512,256]{0,1:T(8,128)(2,1)S(1)}, bf16[512,256]{0,1:T(8,128)(2,1)S(1)}, u32[]{:S(2)}, u32[]{:S(2)}) collective-permute-start(bf16[512,256]{0,1:T(8,128)(2,1)S(1)} %get-tuple-element.30), channel_id=1, source_target_pairs={{2,0},{3,1},{6,4},{7,5},{10,8},{11,9},{14,12},{15,13},{18,16},{19,... | collective-permute-start | bytes 786440 | tf_op jit(solution)/shard_map/ppermute | solution.py:24
  167.8 4.0 %copy-start.6 = (bf16[32768,128]{1,0:T(8,128)(2,1)S(1)}, bf16[32768,128]{1,0:T(8,128)(2,1)}, u32[]{:S(2)}) copy-start(bf16[32768,128]{1,0:T(8,128)(2,1)} %all-gather.3.cloned.1.call-done) | copy-start | bytes 25165828
  167.8 4.1 %copy-start.7 = (bf16[1,4,128,768]{3,2,0,1:T(8,128)(2,1)S(1)}, bf16[1,4,128,768]{3,2,0,1:T(8,128)(2,1)}, u32[]{:S(2)}) copy-start(bf16[1,4,128,768]{3,2,0,1:T(8,128)(2,1)} %get-tuple-element.26) | copy-start | bytes 2359300
  175.6 4.6 %copy-start.1 = (bf16[512,128]{1,0:T(8,128)(2,1)S(1)}, bf16[512,128]{1,0:T(8,128)(2,1)}, u32[]{:S(2)}) copy-start(bf16[512,128]{1,0:T(8,128)(2,1)} %param.8) | copy-start | bytes 393220
  (9 other events, 20.0 us)
Sparse Core Ops, SparseCore 0:
  48.5 96.9 all-gather.2

commit v2 on v1

--- a/solution.py
+++ b/solution.py
@@ -108,7 +108,7 @@
             "tf,hf->th", grad_rows, weight_perm, preferred_element_type=jnp.float32
         ).astype(jnp.bfloat16)
         partial = pp_reduce_scatter_cols(partial, "core", n_core).astype(jnp.bfloat16)
-        context, partial = lax.optimization_barrier((context, partial))
+        context, partial, by_depth = lax.optimization_barrier((context, partial, by_depth))
         ctx_all = lax.all_gather(context[None], ("zh", DEP, "x", "core"), axis=0, tiled=True)
         ctx_all = ctx_all.reshape(n_zh, n_dep, n_x, n_core, tok_depth, head_dim)
         partial = pp_reduce_scatter_cols(partial, "x", n_x).astype(jnp.bfloat16)

time: 187 us -> 188 us (level)
  starting transfers between devices: 47.7 us -> 43.4 us
  local copies, waits for them, and re-layouts: 15.7 us -> 19.6 us
  waiting for transfers between devices: 74 us -> 76.6 us
  matrix products: 22 us -> 20.1 us
    ppermute x14, waiting for transfers between devices: 54.9 us -> 30.6 us  [shift(): return lax.ppermute(x, axis, [(i, (i + s) % n) for i in range(n)])]
    ppermute x6, waiting for transfers between devices: 19.1 us -> 33.6 us  [shift_open(): lax.ppermute(x, axis, [(i, i + s) for i in range(n) if 0 <= i + s < n])]
    all_gather x1, waiting for transfers between devices: 0.01 us -> 12.4 us  [shards(): lax.all_gather(context[None], ('zh', DEP, 'x', 'core'), axis=0, tiled=True)]
    ppermute x14, starting transfers between devices: 33.1 us -> 27.3 us  [shift(): return lax.ppermute(x, axis, [(i, (i + s) % n) for i in range(n)])]
    unnamed x51, local copies, waits for them, and re-layouts: 7.34 us -> 11.4 us
    dot_general x1, matrix products: 3.72 us -> 1.82 us  [shards(): jnp.einsum('tf,hf->th', grad_rows, weight_perm, preferred_element_type=jn...]
  transfers between devices with their start and end apart: 21 -> 21, of which waited for: 8 -> 9; matrix products, arithmetic and copies ran while one was open for 17% -> 19% of each run, Pallas kernels for 0% -> 0%
where the time goes in v2:
time: 188 us; the launch traced here: 187 us
  waiting for transfers between devices  76.6 us (41%)
  starting transfers between devices  43.4 us (23%)
  matrix products  20.1 us (11%)
  local copies, waits for them, and re-layouts  19.6 us (10%)
  between operations  14.6 us (8%)
  other arithmetic  13 us (7%)
    ppermute x6, waiting for transfers between devices, shift_open(): lax.ppermute(x, axis, [(i, i + s) for i in range(n) if 0 <= i + s < n])  33.6 us
    ppermute x14, waiting for transfers between devices, shift(): return lax.ppermute(x, axis, [(i, (i + s) % n) for i in range(n)])  30.6 us
    ppermute x14, starting transfers between devices, shift(): return lax.ppermute(x, axis, [(i, (i + s) % n) for i in range(n)])  27.3 us
    ppermute x6, starting transfers between devices, shift_open(): lax.ppermute(x, axis, [(i, i + s) for i in range(n) if 0 <= i + s < n])  16 us
    all_gather x1, waiting for transfers between devices, shards(): lax.all_gather(context[None], ('zh', DEP, 'x', 'core'), axis=0, tiled=True)  12.4 us
    dot_general x4, matrix products, shards(): jnp.einsum('zxcth,tf->zxchf', ctx_all[:, depth], rows_all[depth].reshape(...  11.8 us
    unnamed x51, local copies, waits for them, and re-layouts  11.4 us
  transfers between devices with their start and end apart: 21, of which 9 were waited for; matrix products, arithmetic and copies ran while one was open for 19% of the time, Pallas kernels for 0%

profile of v2, /device:TPU:1, one launch (start us, length us, event | category | flops | bytes accessed | tf_op | source)
XLA Modules:
  0.0 187.3 jit_solution(7235533875489083157)
XLA Ops:
  7.2 2.5 %collective-permute-start.9 = (bf16[128,768]{1,0:T(8,128)(2,1)}, bf16[128,768]{1,0:T(8,128)(2,1)}, u32[]{:S(2)}, u32[]{:S(2)}) collective-permute-start(bf16[128,768]{1,0:T(8,128)(2,1)} %bitcast.108), channel_id=1, source_target_pairs={{0,1},{1,2},{2,3},{3,0},{4,5},{5,6},{6,7},{7,4},{8,9},{9,10},{10,1... | collective-permute-start | bytes 589832 | tf_op jit(solution)/shard_map/ppermute | solution.py:20
  9.8 3.0 %collective-permute-start.8 = (bf16[128,768]{1,0:T(8,128)(2,1)}, bf16[128,768]{1,0:T(8,128)(2,1)}, u32[]{:S(2)}, u32[]{:S(2)}) collective-permute-start(bf16[128,768]{1,0:T(8,128)(2,1)} %bitcast.109), channel_id=1, source_target_pairs={{0,2},{1,3},{2,0},{3,1},{4,6},{5,7},{6,4},{7,5},{8,10},{9,11},{10,... | collective-permute-start | bytes 589832 | tf_op jit(solution)/shard_map/ppermute | solution.py:20
  14.8 2.6 %collective-permute-start.4 = (bf16[128,768]{1,0:T(8,128)(2,1)}, bf16[128,768]{1,0:T(8,128)(2,1)}, u32[]{:S(2)}, u32[]{:S(2)}) collective-permute-start(bf16[128,768]{1,0:T(8,128)(2,1)} %bitcast.112), channel_id=1, source_target_pairs={{0,128},{64,192},{128,0},{192,64},{1,129},{65,193},{129,1},{193,65... | collective-permute-start | bytes 589832 | tf_op jit(solution)/shard_map/ppermute | solution.py:20
  18.3 1.6 constant_dynamic-update-slice_fusion.1
  19.9 2.1 %copy.35 = bf16[2,4,2,128,768]{4,3,2,1,0:T(8,128)(2,1)S(1)} copy(bf16[2,4,2,128,768]{4,3,0,1,2:T(8,128)(2,1)} %bitcast.106) | data formatting | bytes 6291456 | tf_op jit(solution)/shard_map/transpose | solution.py:104
  22.1 1.6 constant_dynamic-update-slice_fusion
  23.8 2.0 %collective-permute-start.3 = (bf16[128,768]{1,0:T(8,128)(2,1)S(1)}, bf16[128,768]{1,0:T(8,128)(2,1)S(1)}, u32[]{:S(2)}, u32[]{:S(2)}) collective-permute-start(bf16[128,768]{1,0:T(8,128)(2,1)S(1)} %bitcast.113), channel_id=1, source_target_pairs={{0,192},{64,0},{128,64},{192,128},{1,193},{65,1},{129,65},{193,129... | collective-permute-start | bytes 589832 | tf_op jit(solution)/shard_map/ppermute | solution.py:20
  26.8 5.9 %collective-permute-start.2 = (bf16[512,256]{1,0:T(8,128)(2,1)}, bf16[512,256]{1,0:T(8,128)(2,1)S(1)}, u32[]{:S(2)}, u32[]{:S(2)}) collective-permute-start(bf16[512,256]{1,0:T(8,128)(2,1)} %constant_dynamic-update-slice_fusion), channel_id=1, source_target_pairs={{0,3},{4,7},{8,11},{12,15},{16,19},{20,23},{24,27},{28,31},{32,35}... | collective-permute-start | bytes 786440 | tf_op jit(solution)/shard_map/ppermute | solution.py:24
  33.6 3.7 %collective-permute-start.1 = (bf16[512,256]{1,0:T(8,128)(2,1)}, bf16[512,256]{1,0:T(8,128)(2,1)S(1)}, u32[]{:S(2)}, u32[]{:S(2)}) collective-permute-start(bf16[512,256]{1,0:T(8,128)(2,1)} %constant_dynamic-update-slice_fusion), channel_id=1, source_target_pairs={{0,2},{1,3},{4,6},{5,7},{8,10},{9,11},{12,14},{13,15},{16,18},{17,... | collective-permute-start | bytes 786440 | tf_op jit(solution)/shard_map/ppermute | solution.py:24
  38.3 2.3 %collective-permute-start = (bf16[512,256]{1,0:T(8,128)(2,1)}, bf16[512,256]{1,0:T(8,128)(2,1)S(1)}, u32[]{:S(2)}, u32[]{:S(2)}) collective-permute-start(bf16[512,256]{1,0:T(8,128)(2,1)} %constant_dynamic-update-slice_fusion), channel_id=1, source_target_pairs={{0,1},{1,2},{2,3},{4,5},{5,6},{6,7},{8,9},{9,10},{10,11},{12,13},{... | collective-permute-start | bytes 786440 | tf_op jit(solution)/shard_map/ppermute | solution.py:24
  41.8 1.8 convolution_convert_fusion
  50.8 1.8 fusion.3
  52.6 1.9 %fusion.2 = f32[512,2048]{0,1:T(8,128)S(1)} fusion(f32[2048,512]{1,0:T(8,128)S(1)} %get-tuple-element.37, f32[512]{0:T(512)S(1)} %fusion.3, f32[512]{0:T(512)S(1)} %get-tuple-element.36, s32[512]{0:T(512)S(1)} %iota_add_fusion, s32[512]{0:T(512)S(1)} %convert_reduce_fusion.1, s32[2048]{0:T(1024)S(1)} %bitcast.123, s32[2048]{0:T(1024)S(1)} %convert_reduce_fusion), kind=kLoop, calls=%fused_computation.14 | loop fusion | flops 8388608 | bytes 8413184 | tf_op jit(solution)/shard_map/div | solution.py:95
  54.5 2.0 %copy-done.2 = f32[512,2048]{0,1:T(8,128)} copy-done((f32[512,2048]{0,1:T(8,128)}, f32[512,2048]{0,1:T(8,128)S(1)}, u32[]{:S(2)}) %copy-start.2) | copy-done | bytes 4194328
  58.5 1.6 add_convert_fusion
  60.2 1.8 collective-permute-start.11
  67.5 12.3 %collective-permute-done.11 = bf16[4,128,768]{2,1,0:T(8,128)(2,1)S(1)} collective-permute-done((bf16[4,128,768]{2,1,0:T(8,128)(2,1)}, bf16[4,128,768]{2,1,0:T(8,128)(2,1)S(1)}, u32[]{:S(2)}, u32[]{:S(2)}) %collective-permute-start.11) | collective-permute-done | bytes 786464 | tf_op jit(solution)/shard_map/ppermute | solution.py:20
  79.8 2.7 %collective-permute-start.14 = (bf16[512,256]{1,0:T(8,128)(2,1)S(1)}, bf16[512,256]{1,0:T(8,128)(2,1)S(1)}, u32[]{:S(2)}, u32[]{:S(2)}) collective-permute-start(bf16[512,256]{1,0:T(8,128)(2,1)S(1)} %get-tuple-element.33), channel_id=1, source_target_pairs={{0,16},{8,24},{16,0},{24,8},{1,17},{9,25},{17,1},{25,9},{2,18},{10... | collective-permute-start | bytes 786440 | tf_op jit(solution)/shard_map/ppermute | solution.py:20
  82.5 14.0 %collective-permute-done.10 = bf16[4,128,768]{2,1,0:T(8,128)(2,1)} collective-permute-done((bf16[4,128,768]{2,1,0:T(8,128)(2,1)}, bf16[4,128,768]{2,1,0:T(8,128)(2,1)}, u32[]{:S(2)}, u32[]{:S(2)}) %collective-permute-start.10) | collective-permute-done | bytes 786464 | tf_op jit(solution)/shard_map/ppermute | solution.py:20
  96.5 1.9 %collective-permute-done.12 = bf16[4,128,768]{2,1,0:T(8,128)(2,1)} collective-permute-done((bf16[4,128,768]{2,1,0:T(8,128)(2,1)}, bf16[4,128,768]{2,1,0:T(8,128)(2,1)}, u32[]{:S(2)}, u32[]{:S(2)}) %collective-permute-start.12) | collective-permute-done | bytes 786464 | tf_op jit(solution)/shard_map/ppermute | solution.py:20
  98.4 1.6 pad_maximum_fusion
  100.2 5.2 %collective-permute-start.16 = (bf16[512,128]{1,0:T(8,128)(2,1)S(1)}, bf16[512,128]{1,0:T(8,128)(2,1)S(1)}, u32[]{:S(2)}, u32[]{:S(2)}) collective-permute-start(bf16[512,128]{1,0:T(8,128)(2,1)S(1)} %constant_dynamic-slice_fusion), channel_id=1, source_target_pairs={{0,32},{32,0},{1,33},{33,1},{2,34},{34,2},{3,35},{35,3},{4,36},{36... | collective-permute-start | bytes 393224 | tf_op jit(solution)/shard_map/ppermute | solution.py:20
  106.6 2.5 %collective-permute-done.16 = bf16[512,128]{1,0:T(8,128)(2,1)S(1)} collective-permute-done((bf16[512,128]{1,0:T(8,128)(2,1)S(1)}, bf16[512,128]{1,0:T(8,128)(2,1)S(1)}, u32[]{:S(2)}, u32[]{:S(2)}) %collective-permute-start.16) | collective-permute-done | bytes 131104 | tf_op jit(solution)/shard_map/ppermute | solution.py:20
  111.3 2.2 %multiply_convert_fusion = bf16[512,2048]{0,1:T(8,128)(2,1)S(1)} fusion(f32[512,2048]{0,1:T(8,128)S(1)} %get-tuple-element.39, f32[512]{0:T(512)S(1)} %get-tuple-element.38, f32[512]{0:T(512)S(1)} %copy-done.19, f32[512]{0:T(512)S(1)} %copy-done.17, f32[2048,512]{1,0:T(8,128)S(1)} %copy-done.5, s32[512]{0:T(512)S(1)} %copy-done.13, s32[2048]{0:T(1024)S(1)} %bitcast.124, ...), kind=kLoop, calls=%fused_computation.1 | loop fusion | flops 11534336 | bytes 10512384 | tf_op jit(solution)/shard_map/convert_element_type | solution.py:120
  121.1 14.2 %collective-permute-done.17 = bf16[512,256]{0,1:T(8,128)(2,1)S(1)} collective-permute-done((bf16[512,256]{0,1:T(8,128)(2,1)S(1)}, bf16[512,256]{0,1:T(8,128)(2,1)S(1)}, u32[]{:S(2)}, u32[]{:S(2)}) %collective-permute-start.17) | collective-permute-done | bytes 262176 | tf_op jit(solution)/shard_map/ppermute | solution.py:24
  135.3 13.5 %collective-permute-done.19 = bf16[512,256]{0,1:T(8,128)(2,1)S(1)} collective-permute-done((bf16[512,256]{0,1:T(8,128)(2,1)S(1)}, bf16[512,256]{0,1:T(8,128)(2,1)S(1)}, u32[]{:S(2)}, u32[]{:S(2)}) %collective-permute-start.19) | collective-permute-done | bytes 262176 | tf_op jit(solution)/shard_map/ppermute | solution.py:24
  148.9 5.1 %collective-permute-done.18 = bf16[512,256]{0,1:T(8,128)(2,1)S(1)} collective-permute-done((bf16[512,256]{0,1:T(8,128)(2,1)S(1)}, bf16[512,256]{0,1:T(8,128)(2,1)S(1)}, u32[]{:S(2)}, u32[]{:S(2)}) %collective-permute-start.18) | collective-permute-done | bytes 262176 | tf_op jit(solution)/shard_map/ppermute | solution.py:24
  155.7 12.4 %all-gather.3.cloned.1.call-done = bf16[32768,128]{1,0:T(8,128)(2,1)} async-done(((bf16[512,128]{1,0:T(8,128)(2,1)}), bf16[32768,128]{1,0:T(8,128)(2,1)}) %all-gather.3.cloned.1.call-update) | async-done | bytes 8388624 | tf_op jit(solution)/shard_map/all_gather | solution.py:112
  168.0 3.6 %fusion.4 = f32[2,4,2,128,768]{4,3,2,1,0:T(8,128)S(1)} fusion(bf16[512,768,1,1,1]{1,0,4,3,2:T(8,128)(2,1)S(1)} %bitcast.105, bf16[2,4,4,2,512,128]{5,4,3,2,1,0:T(8,128)(2,1)} %bitcast.93), kind=kOutput, calls=%fused_computation.20 | convolution fusion | flops 1610612736 | bytes 9175040 | tf_op jit(solution)/shard_map/zxcth,tf->zxchf/dot_general | solution.py:142
  172.2 1.8 convolution_add_fusion.2
  174.0 1.8 convolution_add_fusion.1
  175.9 4.5 %convolution_add_fusion = f32[2,4,2,128,768]{4,3,2,1,0:T(8,128)} fusion(f32[2,4,2,128,768]{4,3,2,1,0:T(8,128)S(1)} %convolution_add_fusion.1, bf16[512,768,1,1,1]{1,0,4,3,2:T(8,128)(2,1)S(1)} %bitcast.102, bf16[2,4,4,2,512,128]{5,4,3,2,1,0:T(8,128)(2,1)S(1)} %bitcast.96), kind=kOutput, calls=%fused_computation.8 | convolution fusion | flops 1612185600 | bytes 15466496 | tf_op jit(solution)/shard_map/zxcth,tf->zxchf/dot_general | solution.py:142
  (101 shorter events, 35.1 us)
Async XLA Ops:
  7.2 42.5 %copy-start = (bf16[512,128]{1,0:T(8,128)(2,1)S(1)}, bf16[512,128]{1,0:T(8,128)(2,1)}, u32[]{:S(2)}) copy-start(bf16[512,128]{1,0:T(8,128)(2,1)} %param.8) | copy-start | bytes 393220
  7.2 16.6 %copy-start.10 = (bf16[1,128,768]{2,1,0:T(8,128)(2,1)S(1)}, bf16[1,128,768]{2,1,0:T(8,128)(2,1)}, u32[]{:S(2)}) copy-start(bf16[1,128,768]{2,1,0:T(8,128)(2,1)} %param.6) | copy-start | bytes 589828
  7.2 160.8 %all-gather.3.cloned.1.call-start = ((), (), s32[]{:S(2)}) async-start(), calls=%async_computation | async-start | bytes 8519680 | tf_op jit(solution)/shard_map/all_gather | solution.py:112
  7.2 26.4 %collective-permute-start.9 = (bf16[128,768]{1,0:T(8,128)(2,1)}, bf16[128,768]{1,0:T(8,128)(2,1)}, u32[]{:S(2)}, u32[]{:S(2)}) collective-permute-start(bf16[128,768]{1,0:T(8,128)(2,1)} %bitcast.108), channel_id=1, source_target_pairs={{0,1},{1,2},{2,3},{3,0},{4,5},{5,6},{6,7},{7,4},{8,9},{9,10},{10,1... | collective-permute-start | bytes 589832 | tf_op jit(solution)/shard_map/ppermute | solution.py:20
  9.8 17.0 %collective-permute-start.8 = (bf16[128,768]{1,0:T(8,128)(2,1)}, bf16[128,768]{1,0:T(8,128)(2,1)}, u32[]{:S(2)}, u32[]{:S(2)}) collective-permute-start(bf16[128,768]{1,0:T(8,128)(2,1)} %bitcast.109), channel_id=1, source_target_pairs={{0,2},{1,3},{2,0},{3,1},{4,6},{5,7},{6,4},{7,5},{8,10},{9,11},{10,... | collective-permute-start | bytes 589832 | tf_op jit(solution)/shard_map/ppermute | solution.py:20
  12.8 11.0 %collective-permute-start.7 = (bf16[128,768]{1,0:T(8,128)(2,1)}, bf16[128,768]{1,0:T(8,128)(2,1)}, u32[]{:S(2)}, u32[]{:S(2)}) collective-permute-start(bf16[128,768]{1,0:T(8,128)(2,1)} %bitcast.110), channel_id=1, source_target_pairs={{0,3},{1,0},{2,1},{3,2},{4,7},{5,4},{6,5},{7,6},{8,11},{9,8},{10,9... | collective-permute-start | bytes 589832 | tf_op jit(solution)/shard_map/ppermute | solution.py:20
  13.5 24.8 %collective-permute-start.5 = (bf16[128,768]{1,0:T(8,128)(2,1)}, bf16[128,768]{1,0:T(8,128)(2,1)}, u32[]{:S(2)}, u32[]{:S(2)}) collective-permute-start(bf16[128,768]{1,0:T(8,128)(2,1)} %bitcast.111), channel_id=1, source_target_pairs={{0,64},{64,128},{128,192},{192,0},{1,65},{65,129},{129,193},{193,1... | collective-permute-start | bytes 589832 | tf_op jit(solution)/shard_map/ppermute | solution.py:20
  14.8 25.9 %collective-permute-start.4 = (bf16[128,768]{1,0:T(8,128)(2,1)}, bf16[128,768]{1,0:T(8,128)(2,1)}, u32[]{:S(2)}, u32[]{:S(2)}) collective-permute-start(bf16[128,768]{1,0:T(8,128)(2,1)} %bitcast.112), channel_id=1, source_target_pairs={{0,128},{64,192},{128,0},{192,64},{1,129},{65,193},{129,1},{193,65... | collective-permute-start | bytes 589832 | tf_op jit(solution)/shard_map/ppermute | solution.py:20
  18.3 34.3 %copy-start.12 = (s32[512]{0:T(512)}, s32[512]{0:T(512)S(1)}, u32[]{:S(2)}) copy-start(s32[512]{0:T(512)S(1)} %iota_add_fusion) | copy-start | bytes 6148
  23.8 28.8 %copy-start.14 = (s32[512]{0:T(512)}, s32[512]{0:T(512)S(1)}, u32[]{:S(2)}) copy-start(s32[512]{0:T(512)S(1)} %convert_reduce_fusion.1) | copy-start | bytes 6148
  23.8 16.9 %collective-permute-start.3 = (bf16[128,768]{1,0:T(8,128)(2,1)S(1)}, bf16[128,768]{1,0:T(8,128)(2,1)S(1)}, u32[]{:S(2)}, u32[]{:S(2)}) collective-permute-start(bf16[128,768]{1,0:T(8,128)(2,1)S(1)} %bitcast.113), channel_id=1, source_target_pairs={{0,192},{64,0},{128,64},{192,128},{1,193},{65,1},{129,65},{193,129... | collective-permute-start | bytes 589832 | tf_op jit(solution)/shard_map/ppermute | solution.py:20
  26.8 21.9 %collective-permute-start.2 = (bf16[512,256]{1,0:T(8,128)(2,1)}, bf16[512,256]{1,0:T(8,128)(2,1)S(1)}, u32[]{:S(2)}, u32[]{:S(2)}) collective-permute-start(bf16[512,256]{1,0:T(8,128)(2,1)} %constant_dynamic-update-slice_fusion), channel_id=1, source_target_pairs={{0,3},{4,7},{8,11},{12,15},{16,19},{20,23},{24,27},{28,31},{32,35}... | collective-permute-start | bytes 786440 | tf_op jit(solution)/shard_map/ppermute | solution.py:24
  33.6 15.1 %collective-permute-start.1 = (bf16[512,256]{1,0:T(8,128)(2,1)}, bf16[512,256]{1,0:T(8,128)(2,1)S(1)}, u32[]{:S(2)}, u32[]{:S(2)}) collective-permute-start(bf16[512,256]{1,0:T(8,128)(2,1)} %constant_dynamic-update-slice_fusion), channel_id=1, source_target_pairs={{0,2},{1,3},{4,6},{5,7},{8,10},{9,11},{12,14},{13,15},{16,18},{17,... | collective-permute-start | bytes 786440 | tf_op jit(solution)/shard_map/ppermute | solution.py:24
  38.3 11.2 %collective-permute-start = (bf16[512,256]{1,0:T(8,128)(2,1)}, bf16[512,256]{1,0:T(8,128)(2,1)S(1)}, u32[]{:S(2)}, u32[]{:S(2)}) collective-permute-start(bf16[512,256]{1,0:T(8,128)(2,1)} %constant_dynamic-update-slice_fusion), channel_id=1, source_target_pairs={{0,1},{1,2},{2,3},{4,5},{5,6},{6,7},{8,9},{9,10},{10,11},{12,13},{... | collective-permute-start | bytes 786440 | tf_op jit(solution)/shard_map/ppermute | solution.py:24
  43.6 7.1 %copy-start.8 = (bf16[512,2048]{1,0:T(8,128)(2,1)}, bf16[512,2048]{1,0:T(8,128)(2,1)S(1)}, u32[]{:S(2)}) copy-start(bf16[512,2048]{1,0:T(8,128)(2,1)S(1)} %convolution_convert_fusion) | copy-start | bytes 6291460
  43.7 5.8 %copy-start.11 = (bf16[512,256]{1,0:T(8,128)(2,1)S(1)}, bf16[512,256]{1,0:T(8,128)(2,1)}, u32[]{:S(2)}) copy-start(bf16[512,256]{1,0:T(8,128)(2,1)} %constant_dynamic-update-slice_fusion) | copy-start | bytes 786436
  43.8 14.7 %collective-permute-start.6 = (bf16[512,1024]{1,0:T(8,128)(2,1)S(1)}, bf16[512,1024]{1,0:T(8,128)(2,1)S(1)}, u32[]{:S(2)}, u32[]{:S(2)}) collective-permute-start(bf16[512,1024]{1,0:T(8,128)(2,1)S(1)} %constant_dynamic-slice_fusion.5), channel_id=1, source_target_pairs={{0,4},{4,0},{1,5},{5,1},{2,6},{6,2},{3,7},{7,3},{8,12},{12,8},{9,1... | collective-permute-start | bytes 3145736 | tf_op jit(solution)/shard_map/ppermute | solution.py:20
  50.7 3.8 %copy-start.4 = (f32[2048,512]{1,0:T(8,128)}, f32[2048,512]{1,0:T(8,128)S(1)}, u32[]{:S(2)}) copy-start(f32[2048,512]{1,0:T(8,128)S(1)} %get-tuple-element.37) | copy-start | bytes 12582916
  60.2 19.6 %collective-permute-start.11 = (bf16[4,128,768]{2,1,0:T(8,128)(2,1)}, bf16[4,128,768]{2,1,0:T(8,128)(2,1)S(1)}, u32[]{:S(2)}, u32[]{:S(2)}) collective-permute-start(bf16[4,128,768]{2,1,0:T(8,128)(2,1)} %constant_dynamic-slice_fusion.4), channel_id=1, source_target_pairs={{0,128},{64,192},{128,0},{192,64},{1,129},{65,193},{129,1},{193,65... | collective-permute-start | bytes 2359304 | tf_op jit(solution)/shard_map/ppermute | solution.py:20
  62.0 34.5 %collective-permute-start.10 = (bf16[4,128,768]{2,1,0:T(8,128)(2,1)}, bf16[4,128,768]{2,1,0:T(8,128)(2,1)}, u32[]{:S(2)}, u32[]{:S(2)}) collective-permute-start(bf16[4,128,768]{2,1,0:T(8,128)(2,1)} %constant_dynamic-slice_fusion.4), channel_id=1, source_target_pairs={{0,192},{64,0},{128,64},{192,128},{1,193},{65,1},{129,65},{193,129... | collective-permute-start | bytes 2359304 | tf_op jit(solution)/shard_map/ppermute | solution.py:20
  62.7 35.6 %collective-permute-start.12 = (bf16[4,128,768]{2,1,0:T(8,128)(2,1)}, bf16[4,128,768]{2,1,0:T(8,128)(2,1)}, u32[]{:S(2)}, u32[]{:S(2)}) collective-permute-start(bf16[4,128,768]{2,1,0:T(8,128)(2,1)} %constant_dynamic-slice_fusion.4), channel_id=1, source_target_pairs={{0,64},{64,128},{128,192},{192,0},{1,65},{65,129},{129,193},{193,1... | collective-permute-start | bytes 2359304 | tf_op jit(solution)/shard_map/ppermute | solution.py:20
  64.7 35.2 %collective-permute-start.13 = (bf16[512,256]{1,0:T(8,128)(2,1)S(1)}, bf16[512,256]{1,0:T(8,128)(2,1)S(1)}, u32[]{:S(2)}, u32[]{:S(2)}) collective-permute-start(bf16[512,256]{1,0:T(8,128)(2,1)S(1)} %get-tuple-element.31), channel_id=1, source_target_pairs={{0,8},{8,16},{16,24},{24,0},{1,9},{9,17},{17,25},{25,1},{2,10},{10... | collective-permute-start | bytes 786440 | tf_op jit(solution)/shard_map/ppermute | solution.py:20
  66.0 34.0 %collective-permute-start.15 = (bf16[512,256]{1,0:T(8,128)(2,1)S(1)}, bf16[512,256]{1,0:T(8,128)(2,1)S(1)}, u32[]{:S(2)}, u32[]{:S(2)}) collective-permute-start(bf16[512,256]{1,0:T(8,128)(2,1)S(1)} %get-tuple-element.32), channel_id=1, source_target_pairs={{0,24},{8,0},{16,8},{24,16},{1,25},{9,1},{17,9},{25,17},{2,26},{10... | collective-permute-start | bytes 786440 | tf_op jit(solution)/shard_map/ppermute | solution.py:20
  79.8 20.2 %collective-permute-start.14 = (bf16[512,256]{1,0:T(8,128)(2,1)S(1)}, bf16[512,256]{1,0:T(8,128)(2,1)S(1)}, u32[]{:S(2)}, u32[]{:S(2)}) collective-permute-start(bf16[512,256]{1,0:T(8,128)(2,1)S(1)} %get-tuple-element.33), channel_id=1, source_target_pairs={{0,16},{8,24},{16,0},{24,8},{1,17},{9,25},{17,1},{25,9},{2,18},{10... | collective-permute-start | bytes 786440 | tf_op jit(solution)/shard_map/ppermute | solution.py:20
  100.0 9.1 %copy-start.3 = (f32[512,2048]{0,1:T(8,128)S(1)}, f32[512,2048]{0,1:T(8,128)}, u32[]{:S(2)}) copy-start(f32[512,2048]{0,1:T(8,128)} %copy-done.2) | copy-start | bytes 12582916
  100.2 8.8 %collective-permute-start.16 = (bf16[512,128]{1,0:T(8,128)(2,1)S(1)}, bf16[512,128]{1,0:T(8,128)(2,1)S(1)}, u32[]{:S(2)}, u32[]{:S(2)}) collective-permute-start(bf16[512,128]{1,0:T(8,128)(2,1)S(1)} %constant_dynamic-slice_fusion), channel_id=1, source_target_pairs={{0,32},{32,0},{1,33},{33,1},{2,34},{34,2},{3,35},{35,3},{4,36},{36... | collective-permute-start | bytes 393224 | tf_op jit(solution)/shard_map/ppermute | solution.py:20
  115.6 19.7 %collective-permute-start.17 = (bf16[512,256]{0,1:T(8,128)(2,1)S(1)}, bf16[512,256]{0,1:T(8,128)(2,1)S(1)}, u32[]{:S(2)}, u32[]{:S(2)}) collective-permute-start(bf16[512,256]{0,1:T(8,128)(2,1)S(1)} %get-tuple-element.28), channel_id=1, source_target_pairs={{1,0},{2,1},{3,2},{5,4},{6,5},{7,6},{9,8},{10,9},{11,10},{13,12},{... | collective-permute-start | bytes 786440 | tf_op jit(solution)/shard_map/ppermute | solution.py:24
  116.9 32.0 %collective-permute-start.19 = (bf16[512,256]{0,1:T(8,128)(2,1)S(1)}, bf16[512,256]{0,1:T(8,128)(2,1)S(1)}, u32[]{:S(2)}, u32[]{:S(2)}) collective-permute-start(bf16[512,256]{0,1:T(8,128)(2,1)S(1)} %get-tuple-element.29), channel_id=1, source_target_pairs={{3,0},{7,4},{11,8},{15,12},{19,16},{23,20},{27,24},{31,28},{35,32}... | collective-permute-start | bytes 786440 | tf_op jit(solution)/shard_map/ppermute | solution.py:24
  118.2 35.8 %collective-permute-start.18 = (bf16[512,256]{0,1:T(8,128)(2,1)S(1)}, bf16[512,256]{0,1:T(8,128)(2,1)S(1)}, u32[]{:S(2)}, u32[]{:S(2)}) collective-permute-start(bf16[512,256]{0,1:T(8,128)(2,1)S(1)} %get-tuple-element.30), channel_id=1, source_target_pairs={{2,0},{3,1},{6,4},{7,5},{10,8},{11,9},{14,12},{15,13},{18,16},{19,... | collective-permute-start | bytes 786440 | tf_op jit(solution)/shard_map/ppermute | solution.py:24
  168.0 4.0 %copy-start.6 = (bf16[32768,128]{1,0:T(8,128)(2,1)S(1)}, bf16[32768,128]{1,0:T(8,128)(2,1)}, u32[]{:S(2)}) copy-start(bf16[32768,128]{1,0:T(8,128)(2,1)} %all-gather.3.cloned.1.call-done) | copy-start | bytes 25165828
  168.0 4.1 %copy-start.7 = (bf16[1,4,128,768]{3,2,0,1:T(8,128)(2,1)S(1)}, bf16[1,4,128,768]{3,2,0,1:T(8,128)(2,1)}, u32[]{:S(2)}) copy-start(bf16[1,4,128,768]{3,2,0,1:T(8,128)(2,1)} %get-tuple-element.26) | copy-start | bytes 2359300
  175.9 4.6 %copy-start.1 = (bf16[512,128]{1,0:T(8,128)(2,1)S(1)}, bf16[512,128]{1,0:T(8,128)(2,1)}, u32[]{:S(2)}) copy-start(bf16[512,128]{1,0:T(8,128)(2,1)} %param.8) | copy-start | bytes 393220
  (9 other events, 21.6 us)
Sparse Core Ops, SparseCore 0:
  60.3 107.6 all-gather.2

commit v3 on v2

--- a/solution.py
+++ b/solution.py
@@ -79,7 +79,10 @@
         ).reshape(-1)
         seg_ends = jnp.cumsum(seg_lengths)
         key_seg = segment_count(key_pos, seg_ends)
-        query_pos = me_d * tok_depth + jnp.arange(tok_depth, dtype=jnp.int32)
+        query_rows = roll_rows(query_rows, -me_r * n_tok, 0)
+        query_pos = me_d * tok_depth + (
+            jnp.arange(tok_depth, dtype=jnp.int32) + me_r * n_tok
+        ) % tok_depth
         query_seg = segment_count(query_pos, seg_ends)
         allowed = (query_seg[:, None] == key_seg[None, :]) & (
             key_pos[None, :] <= query_pos[:, None]
@@ -99,7 +102,6 @@
         )
 
         rows_all = rolled_gather(by_depth, "row", n_row, stack_axis=1)
-        context = roll_rows(context, -me_r * n_tok, 0)
 
         weight_perm = jnp.transpose(
             out_weight.reshape(n_zh, n_x, n_core, head_dim, feat), (2, 1, 0, 3, 4)
@@ -113,7 +115,7 @@
         ctx_all = ctx_all.reshape(n_zh, n_dep, n_x, n_core, tok_depth, head_dim)
         partial = pp_reduce_scatter_cols(partial, "x", n_x).astype(jnp.bfloat16)
         partial = pp_reduce_scatter_cols(partial, "zh", n_zh).astype(jnp.bfloat16)
-        context_grad = roll_rows(partial, me_r * n_tok, 0)
+        context_grad = partial
 
         grad_prob = jnp.dot(context_grad, values_all.T, preferred_element_type=jnp.float32)
         delta_row = jnp.sum(prob_full * grad_prob, axis=1, keepdims=True)
@@ -149,6 +151,7 @@
             if depth < n_dep - 1:
                 grad_weight = lax.optimization_barrier(grad_weight)
         grad_weight = grad_weight.reshape(n_zh * n_x * n_core * head_dim, feat)
+        grad_query = roll_rows(grad_query, me_r * n_tok, 0)
         return (grad_weight, grad_query, grad_key, grad_value)
 
     return shards

time: 188 us -> 186 us (0.989)
  local copies, waits for them, and re-layouts: 19.6 us -> 16.9 us
    all_gather x1, waiting for transfers between devices: 12.4 us -> 14.6 us  [shards(): lax.all_gather(context[None], ('zh', DEP, 'x', 'core'), axis=0, tiled=True)]
where the time goes in v3:
time: 186 us
  waiting for transfers between devices  78.2 us (42%)
  starting transfers between devices  41.7 us (22%)
  matrix products  19.5 us (10%)
  local copies, waits for them, and re-layouts  16.9 us (9%)
  other arithmetic  14.7 us (8%)
  between operations  14.6 us (8%)
    ppermute x6, waiting for transfers between devices, shift_open(): lax.ppermute(x, axis, [(i, i + s) for i in range(n) if 0 <= i + s < n])  32.8 us
    ppermute x14, waiting for transfers between devices, shift(): return lax.ppermute(x, axis, [(i, (i + s) % n) for i in range(n)])  30.8 us
    ppermute x14, starting transfers between devices, shift(): return lax.ppermute(x, axis, [(i, (i + s) % n) for i in range(n)])  26.6 us
    ppermute x6, starting transfers between devices, shift_open(): lax.ppermute(x, axis, [(i, i + s) for i in range(n) if 0 <= i + s < n])  15 us
    all_gather x1, waiting for transfers between devices, shards(): lax.all_gather(context[None], ('zh', DEP, 'x', 'core'), axis=0, tiled=True)  14.6 us
    dot_general x4, matrix products, shards(): jnp.einsum('zxcth,tf->zxchf', ctx_all[:, depth], rows_all[depth].reshape(...  11.8 us
    unnamed x51, local copies, waits for them, and re-layouts  9.57 us
  transfers between devices with their start and end apart: 21, of which 9 were waited for; matrix products, arithmetic and copies ran while one was open for 19% of the time, Pallas kernels for 0%

profile of v3, /device:TPU:1, one launch (start us, length us, event | category | flops | bytes accessed | tf_op | source)
XLA Modules:
  0.0 185.7 jit_solution(7708288887920597531)
XLA Ops:
  7.2 2.5 %collective-permute-start.9 = (bf16[128,768]{1,0:T(8,128)(2,1)}, bf16[128,768]{1,0:T(8,128)(2,1)S(1)}, u32[]{:S(2)}, u32[]{:S(2)}) collective-permute-start(bf16[128,768]{1,0:T(8,128)(2,1)} %bitcast.94), channel_id=1, source_target_pairs={{0,1},{1,2},{2,3},{3,0},{4,5},{5,6},{6,7},{7,4},{8,9},{9,10},{10,1... | collective-permute-start | bytes 589832 | tf_op jit(solution)/shard_map/ppermute | solution.py:20
  9.8 3.0 %collective-permute-start.8 = (bf16[128,768]{1,0:T(8,128)(2,1)}, bf16[128,768]{1,0:T(8,128)(2,1)}, u32[]{:S(2)}, u32[]{:S(2)}) collective-permute-start(bf16[128,768]{1,0:T(8,128)(2,1)} %bitcast.95), channel_id=1, source_target_pairs={{0,2},{1,3},{2,0},{3,1},{4,6},{5,7},{6,4},{7,5},{8,10},{9,11},{10,... | collective-permute-start | bytes 589832 | tf_op jit(solution)/shard_map/ppermute | solution.py:20
  14.8 2.6 %collective-permute-start.4 = (bf16[128,768]{1,0:T(8,128)(2,1)}, bf16[128,768]{1,0:T(8,128)(2,1)}, u32[]{:S(2)}, u32[]{:S(2)}) collective-permute-start(bf16[128,768]{1,0:T(8,128)(2,1)} %bitcast.98), channel_id=1, source_target_pairs={{0,128},{64,192},{128,0},{192,64},{1,129},{65,193},{129,1},{193,65... | collective-permute-start | bytes 589832 | tf_op jit(solution)/shard_map/ppermute | solution.py:20
  20.4 2.1 %copy.29 = bf16[2,4,2,128,768]{4,3,2,1,0:T(8,128)(2,1)S(1)} copy(bf16[2,4,2,128,768]{4,3,0,1,2:T(8,128)(2,1)} %bitcast.92) | data formatting | bytes 6291456 | tf_op jit(solution)/shard_map/transpose | solution.py:106
  23.3 1.6 constant_dynamic-update-slice_fusion
  27.7 4.9 %collective-permute-start.2 = (bf16[512,256]{1,0:T(8,128)(2,1)}, bf16[512,256]{1,0:T(8,128)(2,1)S(1)}, u32[]{:S(2)}, u32[]{:S(2)}) collective-permute-start(bf16[512,256]{1,0:T(8,128)(2,1)} %constant_dynamic-update-slice_fusion), channel_id=1, source_target_pairs={{0,3},{4,7},{8,11},{12,15},{16,19},{20,23},{24,27},{28,31},{32,35}... | collective-permute-start | bytes 786440 | tf_op jit(solution)/shard_map/ppermute | solution.py:24
  33.6 3.7 %collective-permute-start.1 = (bf16[512,256]{1,0:T(8,128)(2,1)}, bf16[512,256]{1,0:T(8,128)(2,1)S(1)}, u32[]{:S(2)}, u32[]{:S(2)}) collective-permute-start(bf16[512,256]{1,0:T(8,128)(2,1)} %constant_dynamic-update-slice_fusion), channel_id=1, source_target_pairs={{0,2},{1,3},{4,6},{5,7},{8,10},{9,11},{12,14},{13,15},{16,18},{17,... | collective-permute-start | bytes 786440 | tf_op jit(solution)/shard_map/ppermute | solution.py:24
  37.4 2.3 %collective-permute-start = (bf16[512,256]{1,0:T(8,128)(2,1)}, bf16[512,256]{1,0:T(8,128)(2,1)S(1)}, u32[]{:S(2)}, u32[]{:S(2)}) collective-permute-start(bf16[512,256]{1,0:T(8,128)(2,1)} %constant_dynamic-update-slice_fusion), channel_id=1, source_target_pairs={{0,1},{1,2},{2,3},{4,5},{5,6},{6,7},{8,9},{9,10},{10,11},{12,13},{... | collective-permute-start | bytes 786440 | tf_op jit(solution)/shard_map/ppermute | solution.py:24
  40.9 1.8 convolution_convert_fusion
  46.9 2.5 %collective-permute-done = bf16[512,256]{1,0:T(8,128)(2,1)S(1)} collective-permute-done((bf16[512,256]{1,0:T(8,128)(2,1)}, bf16[512,256]{1,0:T(8,128)(2,1)S(1)}, u32[]{:S(2)}, u32[]{:S(2)}) %collective-permute-start) | collective-permute-done | bytes 262176 | tf_op jit(solution)/shard_map/ppermute | solution.py:24
  49.6 1.6 fusion
  51.3 1.7 fusion.3
  53.0 1.9 %fusion.2 = f32[512,2048]{1,0:T(8,128)S(1)} fusion(f32[512,2048]{1,0:T(8,128)S(1)} %get-tuple-element.37, f32[512]{0:T(512)S(1)} %fusion.3, f32[512]{0:T(512)S(1)} %get-tuple-element.36, s32[2048]{0:T(1024)S(1)} %bitcast.109, s32[2048]{0:T(1024)S(1)} %convert_reduce_fusion, s32[512]{0:T(512)S(1)} %fusion.22, s32[512]{0:T(512)S(1)} %convert_reduce_fusion.1), kind=kLoop, calls=%fused_computation.14 | loop fusion | flops 8388608 | bytes 8413184 | tf_op jit(solution)/shard_map/div | solution.py:98
  54.9 2.0 %copy-done = f32[512,2048]{1,0:T(8,128)} copy-done((f32[512,2048]{1,0:T(8,128)}, f32[512,2048]{1,0:T(8,128)S(1)}, u32[]{:S(2)}) %copy-start) | copy-done | bytes 4194328
  58.3 1.6 add_convert_fusion
  60.0 2.0 %collective-permute-start.11 = (bf16[4,128,768]{2,1,0:T(8,128)(2,1)}, bf16[4,128,768]{2,1,0:T(8,128)(2,1)S(1)}, u32[]{:S(2)}, u32[]{:S(2)}) collective-permute-start(bf16[4,128,768]{2,1,0:T(8,128)(2,1)} %constant_dynamic-slice_fusion.4), channel_id=1, source_target_pairs={{0,128},{64,192},{128,0},{192,64},{1,129},{65,193},{129,1},{193,65... | collective-permute-start | bytes 2359304 | tf_op jit(solution)/shard_map/ppermute | solution.py:20
  67.5 12.2 %collective-permute-done.11 = bf16[4,128,768]{2,1,0:T(8,128)(2,1)S(1)} collective-permute-done((bf16[4,128,768]{2,1,0:T(8,128)(2,1)}, bf16[4,128,768]{2,1,0:T(8,128)(2,1)S(1)}, u32[]{:S(2)}, u32[]{:S(2)}) %collective-permute-start.11) | collective-permute-done | bytes 786464 | tf_op jit(solution)/shard_map/ppermute | solution.py:20
  79.8 2.7 %collective-permute-start.14 = (bf16[512,256]{1,0:T(8,128)(2,1)S(1)}, bf16[512,256]{1,0:T(8,128)(2,1)S(1)}, u32[]{:S(2)}, u32[]{:S(2)}) collective-permute-start(bf16[512,256]{1,0:T(8,128)(2,1)S(1)} %get-tuple-element.33), channel_id=1, source_target_pairs={{0,16},{8,24},{16,0},{24,8},{1,17},{9,25},{17,1},{25,9},{2,18},{10... | collective-permute-start | bytes 786440 | tf_op jit(solution)/shard_map/ppermute | solution.py:20
  82.5 14.0 %collective-permute-done.10 = bf16[4,128,768]{2,1,0:T(8,128)(2,1)} collective-permute-done((bf16[4,128,768]{2,1,0:T(8,128)(2,1)}, bf16[4,128,768]{2,1,0:T(8,128)(2,1)}, u32[]{:S(2)}, u32[]{:S(2)}) %collective-permute-start.10) | collective-permute-done | bytes 786464 | tf_op jit(solution)/shard_map/ppermute | solution.py:20
  96.6 1.8 collective-permute-done.12
  98.4 1.6 pad_maximum_fusion
  100.2 5.2 %collective-permute-start.16 = (bf16[512,128]{1,0:T(8,128)(2,1)S(1)}, bf16[512,128]{1,0:T(8,128)(2,1)S(1)}, u32[]{:S(2)}, u32[]{:S(2)}) collective-permute-start(bf16[512,128]{1,0:T(8,128)(2,1)S(1)} %constant_dynamic-slice_fusion), channel_id=1, source_target_pairs={{0,32},{32,0},{1,33},{33,1},{2,34},{34,2},{3,35},{35,3},{4,36},{36... | collective-permute-start | bytes 393224 | tf_op jit(solution)/shard_map/ppermute | solution.py:20
  106.6 2.6 %collective-permute-done.16 = bf16[512,128]{1,0:T(8,128)(2,1)S(1)} collective-permute-done((bf16[512,128]{1,0:T(8,128)(2,1)S(1)}, bf16[512,128]{1,0:T(8,128)(2,1)S(1)}, u32[]{:S(2)}, u32[]{:S(2)}) %collective-permute-start.16) | collective-permute-done | bytes 131104 | tf_op jit(solution)/shard_map/ppermute | solution.py:20
  110.1 2.2 %multiply_convert_fusion = bf16[512,2048]{1,0:T(8,128)(2,1)S(1)} fusion(f32[512,2048]{1,0:T(8,128)S(1)} %get-tuple-element.39, f32[512]{0:T(512)S(1)} %get-tuple-element.38, f32[512]{0:T(512)S(1)} %copy-done.17, f32[512]{0:T(512)S(1)} %copy-done.15, f32[512,2048]{1,0:T(8,128)S(1)} %copy-done.3, s32[512]{0:T(512)S(1)} %copy-done.11, s32[2048]{0:T(1024)S(1)} %bitcast.110, ...), kind=kLoop, calls=%fused_computation | loop fusion | flops 11534336 | bytes 10512384 | tf_op jit(solution)/shard_map/convert_element_type | solution.py:122
  119.8 12.1 %collective-permute-done.17 = bf16[512,256]{0,1:T(8,128)(2,1)S(1)} collective-permute-done((bf16[512,256]{0,1:T(8,128)(2,1)S(1)}, bf16[512,256]{0,1:T(8,128)(2,1)S(1)}, u32[]{:S(2)}, u32[]{:S(2)}) %collective-permute-start.17) | collective-permute-done | bytes 262176 | tf_op jit(solution)/shard_map/ppermute | solution.py:24
  131.9 12.8 %collective-permute-done.19 = bf16[512,256]{0,1:T(8,128)(2,1)S(1)} collective-permute-done((bf16[512,256]{0,1:T(8,128)(2,1)S(1)}, bf16[512,256]{0,1:T(8,128)(2,1)S(1)}, u32[]{:S(2)}, u32[]{:S(2)}) %collective-permute-start.19) | collective-permute-done | bytes 262176 | tf_op jit(solution)/shard_map/ppermute | solution.py:24
  144.7 5.4 %collective-permute-done.18 = bf16[512,256]{0,1:T(8,128)(2,1)S(1)} collective-permute-done((bf16[512,256]{0,1:T(8,128)(2,1)S(1)}, bf16[512,256]{0,1:T(8,128)(2,1)S(1)}, u32[]{:S(2)}, u32[]{:S(2)}) %collective-permute-start.18) | collective-permute-done | bytes 262176 | tf_op jit(solution)/shard_map/ppermute | solution.py:24
  151.8 14.6 %all-gather.3.cloned.1.call-done = bf16[32768,128]{1,0:T(8,128)(2,1)} async-done(((bf16[512,128]{1,0:T(8,128)(2,1)}), bf16[32768,128]{1,0:T(8,128)(2,1)}) %all-gather.3.cloned.1.call-update) | async-done | bytes 8388624 | tf_op jit(solution)/shard_map/all_gather | solution.py:114
  166.4 3.6 %fusion.4 = f32[2,4,2,128,768]{4,3,2,1,0:T(8,128)S(1)} fusion(bf16[512,768,1,1,1]{1,0,4,3,2:T(8,128)(2,1)S(1)} %bitcast.91, bf16[2,4,4,2,512,128]{5,4,3,2,1,0:T(8,128)(2,1)} %bitcast.79), kind=kOutput, calls=%fused_computation.20 | convolution fusion | flops 1610612736 | bytes 9175040 | tf_op jit(solution)/shard_map/zxcth,tf->zxchf/dot_general | solution.py:144
  170.6 1.8 convolution_add_fusion.2
  172.4 1.8 convolution_add_fusion.1
  174.3 4.5 %convolution_add_fusion = f32[2,4,2,128,768]{4,3,2,1,0:T(8,128)} fusion(f32[2,4,2,128,768]{4,3,2,1,0:T(8,128)S(1)} %convolution_add_fusion.1, bf16[512,768,1,1,1]{1,0,4,3,2:T(8,128)(2,1)S(1)} %bitcast.88, bf16[2,4,4,2,512,128]{5,4,3,2,1,0:T(8,128)(2,1)S(1)} %bitcast.82), kind=kOutput, calls=%fused_computation.8 | convolution fusion | flops 1612185600 | bytes 15466496 | tf_op jit(solution)/shard_map/zxcth,tf->zxchf/dot_general | solution.py:144
  (100 shorter events, 33.9 us)
Async XLA Ops:
  7.2 18.4 %copy-start.8 = (bf16[1,128,768]{2,1,0:T(8,128)(2,1)S(1)}, bf16[1,128,768]{2,1,0:T(8,128)(2,1)}, u32[]{:S(2)}) copy-start(bf16[1,128,768]{2,1,0:T(8,128)(2,1)} %param.6) | copy-start | bytes 589828
  7.2 159.3 %all-gather.3.cloned.1.call-start = ((), (), s32[]{:S(2)}) async-start(), calls=%async_computation | async-start | bytes 8519680 | tf_op jit(solution)/shard_map/all_gather | solution.py:114
  7.2 26.4 %collective-permute-start.9 = (bf16[128,768]{1,0:T(8,128)(2,1)}, bf16[128,768]{1,0:T(8,128)(2,1)S(1)}, u32[]{:S(2)}, u32[]{:S(2)}) collective-permute-start(bf16[128,768]{1,0:T(8,128)(2,1)} %bitcast.94), channel_id=1, source_target_pairs={{0,1},{1,2},{2,3},{3,0},{4,5},{5,6},{6,7},{7,4},{8,9},{9,10},{10,1... | collective-permute-start | bytes 589832 | tf_op jit(solution)/shard_map/ppermute | solution.py:20
  9.8 18.0 %collective-permute-start.8 = (bf16[128,768]{1,0:T(8,128)(2,1)}, bf16[128,768]{1,0:T(8,128)(2,1)}, u32[]{:S(2)}, u32[]{:S(2)}) collective-permute-start(bf16[128,768]{1,0:T(8,128)(2,1)} %bitcast.95), channel_id=1, source_target_pairs={{0,2},{1,3},{2,0},{3,1},{4,6},{5,7},{6,4},{7,5},{8,10},{9,11},{10,... | collective-permute-start | bytes 589832 | tf_op jit(solution)/shard_map/ppermute | solution.py:20
  12.8 12.9 %collective-permute-start.7 = (bf16[128,768]{1,0:T(8,128)(2,1)}, bf16[128,768]{1,0:T(8,128)(2,1)}, u32[]{:S(2)}, u32[]{:S(2)}) collective-permute-start(bf16[128,768]{1,0:T(8,128)(2,1)} %bitcast.96), channel_id=1, source_target_pairs={{0,3},{1,0},{2,1},{3,2},{4,7},{5,4},{6,5},{7,6},{8,11},{9,8},{10,9... | collective-permute-start | bytes 589832 | tf_op jit(solution)/shard_map/ppermute | solution.py:20
  13.5 23.9 %collective-permute-start.5 = (bf16[128,768]{1,0:T(8,128)(2,1)}, bf16[128,768]{1,0:T(8,128)(2,1)}, u32[]{:S(2)}, u32[]{:S(2)}) collective-permute-start(bf16[128,768]{1,0:T(8,128)(2,1)} %bitcast.97), channel_id=1, source_target_pairs={{0,64},{64,128},{128,192},{192,0},{1,65},{65,129},{129,193},{193,1... | collective-permute-start | bytes 589832 | tf_op jit(solution)/shard_map/ppermute | solution.py:20
  14.8 24.9 %collective-permute-start.4 = (bf16[128,768]{1,0:T(8,128)(2,1)}, bf16[128,768]{1,0:T(8,128)(2,1)}, u32[]{:S(2)}, u32[]{:S(2)}) collective-permute-start(bf16[128,768]{1,0:T(8,128)(2,1)} %bitcast.98), channel_id=1, source_target_pairs={{0,128},{64,192},{128,0},{192,64},{1,129},{65,193},{129,1},{193,65... | collective-permute-start | bytes 589832 | tf_op jit(solution)/shard_map/ppermute | solution.py:20
  22.5 30.4 %copy-start.10 = (s32[512]{0:T(512)}, s32[512]{0:T(512)S(1)}, u32[]{:S(2)}) copy-start(s32[512]{0:T(512)S(1)} %fusion.22) | copy-start | bytes 6148
  25.6 27.4 %copy-start.12 = (s32[512]{0:T(512)}, s32[512]{0:T(512)S(1)}, u32[]{:S(2)}) copy-start(s32[512]{0:T(512)S(1)} %convert_reduce_fusion.1) | copy-start | bytes 6148
  25.6 14.1 %collective-permute-start.3 = (bf16[128,768]{1,0:T(8,128)(2,1)S(1)}, bf16[128,768]{1,0:T(8,128)(2,1)S(1)}, u32[]{:S(2)}, u32[]{:S(2)}) collective-permute-start(bf16[128,768]{1,0:T(8,128)(2,1)S(1)} %bitcast.99), channel_id=1, source_target_pairs={{0,192},{64,0},{128,64},{192,128},{1,193},{65,1},{129,65},{193,129... | collective-permute-start | bytes 589832 | tf_op jit(solution)/shard_map/ppermute | solution.py:20
  27.7 19.2 %collective-permute-start.2 = (bf16[512,256]{1,0:T(8,128)(2,1)}, bf16[512,256]{1,0:T(8,128)(2,1)S(1)}, u32[]{:S(2)}, u32[]{:S(2)}) collective-permute-start(bf16[512,256]{1,0:T(8,128)(2,1)} %constant_dynamic-update-slice_fusion), channel_id=1, source_target_pairs={{0,3},{4,7},{8,11},{12,15},{16,19},{20,23},{24,27},{28,31},{32,35}... | collective-permute-start | bytes 786440 | tf_op jit(solution)/shard_map/ppermute | solution.py:24
  33.6 13.3 %collective-permute-start.1 = (bf16[512,256]{1,0:T(8,128)(2,1)}, bf16[512,256]{1,0:T(8,128)(2,1)S(1)}, u32[]{:S(2)}, u32[]{:S(2)}) collective-permute-start(bf16[512,256]{1,0:T(8,128)(2,1)} %constant_dynamic-update-slice_fusion), channel_id=1, source_target_pairs={{0,2},{1,3},{4,6},{5,7},{8,10},{9,11},{12,14},{13,15},{16,18},{17,... | collective-permute-start | bytes 786440 | tf_op jit(solution)/shard_map/ppermute | solution.py:24
  37.4 12.1 %collective-permute-start = (bf16[512,256]{1,0:T(8,128)(2,1)}, bf16[512,256]{1,0:T(8,128)(2,1)S(1)}, u32[]{:S(2)}, u32[]{:S(2)}) collective-permute-start(bf16[512,256]{1,0:T(8,128)(2,1)} %constant_dynamic-update-slice_fusion), channel_id=1, source_target_pairs={{0,1},{1,2},{2,3},{4,5},{5,6},{6,7},{8,9},{9,10},{10,11},{12,13},{... | collective-permute-start | bytes 786440 | tf_op jit(solution)/shard_map/ppermute | solution.py:24
  42.7 8.5 %copy-start.6 = (bf16[512,2048]{1,0:T(8,128)(2,1)}, bf16[512,2048]{1,0:T(8,128)(2,1)S(1)}, u32[]{:S(2)}) copy-start(bf16[512,2048]{1,0:T(8,128)(2,1)S(1)} %convolution_convert_fusion) | copy-start | bytes 6291460
  42.7 6.8 %copy-start.9 = (bf16[512,256]{1,0:T(8,128)(2,1)S(1)}, bf16[512,256]{1,0:T(8,128)(2,1)}, u32[]{:S(2)}) copy-start(bf16[512,256]{1,0:T(8,128)(2,1)} %constant_dynamic-update-slice_fusion) | copy-start | bytes 786436
  42.7 6.9 %copy-start.18 = (bf16[512,128]{1,0:T(8,128)(2,1)S(1)}, bf16[512,128]{1,0:T(8,128)(2,1)}, u32[]{:S(2)}) copy-start(bf16[512,128]{1,0:T(8,128)(2,1)} %param.8) | copy-start | bytes 393220
  42.8 15.5 %collective-permute-start.6 = (bf16[512,1024]{1,0:T(8,128)(2,1)S(1)}, bf16[512,1024]{1,0:T(8,128)(2,1)S(1)}, u32[]{:S(2)}, u32[]{:S(2)}) collective-permute-start(bf16[512,1024]{1,0:T(8,128)(2,1)S(1)} %constant_dynamic-slice_fusion.5), channel_id=1, source_target_pairs={{0,4},{4,0},{1,5},{5,1},{2,6},{6,2},{3,7},{7,3},{8,12},{12,8},{9,1... | collective-permute-start | bytes 3145736 | tf_op jit(solution)/shard_map/ppermute | solution.py:20
  45.9 5.3 %copy-start.7 = (bf16[8,128,768]{2,1,0:T(8,128)(2,1)}, bf16[8,128,768]{2,1,0:T(8,128)(2,1)S(1)}, u32[]{:S(2)}) copy-start(bf16[8,128,768]{2,1,0:T(8,128)(2,1)S(1)} %bitcast_dynamic-update-slice_fusion.1) | copy-start | bytes 4718596
  51.2 3.7 %copy-start.2 = (f32[512,2048]{1,0:T(8,128)}, f32[512,2048]{1,0:T(8,128)S(1)}, u32[]{:S(2)}) copy-start(f32[512,2048]{1,0:T(8,128)S(1)} %get-tuple-element.37) | copy-start | bytes 12582916
  60.0 19.8 %collective-permute-start.11 = (bf16[4,128,768]{2,1,0:T(8,128)(2,1)}, bf16[4,128,768]{2,1,0:T(8,128)(2,1)S(1)}, u32[]{:S(2)}, u32[]{:S(2)}) collective-permute-start(bf16[4,128,768]{2,1,0:T(8,128)(2,1)} %constant_dynamic-slice_fusion.4), channel_id=1, source_target_pairs={{0,128},{64,192},{128,0},{192,64},{1,129},{65,193},{129,1},{193,65... | collective-permute-start | bytes 2359304 | tf_op jit(solution)/shard_map/ppermute | solution.py:20
  62.0 34.5 %collective-permute-start.10 = (bf16[4,128,768]{2,1,0:T(8,128)(2,1)}, bf16[4,128,768]{2,1,0:T(8,128)(2,1)}, u32[]{:S(2)}, u32[]{:S(2)}) collective-permute-start(bf16[4,128,768]{2,1,0:T(8,128)(2,1)} %constant_dynamic-slice_fusion.4), channel_id=1, source_target_pairs={{0,192},{64,0},{128,64},{192,128},{1,193},{65,1},{129,65},{193,129... | collective-permute-start | bytes 2359304 | tf_op jit(solution)/shard_map/ppermute | solution.py:20
  62.8 35.6 %collective-permute-start.12 = (bf16[4,128,768]{2,1,0:T(8,128)(2,1)}, bf16[4,128,768]{2,1,0:T(8,128)(2,1)}, u32[]{:S(2)}, u32[]{:S(2)}) collective-permute-start(bf16[4,128,768]{2,1,0:T(8,128)(2,1)} %constant_dynamic-slice_fusion.4), channel_id=1, source_target_pairs={{0,64},{64,128},{128,192},{192,0},{1,65},{65,129},{129,193},{193,1... | collective-permute-start | bytes 2359304 | tf_op jit(solution)/shard_map/ppermute | solution.py:20
  64.8 35.2 %collective-permute-start.13 = (bf16[512,256]{1,0:T(8,128)(2,1)S(1)}, bf16[512,256]{1,0:T(8,128)(2,1)S(1)}, u32[]{:S(2)}, u32[]{:S(2)}) collective-permute-start(bf16[512,256]{1,0:T(8,128)(2,1)S(1)} %get-tuple-element.31), channel_id=1, source_target_pairs={{0,8},{8,16},{16,24},{24,0},{1,9},{9,17},{17,25},{25,1},{2,10},{10... | collective-permute-start | bytes 786440 | tf_op jit(solution)/shard_map/ppermute | solution.py:20
  66.1 33.9 %collective-permute-start.15 = (bf16[512,256]{1,0:T(8,128)(2,1)S(1)}, bf16[512,256]{1,0:T(8,128)(2,1)S(1)}, u32[]{:S(2)}, u32[]{:S(2)}) collective-permute-start(bf16[512,256]{1,0:T(8,128)(2,1)S(1)} %get-tuple-element.32), channel_id=1, source_target_pairs={{0,24},{8,0},{16,8},{24,16},{1,25},{9,1},{17,9},{25,17},{2,26},{10... | collective-permute-start | bytes 786440 | tf_op jit(solution)/shard_map/ppermute | solution.py:20
  79.8 20.2 %collective-permute-start.14 = (bf16[512,256]{1,0:T(8,128)(2,1)S(1)}, bf16[512,256]{1,0:T(8,128)(2,1)S(1)}, u32[]{:S(2)}, u32[]{:S(2)}) collective-permute-start(bf16[512,256]{1,0:T(8,128)(2,1)S(1)} %get-tuple-element.33), channel_id=1, source_target_pairs={{0,16},{8,24},{16,0},{24,8},{1,17},{9,25},{17,1},{25,9},{2,18},{10... | collective-permute-start | bytes 786440 | tf_op jit(solution)/shard_map/ppermute | solution.py:20
  100.0 9.2 %copy-start.1 = (f32[512,2048]{1,0:T(8,128)S(1)}, f32[512,2048]{1,0:T(8,128)}, u32[]{:S(2)}) copy-start(f32[512,2048]{1,0:T(8,128)} %copy-done) | copy-start | bytes 12582916
  100.2 9.0 %collective-permute-start.16 = (bf16[512,128]{1,0:T(8,128)(2,1)S(1)}, bf16[512,128]{1,0:T(8,128)(2,1)S(1)}, u32[]{:S(2)}, u32[]{:S(2)}) collective-permute-start(bf16[512,128]{1,0:T(8,128)(2,1)S(1)} %constant_dynamic-slice_fusion), channel_id=1, source_target_pairs={{0,32},{32,0},{1,33},{33,1},{2,34},{34,2},{3,35},{35,3},{4,36},{36... | collective-permute-start | bytes 393224 | tf_op jit(solution)/shard_map/ppermute | solution.py:20
  113.8 18.1 %collective-permute-start.17 = (bf16[512,256]{0,1:T(8,128)(2,1)S(1)}, bf16[512,256]{0,1:T(8,128)(2,1)S(1)}, u32[]{:S(2)}, u32[]{:S(2)}) collective-permute-start(bf16[512,256]{0,1:T(8,128)(2,1)S(1)} %get-tuple-element.28), channel_id=1, source_target_pairs={{1,0},{2,1},{3,2},{5,4},{6,5},{7,6},{9,8},{10,9},{11,10},{13,12},{... | collective-permute-start | bytes 786440 | tf_op jit(solution)/shard_map/ppermute | solution.py:24
  115.1 29.6 %collective-permute-start.19 = (bf16[512,256]{0,1:T(8,128)(2,1)S(1)}, bf16[512,256]{0,1:T(8,128)(2,1)S(1)}, u32[]{:S(2)}, u32[]{:S(2)}) collective-permute-start(bf16[512,256]{0,1:T(8,128)(2,1)S(1)} %get-tuple-element.29), channel_id=1, source_target_pairs={{3,0},{7,4},{11,8},{15,12},{19,16},{23,20},{27,24},{31,28},{35,32}... | collective-permute-start | bytes 786440 | tf_op jit(solution)/shard_map/ppermute | solution.py:24
  116.4 33.7 %collective-permute-start.18 = (bf16[512,256]{0,1:T(8,128)(2,1)S(1)}, bf16[512,256]{0,1:T(8,128)(2,1)S(1)}, u32[]{:S(2)}, u32[]{:S(2)}) collective-permute-start(bf16[512,256]{0,1:T(8,128)(2,1)S(1)} %get-tuple-element.30), channel_id=1, source_target_pairs={{2,0},{3,1},{6,4},{7,5},{10,8},{11,9},{14,12},{15,13},{18,16},{19,... | collective-permute-start | bytes 786440 | tf_op jit(solution)/shard_map/ppermute | solution.py:24
  166.4 4.0 %copy-start.4 = (bf16[32768,128]{1,0:T(8,128)(2,1)S(1)}, bf16[32768,128]{1,0:T(8,128)(2,1)}, u32[]{:S(2)}) copy-start(bf16[32768,128]{1,0:T(8,128)(2,1)} %all-gather.3.cloned.1.call-done) | copy-start | bytes 25165828
  166.4 4.1 %copy-start.5 = (bf16[1,4,128,768]{3,2,0,1:T(8,128)(2,1)S(1)}, bf16[1,4,128,768]{3,2,0,1:T(8,128)(2,1)}, u32[]{:S(2)}) copy-start(bf16[1,4,128,768]{3,2,0,1:T(8,128)(2,1)} %get-tuple-element.26) | copy-start | bytes 2359300
  (9 other events, 27.3 us)
Sparse Core Ops, SparseCore 0:
  60.1 106.2 all-gather.2

commit v4 on v3

--- a/solution.py
+++ b/solution.py
@@ -95,7 +95,7 @@
         row_max = jnp.max(masked, axis=1, keepdims=True)
         exponent = jnp.where(allowed, jnp.exp(masked - row_max), 0.0)
         row_sum = jnp.sum(exponent, axis=1, keepdims=True)
-        prob_full = exponent / row_sum
+        prob_full = exponent * (1.0 / row_sum)
         prob_half = prob_full.astype(jnp.bfloat16)
         context = jnp.dot(prob_half, values_all, preferred_element_type=jnp.float32).astype(
             jnp.bfloat16

time: 186 us -> 184 us (0.989)
  other arithmetic: 14.7 us -> 9.34 us
    ppermute x6, waiting for transfers between devices: 32.8 us -> 35.5 us  [shift_open(): lax.ppermute(x, axis, [(i, i + s) for i in range(n) if 0 <= i + s < n])]
    div x1, other arithmetic: 1.9 us -> 0.01 us  [shards(): prob_full = exponent * (1.0 / row_sum)]
    unnamed x51 -> x29, local copies, waits for them, and re-layouts: 9.57 us -> 9.75 us
  transfers between devices with their start and end apart: 21 -> 21, of which waited for: 9 -> 9; matrix products, arithmetic and copies ran while one was open for 19% -> 16% of each run, Pallas kernels for 0% -> 0%
where the time goes in v4:
time: 184 us; the launch traced here: 183 us
  waiting for transfers between devices  79.2 us (43%)
  starting transfers between devices  43.4 us (24%)
  matrix products  19.8 us (11%)
  local copies, waits for them, and re-layouts  17.1 us (9%)
  between operations  14.5 us (8%)
  other arithmetic  9.34 us (5%)
    ppermute x6, waiting for transfers between devices, shift_open(): lax.ppermute(x, axis, [(i, i + s) for i in range(n) if 0 <= i + s < n])  35.5 us
    ppermute x14, waiting for transfers between devices, shift(): return lax.ppermute(x, axis, [(i, (i + s) % n) for i in range(n)])  30.5 us
    ppermute x14, starting transfers between devices, shift(): return lax.ppermute(x, axis, [(i, (i + s) % n) for i in range(n)])  27.4 us
    ppermute x6, starting transfers between devices, shift_open(): lax.ppermute(x, axis, [(i, i + s) for i in range(n) if 0 <= i + s < n])  16 us
    all_gather x1, waiting for transfers between devices, shards(): lax.all_gather(context[None], ('zh', DEP, 'x', 'core'), axis=0, tiled=True)  13.1 us
    dot_general x4, matrix products, shards(): jnp.einsum('zxcth,tf->zxchf', ctx_all[:, depth], rows_all[depth].reshape(...  11.9 us
    unnamed x29, local copies, waits for them, and re-layouts  9.75 us
  transfers between devices with their start and end apart: 21, of which 9 were waited for; matrix products, arithmetic and copies ran while one was open for 16% of the time, Pallas kernels for 0%

profile of v4, /device:TPU:1, one launch (start us, length us, event | category | flops | bytes accessed | tf_op | source)
XLA Modules:
  0.0 183.4 jit_solution(11711248294257555217)
XLA Ops:
  7.2 2.5 %collective-permute-start.9 = (bf16[128,768]{1,0:T(8,128)(2,1)}, bf16[128,768]{1,0:T(8,128)(2,1)S(1)}, u32[]{:S(2)}, u32[]{:S(2)}) collective-permute-start(bf16[128,768]{1,0:T(8,128)(2,1)} %bitcast.94), channel_id=1, source_target_pairs={{0,1},{1,2},{2,3},{3,0},{4,5},{5,6},{6,7},{7,4},{8,9},{9,10},{10,1... | collective-permute-start | bytes 589832 | tf_op jit(solution)/shard_map/ppermute | solution.py:20
  9.8 3.0 %collective-permute-start.8 = (bf16[128,768]{1,0:T(8,128)(2,1)}, bf16[128,768]{1,0:T(8,128)(2,1)}, u32[]{:S(2)}, u32[]{:S(2)}) collective-permute-start(bf16[128,768]{1,0:T(8,128)(2,1)} %bitcast.95), channel_id=1, source_target_pairs={{0,2},{1,3},{2,0},{3,1},{4,6},{5,7},{6,4},{7,5},{8,10},{9,11},{10,... | collective-permute-start | bytes 589832 | tf_op jit(solution)/shard_map/ppermute | solution.py:20
  14.8 2.6 %collective-permute-start.4 = (bf16[128,768]{1,0:T(8,128)(2,1)}, bf16[128,768]{1,0:T(8,128)(2,1)}, u32[]{:S(2)}, u32[]{:S(2)}) collective-permute-start(bf16[128,768]{1,0:T(8,128)(2,1)} %bitcast.98), channel_id=1, source_target_pairs={{0,128},{64,192},{128,0},{192,64},{1,129},{65,193},{129,1},{193,65... | collective-permute-start | bytes 589832 | tf_op jit(solution)/shard_map/ppermute | solution.py:20
  18.3 1.6 constant_dynamic-update-slice_fusion.1
  19.9 2.1 %copy.29 = bf16[2,4,2,128,768]{4,3,2,1,0:T(8,128)(2,1)S(1)} copy(bf16[2,4,2,128,768]{4,3,0,1,2:T(8,128)(2,1)} %bitcast.92) | data formatting | bytes 6291456 | tf_op jit(solution)/shard_map/transpose | solution.py:106
  22.1 1.6 constant_dynamic-update-slice_fusion
  23.8 2.0 %collective-permute-start.3 = (bf16[128,768]{1,0:T(8,128)(2,1)S(1)}, bf16[128,768]{1,0:T(8,128)(2,1)S(1)}, u32[]{:S(2)}, u32[]{:S(2)}) collective-permute-start(bf16[128,768]{1,0:T(8,128)(2,1)S(1)} %bitcast.99), channel_id=1, source_target_pairs={{0,192},{64,0},{128,64},{192,128},{1,193},{65,1},{129,65},{193,129... | collective-permute-start | bytes 589832 | tf_op jit(solution)/shard_map/ppermute | solution.py:20
  26.8 5.9 %collective-permute-start.2 = (bf16[512,256]{1,0:T(8,128)(2,1)}, bf16[512,256]{1,0:T(8,128)(2,1)S(1)}, u32[]{:S(2)}, u32[]{:S(2)}) collective-permute-start(bf16[512,256]{1,0:T(8,128)(2,1)} %constant_dynamic-update-slice_fusion), channel_id=1, source_target_pairs={{0,3},{4,7},{8,11},{12,15},{16,19},{20,23},{24,27},{28,31},{32,35}... | collective-permute-start | bytes 786440 | tf_op jit(solution)/shard_map/ppermute | solution.py:24
  33.6 3.7 %collective-permute-start.1 = (bf16[512,256]{1,0:T(8,128)(2,1)}, bf16[512,256]{1,0:T(8,128)(2,1)S(1)}, u32[]{:S(2)}, u32[]{:S(2)}) collective-permute-start(bf16[512,256]{1,0:T(8,128)(2,1)} %constant_dynamic-update-slice_fusion), channel_id=1, source_target_pairs={{0,2},{1,3},{4,6},{5,7},{8,10},{9,11},{12,14},{13,15},{16,18},{17,... | collective-permute-start | bytes 786440 | tf_op jit(solution)/shard_map/ppermute | solution.py:24
  37.4 2.3 %collective-permute-start = (bf16[512,256]{1,0:T(8,128)(2,1)}, bf16[512,256]{1,0:T(8,128)(2,1)S(1)}, u32[]{:S(2)}, u32[]{:S(2)}) collective-permute-start(bf16[512,256]{1,0:T(8,128)(2,1)} %constant_dynamic-update-slice_fusion), channel_id=1, source_target_pairs={{0,1},{1,2},{2,3},{4,5},{5,6},{6,7},{8,9},{9,10},{10,11},{12,13},{... | collective-permute-start | bytes 786440 | tf_op jit(solution)/shard_map/ppermute | solution.py:24
  40.9 1.8 convolution_convert_fusion
  47.0 2.5 %collective-permute-done = bf16[512,256]{1,0:T(8,128)(2,1)S(1)} collective-permute-done((bf16[512,256]{1,0:T(8,128)(2,1)}, bf16[512,256]{1,0:T(8,128)(2,1)S(1)}, u32[]{:S(2)}, u32[]{:S(2)}) %collective-permute-start) | collective-permute-done | bytes 262176 | tf_op jit(solution)/shard_map/ppermute | solution.py:24
  49.6 1.6 fusion
  51.2 1.7 fusion.21
  53.0 2.0 %copy-done = f32[512,2048]{1,0:T(8,128)} copy-done((f32[512,2048]{1,0:T(8,128)}, f32[512,2048]{1,0:T(8,128)S(1)}, u32[]{:S(2)}) %copy-start) | copy-done | bytes 4194328
  56.4 1.6 add_convert_fusion
  58.0 1.9 %collective-permute-start.11 = (bf16[4,128,768]{2,1,0:T(8,128)(2,1)}, bf16[4,128,768]{2,1,0:T(8,128)(2,1)S(1)}, u32[]{:S(2)}, u32[]{:S(2)}) collective-permute-start(bf16[4,128,768]{2,1,0:T(8,128)(2,1)} %constant_dynamic-slice_fusion.4), channel_id=1, source_target_pairs={{0,128},{64,192},{128,0},{192,64},{1,129},{65,193},{129,1},{193,65... | collective-permute-start | bytes 2359304 | tf_op jit(solution)/shard_map/ppermute | solution.py:20
  65.4 12.2 %collective-permute-done.11 = bf16[4,128,768]{2,1,0:T(8,128)(2,1)S(1)} collective-permute-done((bf16[4,128,768]{2,1,0:T(8,128)(2,1)}, bf16[4,128,768]{2,1,0:T(8,128)(2,1)S(1)}, u32[]{:S(2)}, u32[]{:S(2)}) %collective-permute-start.11) | collective-permute-done | bytes 786464 | tf_op jit(solution)/shard_map/ppermute | solution.py:20
  77.6 2.7 %collective-permute-start.14 = (bf16[512,256]{1,0:T(8,128)(2,1)S(1)}, bf16[512,256]{1,0:T(8,128)(2,1)S(1)}, u32[]{:S(2)}, u32[]{:S(2)}) collective-permute-start(bf16[512,256]{1,0:T(8,128)(2,1)S(1)} %get-tuple-element.35), channel_id=1, source_target_pairs={{0,16},{8,24},{16,0},{24,8},{1,17},{9,25},{17,1},{25,9},{2,18},{10... | collective-permute-start | bytes 786440 | tf_op jit(solution)/shard_map/ppermute | solution.py:20
  80.4 14.0 %collective-permute-done.10 = bf16[4,128,768]{2,1,0:T(8,128)(2,1)} collective-permute-done((bf16[4,128,768]{2,1,0:T(8,128)(2,1)}, bf16[4,128,768]{2,1,0:T(8,128)(2,1)}, u32[]{:S(2)}, u32[]{:S(2)}) %collective-permute-start.10) | collective-permute-done | bytes 786464 | tf_op jit(solution)/shard_map/ppermute | solution.py:20
  94.4 1.8 collective-permute-done.12
  96.2 1.6 pad_maximum_fusion
  98.0 5.2 %collective-permute-start.16 = (bf16[512,128]{1,0:T(8,128)(2,1)S(1)}, bf16[512,128]{1,0:T(8,128)(2,1)S(1)}, u32[]{:S(2)}, u32[]{:S(2)}) collective-permute-start(bf16[512,128]{1,0:T(8,128)(2,1)S(1)} %constant_dynamic-slice_fusion), channel_id=1, source_target_pairs={{0,32},{32,0},{1,33},{33,1},{2,34},{34,2},{3,35},{35,3},{4,36},{36... | collective-permute-start | bytes 393224 | tf_op jit(solution)/shard_map/ppermute | solution.py:20
  104.4 2.4 %collective-permute-done.16 = bf16[512,128]{1,0:T(8,128)(2,1)S(1)} collective-permute-done((bf16[512,128]{1,0:T(8,128)(2,1)S(1)}, bf16[512,128]{1,0:T(8,128)(2,1)S(1)}, u32[]{:S(2)}, u32[]{:S(2)}) %collective-permute-start.16) | collective-permute-done | bytes 131104 | tf_op jit(solution)/shard_map/ppermute | solution.py:20
  116.2 14.3 %collective-permute-done.17 = bf16[512,256]{0,1:T(8,128)(2,1)S(1)} collective-permute-done((bf16[512,256]{0,1:T(8,128)(2,1)S(1)}, bf16[512,256]{0,1:T(8,128)(2,1)S(1)}, u32[]{:S(2)}, u32[]{:S(2)}) %collective-permute-start.17) | collective-permute-done | bytes 262176 | tf_op jit(solution)/shard_map/ppermute | solution.py:24
  130.5 10.7 %collective-permute-done.19 = bf16[512,256]{0,1:T(8,128)(2,1)S(1)} collective-permute-done((bf16[512,256]{0,1:T(8,128)(2,1)S(1)}, bf16[512,256]{0,1:T(8,128)(2,1)S(1)}, u32[]{:S(2)}, u32[]{:S(2)}) %collective-permute-start.19) | collective-permute-done | bytes 262176 | tf_op jit(solution)/shard_map/ppermute | solution.py:24
  141.2 8.0 %collective-permute-done.18 = bf16[512,256]{0,1:T(8,128)(2,1)S(1)} collective-permute-done((bf16[512,256]{0,1:T(8,128)(2,1)S(1)}, bf16[512,256]{0,1:T(8,128)(2,1)S(1)}, u32[]{:S(2)}, u32[]{:S(2)}) %collective-permute-start.18) | collective-permute-done | bytes 262176 | tf_op jit(solution)/shard_map/ppermute | solution.py:24
  150.9 13.1 %all-gather.3.cloned.1.call-done = bf16[32768,128]{1,0:T(8,128)(2,1)} async-done(((bf16[512,128]{1,0:T(8,128)(2,1)}), bf16[32768,128]{1,0:T(8,128)(2,1)}) %all-gather.3.cloned.1.call-update) | async-done | bytes 8388624 | tf_op jit(solution)/shard_map/all_gather | solution.py:114
  164.0 3.7 %fusion.2 = f32[2,4,2,128,768]{4,3,2,1,0:T(8,128)S(1)} fusion(bf16[512,768,1,1,1]{1,0,4,3,2:T(8,128)(2,1)} %bitcast.91, bf16[2,4,4,2,512,128]{5,4,3,2,1,0:T(8,128)(2,1)} %bitcast.79), kind=kOutput, calls=%fused_computation.19 | convolution fusion | flops 1610612736 | bytes 9175040 | tf_op jit(solution)/shard_map/zxcth,tf->zxchf/dot_general | solution.py:144
  168.3 1.8 convolution_add_fusion.2
  170.1 1.8 convolution_add_fusion.1
  172.0 4.5 %convolution_add_fusion = f32[2,4,2,128,768]{4,3,2,1,0:T(8,128)} fusion(f32[2,4,2,128,768]{4,3,2,1,0:T(8,128)S(1)} %convolution_add_fusion.1, bf16[512,768,1,1,1]{1,0,4,3,2:T(8,128)(2,1)S(1)} %bitcast.88, bf16[2,4,4,2,512,128]{5,4,3,2,1,0:T(8,128)(2,1)S(1)} %bitcast.82), kind=kOutput, calls=%fused_computation.9 | convolution fusion | flops 1612185600 | bytes 15466496 | tf_op jit(solution)/shard_map/zxcth,tf->zxchf/dot_general | solution.py:144
  (78 shorter events, 30.4 us)
Async XLA Ops:
  7.2 16.6 %copy-start.5 = (bf16[1,128,768]{2,1,0:T(8,128)(2,1)S(1)}, bf16[1,128,768]{2,1,0:T(8,128)(2,1)}, u32[]{:S(2)}) copy-start(bf16[1,128,768]{2,1,0:T(8,128)(2,1)} %param.6) | copy-start | bytes 589828
  7.2 156.9 %all-gather.3.cloned.1.call-start = ((), (), s32[]{:S(2)}) async-start(), calls=%async_computation | async-start | bytes 8519680 | tf_op jit(solution)/shard_map/all_gather | solution.py:114
  7.2 26.4 %collective-permute-start.9 = (bf16[128,768]{1,0:T(8,128)(2,1)}, bf16[128,768]{1,0:T(8,128)(2,1)S(1)}, u32[]{:S(2)}, u32[]{:S(2)}) collective-permute-start(bf16[128,768]{1,0:T(8,128)(2,1)} %bitcast.94), channel_id=1, source_target_pairs={{0,1},{1,2},{2,3},{3,0},{4,5},{5,6},{6,7},{7,4},{8,9},{9,10},{10,1... | collective-permute-start | bytes 589832 | tf_op jit(solution)/shard_map/ppermute | solution.py:20
  9.8 17.0 %collective-permute-start.8 = (bf16[128,768]{1,0:T(8,128)(2,1)}, bf16[128,768]{1,0:T(8,128)(2,1)}, u32[]{:S(2)}, u32[]{:S(2)}) collective-permute-start(bf16[128,768]{1,0:T(8,128)(2,1)} %bitcast.95), channel_id=1, source_target_pairs={{0,2},{1,3},{2,0},{3,1},{4,6},{5,7},{6,4},{7,5},{8,10},{9,11},{10,... | collective-permute-start | bytes 589832 | tf_op jit(solution)/shard_map/ppermute | solution.py:20
  12.8 11.0 %collective-permute-start.7 = (bf16[128,768]{1,0:T(8,128)(2,1)}, bf16[128,768]{1,0:T(8,128)(2,1)}, u32[]{:S(2)}, u32[]{:S(2)}) collective-permute-start(bf16[128,768]{1,0:T(8,128)(2,1)} %bitcast.96), channel_id=1, source_target_pairs={{0,3},{1,0},{2,1},{3,2},{4,7},{5,4},{6,5},{7,6},{8,11},{9,8},{10,9... | collective-permute-start | bytes 589832 | tf_op jit(solution)/shard_map/ppermute | solution.py:20
  13.5 23.9 %collective-permute-start.5 = (bf16[128,768]{1,0:T(8,128)(2,1)}, bf16[128,768]{1,0:T(8,128)(2,1)}, u32[]{:S(2)}, u32[]{:S(2)}) collective-permute-start(bf16[128,768]{1,0:T(8,128)(2,1)} %bitcast.97), channel_id=1, source_target_pairs={{0,64},{64,128},{128,192},{192,0},{1,65},{65,129},{129,193},{193,1... | collective-permute-start | bytes 589832 | tf_op jit(solution)/shard_map/ppermute | solution.py:20
  14.8 24.9 %collective-permute-start.4 = (bf16[128,768]{1,0:T(8,128)(2,1)}, bf16[128,768]{1,0:T(8,128)(2,1)}, u32[]{:S(2)}, u32[]{:S(2)}) collective-permute-start(bf16[128,768]{1,0:T(8,128)(2,1)} %bitcast.98), channel_id=1, source_target_pairs={{0,128},{64,192},{128,0},{192,64},{1,129},{65,193},{129,1},{193,65... | collective-permute-start | bytes 589832 | tf_op jit(solution)/shard_map/ppermute | solution.py:20
  23.8 15.9 %collective-permute-start.3 = (bf16[128,768]{1,0:T(8,128)(2,1)S(1)}, bf16[128,768]{1,0:T(8,128)(2,1)S(1)}, u32[]{:S(2)}, u32[]{:S(2)}) collective-permute-start(bf16[128,768]{1,0:T(8,128)(2,1)S(1)} %bitcast.99), channel_id=1, source_target_pairs={{0,192},{64,0},{128,64},{192,128},{1,193},{65,1},{129,65},{193,129... | collective-permute-start | bytes 589832 | tf_op jit(solution)/shard_map/ppermute | solution.py:20
  26.8 20.2 %collective-permute-start.2 = (bf16[512,256]{1,0:T(8,128)(2,1)}, bf16[512,256]{1,0:T(8,128)(2,1)S(1)}, u32[]{:S(2)}, u32[]{:S(2)}) collective-permute-start(bf16[512,256]{1,0:T(8,128)(2,1)} %constant_dynamic-update-slice_fusion), channel_id=1, source_target_pairs={{0,3},{4,7},{8,11},{12,15},{16,19},{20,23},{24,27},{28,31},{32,35}... | collective-permute-start | bytes 786440 | tf_op jit(solution)/shard_map/ppermute | solution.py:24
  33.6 13.4 %collective-permute-start.1 = (bf16[512,256]{1,0:T(8,128)(2,1)}, bf16[512,256]{1,0:T(8,128)(2,1)S(1)}, u32[]{:S(2)}, u32[]{:S(2)}) collective-permute-start(bf16[512,256]{1,0:T(8,128)(2,1)} %constant_dynamic-update-slice_fusion), channel_id=1, source_target_pairs={{0,2},{1,3},{4,6},{5,7},{8,10},{9,11},{12,14},{13,15},{16,18},{17,... | collective-permute-start | bytes 786440 | tf_op jit(solution)/shard_map/ppermute | solution.py:24
  37.4 12.1 %collective-permute-start = (bf16[512,256]{1,0:T(8,128)(2,1)}, bf16[512,256]{1,0:T(8,128)(2,1)S(1)}, u32[]{:S(2)}, u32[]{:S(2)}) collective-permute-start(bf16[512,256]{1,0:T(8,128)(2,1)} %constant_dynamic-update-slice_fusion), channel_id=1, source_target_pairs={{0,1},{1,2},{2,3},{4,5},{5,6},{6,7},{8,9},{9,10},{10,11},{12,13},{... | collective-permute-start | bytes 786440 | tf_op jit(solution)/shard_map/ppermute | solution.py:24
  42.7 6.9 %copy-start.3 = (bf16[512,2048]{1,0:T(8,128)(2,1)}, bf16[512,2048]{1,0:T(8,128)(2,1)S(1)}, u32[]{:S(2)}) copy-start(bf16[512,2048]{1,0:T(8,128)(2,1)S(1)} %convolution_convert_fusion) | copy-start | bytes 6291460
  42.7 6.8 %copy-start.6 = (bf16[512,256]{1,0:T(8,128)(2,1)S(1)}, bf16[512,256]{1,0:T(8,128)(2,1)}, u32[]{:S(2)}) copy-start(bf16[512,256]{1,0:T(8,128)(2,1)} %constant_dynamic-update-slice_fusion) | copy-start | bytes 786436
  42.7 6.9 %copy-start.7 = (bf16[512,128]{1,0:T(8,128)(2,1)S(1)}, bf16[512,128]{1,0:T(8,128)(2,1)}, u32[]{:S(2)}) copy-start(bf16[512,128]{1,0:T(8,128)(2,1)} %param.8) | copy-start | bytes 393220
  42.8 13.5 %collective-permute-start.6 = (bf16[512,1024]{1,0:T(8,128)(2,1)S(1)}, bf16[512,1024]{1,0:T(8,128)(2,1)S(1)}, u32[]{:S(2)}, u32[]{:S(2)}) collective-permute-start(bf16[512,1024]{1,0:T(8,128)(2,1)S(1)} %constant_dynamic-slice_fusion.5), channel_id=1, source_target_pairs={{0,4},{4,0},{1,5},{5,1},{2,6},{6,2},{3,7},{7,3},{8,12},{12,8},{9,1... | collective-permute-start | bytes 3145736 | tf_op jit(solution)/shard_map/ppermute | solution.py:20
  45.9 5.3 %copy-start.4 = (bf16[8,128,768]{2,1,0:T(8,128)(2,1)}, bf16[8,128,768]{2,1,0:T(8,128)(2,1)S(1)}, u32[]{:S(2)}) copy-start(bf16[8,128,768]{2,1,0:T(8,128)(2,1)S(1)} %bitcast_dynamic-update-slice_fusion.1) | copy-start | bytes 4718596
  53.0 2.0 %copy-start = (f32[512,2048]{1,0:T(8,128)}, f32[512,2048]{1,0:T(8,128)S(1)}, u32[]{:S(2)}) copy-start(f32[512,2048]{1,0:T(8,128)S(1)} %get-tuple-element.25) | copy-start | bytes 12582916
  58.0 19.6 %collective-permute-start.11 = (bf16[4,128,768]{2,1,0:T(8,128)(2,1)}, bf16[4,128,768]{2,1,0:T(8,128)(2,1)S(1)}, u32[]{:S(2)}, u32[]{:S(2)}) collective-permute-start(bf16[4,128,768]{2,1,0:T(8,128)(2,1)} %constant_dynamic-slice_fusion.4), channel_id=1, source_target_pairs={{0,128},{64,192},{128,0},{192,64},{1,129},{65,193},{129,1},{193,65... | collective-permute-start | bytes 2359304 | tf_op jit(solution)/shard_map/ppermute | solution.py:20
  59.9 34.5 %collective-permute-start.10 = (bf16[4,128,768]{2,1,0:T(8,128)(2,1)}, bf16[4,128,768]{2,1,0:T(8,128)(2,1)}, u32[]{:S(2)}, u32[]{:S(2)}) collective-permute-start(bf16[4,128,768]{2,1,0:T(8,128)(2,1)} %constant_dynamic-slice_fusion.4), channel_id=1, source_target_pairs={{0,192},{64,0},{128,64},{192,128},{1,193},{65,1},{129,65},{193,129... | collective-permute-start | bytes 2359304 | tf_op jit(solution)/shard_map/ppermute | solution.py:20
  60.7 35.6 %collective-permute-start.12 = (bf16[4,128,768]{2,1,0:T(8,128)(2,1)}, bf16[4,128,768]{2,1,0:T(8,128)(2,1)}, u32[]{:S(2)}, u32[]{:S(2)}) collective-permute-start(bf16[4,128,768]{2,1,0:T(8,128)(2,1)} %constant_dynamic-slice_fusion.4), channel_id=1, source_target_pairs={{0,64},{64,128},{128,192},{192,0},{1,65},{65,129},{129,193},{193,1... | collective-permute-start | bytes 2359304 | tf_op jit(solution)/shard_map/ppermute | solution.py:20
  62.7 35.2 %collective-permute-start.13 = (bf16[512,256]{1,0:T(8,128)(2,1)S(1)}, bf16[512,256]{1,0:T(8,128)(2,1)S(1)}, u32[]{:S(2)}, u32[]{:S(2)}) collective-permute-start(bf16[512,256]{1,0:T(8,128)(2,1)S(1)} %get-tuple-element.33), channel_id=1, source_target_pairs={{0,8},{8,16},{16,24},{24,0},{1,9},{9,17},{17,25},{25,1},{2,10},{10... | collective-permute-start | bytes 786440 | tf_op jit(solution)/shard_map/ppermute | solution.py:20
  63.9 33.9 %collective-permute-start.15 = (bf16[512,256]{1,0:T(8,128)(2,1)S(1)}, bf16[512,256]{1,0:T(8,128)(2,1)S(1)}, u32[]{:S(2)}, u32[]{:S(2)}) collective-permute-start(bf16[512,256]{1,0:T(8,128)(2,1)S(1)} %get-tuple-element.34), channel_id=1, source_target_pairs={{0,24},{8,0},{16,8},{24,16},{1,25},{9,1},{17,9},{25,17},{2,26},{10... | collective-permute-start | bytes 786440 | tf_op jit(solution)/shard_map/ppermute | solution.py:20
  77.6 20.2 %collective-permute-start.14 = (bf16[512,256]{1,0:T(8,128)(2,1)S(1)}, bf16[512,256]{1,0:T(8,128)(2,1)S(1)}, u32[]{:S(2)}, u32[]{:S(2)}) collective-permute-start(bf16[512,256]{1,0:T(8,128)(2,1)S(1)} %get-tuple-element.35), channel_id=1, source_target_pairs={{0,16},{8,24},{16,0},{24,8},{1,17},{9,25},{17,1},{25,9},{2,18},{10... | collective-permute-start | bytes 786440 | tf_op jit(solution)/shard_map/ppermute | solution.py:20
  97.8 9.0 %copy-start.1 = (f32[512,2048]{1,0:T(8,128)S(1)}, f32[512,2048]{1,0:T(8,128)}, u32[]{:S(2)}) copy-start(f32[512,2048]{1,0:T(8,128)} %copy-done) | copy-start | bytes 12582916
  98.0 8.8 %collective-permute-start.16 = (bf16[512,128]{1,0:T(8,128)(2,1)S(1)}, bf16[512,128]{1,0:T(8,128)(2,1)S(1)}, u32[]{:S(2)}, u32[]{:S(2)}) collective-permute-start(bf16[512,128]{1,0:T(8,128)(2,1)S(1)} %constant_dynamic-slice_fusion), channel_id=1, source_target_pairs={{0,32},{32,0},{1,33},{33,1},{2,34},{34,2},{3,35},{35,3},{4,36},{36... | collective-permute-start | bytes 393224 | tf_op jit(solution)/shard_map/ppermute | solution.py:20
  107.7 0.9 copy-start.8
  110.2 20.3 %collective-permute-start.17 = (bf16[512,256]{0,1:T(8,128)(2,1)S(1)}, bf16[512,256]{0,1:T(8,128)(2,1)S(1)}, u32[]{:S(2)}, u32[]{:S(2)}) collective-permute-start(bf16[512,256]{0,1:T(8,128)(2,1)S(1)} %get-tuple-element.30), channel_id=1, source_target_pairs={{1,0},{2,1},{3,2},{5,4},{6,5},{7,6},{9,8},{10,9},{11,10},{13,12},{... | collective-permute-start | bytes 786440 | tf_op jit(solution)/shard_map/ppermute | solution.py:24
  111.5 29.7 %collective-permute-start.19 = (bf16[512,256]{0,1:T(8,128)(2,1)S(1)}, bf16[512,256]{0,1:T(8,128)(2,1)S(1)}, u32[]{:S(2)}, u32[]{:S(2)}) collective-permute-start(bf16[512,256]{0,1:T(8,128)(2,1)S(1)} %get-tuple-element.31), channel_id=1, source_target_pairs={{3,0},{7,4},{11,8},{15,12},{19,16},{23,20},{27,24},{31,28},{35,32}... | collective-permute-start | bytes 786440 | tf_op jit(solution)/shard_map/ppermute | solution.py:24
  112.8 36.4 %collective-permute-start.18 = (bf16[512,256]{0,1:T(8,128)(2,1)S(1)}, bf16[512,256]{0,1:T(8,128)(2,1)S(1)}, u32[]{:S(2)}, u32[]{:S(2)}) collective-permute-start(bf16[512,256]{0,1:T(8,128)(2,1)S(1)} %get-tuple-element.32), channel_id=1, source_target_pairs={{2,0},{3,1},{6,4},{7,5},{10,8},{11,9},{14,12},{15,13},{18,16},{19,... | collective-permute-start | bytes 786440 | tf_op jit(solution)/shard_map/ppermute | solution.py:24
  164.0 4.2 %copy-start.2 = (bf16[32768,128]{1,0:T(8,128)(2,1)S(1)}, bf16[32768,128]{1,0:T(8,128)(2,1)}, u32[]{:S(2)}) copy-start(bf16[32768,128]{1,0:T(8,128)(2,1)} %all-gather.3.cloned.1.call-done) | copy-start | bytes 25165828
Sparse Core Ops, SparseCore 0:
  58.1 105.8 all-gather.2

commit v5 on v4

--- a/solution.py
+++ b/solution.py
@@ -70,7 +70,7 @@
             [kv] + [shift_open(kv, DEP, n_dep, t) for t in range(1, n_dep)], axis=0
         ).reshape(n_dep * tok_depth, 2 * head_dim)
         keys_all, values_all = kv_all[:, :head_dim], kv_all[:, head_dim:]
-        by_depth = roll_rows(rolled_gather(local, DEP, n_dep), me_d, 0)
+        by_depth = rolled_gather(local, DEP, n_dep)
 
         src_depth = me_d - jnp.arange(n_dep, dtype=jnp.int32)
         key_pos = (
@@ -101,7 +101,6 @@
             jnp.bfloat16
         )
 
-        rows_all = rolled_gather(by_depth, "row", n_row, stack_axis=1)
 
         weight_perm = jnp.transpose(
             out_weight.reshape(n_zh, n_x, n_core, head_dim, feat), (2, 1, 0, 3, 4)
@@ -111,6 +110,8 @@
         ).astype(jnp.bfloat16)
         partial = pp_reduce_scatter_cols(partial, "core", n_core).astype(jnp.bfloat16)
         context, partial, by_depth = lax.optimization_barrier((context, partial, by_depth))
+        by_depth = roll_rows(by_depth, me_d, 0)
+        rows_all = rolled_gather(by_depth, "row", n_row, stack_axis=1)
         ctx_all = lax.all_gather(context[None], ("zh", DEP, "x", "core"), axis=0, tiled=True)
         ctx_all = ctx_all.reshape(n_zh, n_dep, n_x, n_core, tok_depth, head_dim)
         partial = pp_reduce_scatter_cols(partial, "x", n_x).astype(jnp.bfloat16)

time: 184 us -> 174 us (0.946)
  local copies, waits for them, and re-layouts: 17.1 us -> 9.22 us
  waiting for transfers between devices: 79.2 us -> 74.1 us
  matrix products: 19.8 us -> 23.8 us
  starting transfers between devices: 43.4 us -> 40.4 us
  other arithmetic: 9.34 us -> 11.2 us
    ppermute x14, waiting for transfers between devices: 30.5 us -> 14.5 us  [shift(): return lax.ppermute(x, axis, [(i, (i + s) % n) for i in range(n)])]
    ppermute x6, waiting for transfers between devices: 35.5 us -> 41.5 us  [shift_open(): lax.ppermute(x, axis, [(i, i + s) for i in range(n) if 0 <= i + s < n])]
    unnamed x29 -> x20, local copies, waits for them, and re-layouts: 9.75 us -> 4.01 us
    all_gather x1, waiting for transfers between devices: 13.1 us -> 18.1 us  [shards(): lax.all_gather(context[None], ('zh', DEP, 'x', 'core'), axis=0, tiled=True)]
    ppermute x6, starting transfers between devices: 16 us -> 13.7 us  [shift_open(): lax.ppermute(x, axis, [(i, i + s) for i in range(n) if 0 <= i + s < n])]
    dot_general x1, matrix products: 0.83 us -> 2.99 us  [shards(): jnp.dot(context_grad, values_all.T, preferred_element_type=jnp.float32)]
    dot_general x1, matrix products: 1.83 us -> 3.72 us  [shards(): jnp.einsum('tf,hf->th', grad_rows, weight_perm, preferred_element_type=jn...]
  transfers between devices with their start and end apart: 21 -> 21, of which waited for: 9 -> 10; matrix products, arithmetic and copies ran while one was open for 16% -> 16% of each run, Pallas kernels for 0% -> 0%
where the time goes in v5:
time: 174 us; the launch traced here: 173 us
  waiting for transfers between devices  74.1 us (43%)
  starting transfers between devices  40.4 us (23%)
  matrix products  23.8 us (14%)
  between operations  14.4 us (8%)
  other arithmetic  11.2 us (6%)
  local copies, waits for them, and re-layouts  9.22 us (5%)
    ppermute x6, waiting for transfers between devices, shift_open(): lax.ppermute(x, axis, [(i, i + s) for i in range(n) if 0 <= i + s < n])  41.5 us
    ppermute x14, starting transfers between devices, shift(): return lax.ppermute(x, axis, [(i, (i + s) % n) for i in range(n)])  26.7 us
    all_gather x1, waiting for transfers between devices, shards(): lax.all_gather(context[None], ('zh', DEP, 'x', 'core'), axis=0, tiled=True)  18.1 us
    ppermute x14, waiting for transfers between devices, shift(): return lax.ppermute(x, axis, [(i, (i + s) % n) for i in range(n)])  14.5 us
    ppermute x6, starting transfers between devices, shift_open(): lax.ppermute(x, axis, [(i, i + s) for i in range(n) if 0 <= i + s < n])  13.7 us
    dot_general x4, matrix products, shards(): jnp.einsum('zxcth,tf->zxchf', ctx_all[:, depth], rows_all[depth].reshape(...  11.8 us
    unnamed x20, local copies, waits for them, and re-layouts  4.01 us
    transpose x1, local copies, waits for them, and re-layouts, shards(): jnp.transpose(out_weight.reshape(n_zh, n_x, n_core, head_dim, feat), (2,...  3.83 us
  transfers between devices with their start and end apart: 21, of which 10 were waited for; matrix products, arithmetic and copies ran while one was open for 16% of the time, Pallas kernels for 0%

profile of v5, /device:TPU:1, one launch (start us, length us, event | category | flops | bytes accessed | tf_op | source)
XLA Modules:
  0.0 173.1 jit_solution(16478914064638914497)
XLA Ops:
  7.2 2.5 %collective-permute-start.9 = (bf16[128,768]{1,0:T(8,128)(2,1)}, bf16[128,768]{1,0:T(8,128)(2,1)S(1)}, u32[]{:S(2)}, u32[]{:S(2)}) collective-permute-start(bf16[128,768]{1,0:T(8,128)(2,1)} %bitcast.94), channel_id=1, source_target_pairs={{0,1},{1,2},{2,3},{3,0},{4,5},{5,6},{6,7},{7,4},{8,9},{9,10},{10,1... | collective-permute-start | bytes 589832 | tf_op jit(solution)/shard_map/ppermute | solution.py:20
  9.8 3.0 %collective-permute-start.8 = (bf16[128,768]{1,0:T(8,128)(2,1)}, bf16[128,768]{1,0:T(8,128)(2,1)S(1)}, u32[]{:S(2)}, u32[]{:S(2)}) collective-permute-start(bf16[128,768]{1,0:T(8,128)(2,1)} %bitcast.95), channel_id=1, source_target_pairs={{0,2},{1,3},{2,0},{3,1},{4,6},{5,7},{6,4},{7,5},{8,10},{9,11},{10,... | collective-permute-start | bytes 589832 | tf_op jit(solution)/shard_map/ppermute | solution.py:20
  14.8 2.6 %collective-permute-start.4 = (bf16[128,768]{1,0:T(8,128)(2,1)}, bf16[128,768]{1,0:T(8,128)(2,1)S(1)}, u32[]{:S(2)}, u32[]{:S(2)}) collective-permute-start(bf16[128,768]{1,0:T(8,128)(2,1)} %bitcast.98), channel_id=1, source_target_pairs={{0,128},{64,192},{128,0},{192,64},{1,129},{65,193},{129,1},{193,65... | collective-permute-start | bytes 589832 | tf_op jit(solution)/shard_map/ppermute | solution.py:20
  18.3 3.8 %copy.29 = bf16[2,4,2,128,768]{4,3,2,1,0:T(8,128)(2,1)} copy(bf16[2,4,2,128,768]{4,3,0,1,2:T(8,128)(2,1)} %bitcast.86) | data formatting | bytes 6291456 | tf_op jit(solution)/shard_map/transpose | solution.py:105
  23.6 2.9 %collective-permute-done.8 = bf16[128,768]{1,0:T(8,128)(2,1)S(1)} collective-permute-done((bf16[128,768]{1,0:T(8,128)(2,1)}, bf16[128,768]{1,0:T(8,128)(2,1)S(1)}, u32[]{:S(2)}, u32[]{:S(2)}) %collective-permute-start.8) | collective-permute-done | bytes 196640 | tf_op jit(solution)/shard_map/ppermute | solution.py:20
  26.5 6.1 %collective-permute-start.2 = (bf16[512,256]{1,0:T(8,128)(2,1)S(1)}, bf16[512,256]{1,0:T(8,128)(2,1)S(1)}, u32[]{:S(2)}, u32[]{:S(2)}) collective-permute-start(bf16[512,256]{1,0:T(8,128)(2,1)S(1)} %constant_dynamic-update-slice_fusion), channel_id=1, source_target_pairs={{0,3},{4,7},{8,11},{12,15},{16,19},{20,23},{24,27},{28,31},{32,35}... | collective-permute-start | bytes 786440 | tf_op jit(solution)/shard_map/ppermute | solution.py:24
  33.9 2.2 %collective-permute-start = (bf16[512,256]{1,0:T(8,128)(2,1)S(1)}, bf16[512,256]{1,0:T(8,128)(2,1)S(1)}, u32[]{:S(2)}, u32[]{:S(2)}) collective-permute-start(bf16[512,256]{1,0:T(8,128)(2,1)S(1)} %constant_dynamic-update-slice_fusion), channel_id=1, source_target_pairs={{0,1},{1,2},{2,3},{4,5},{5,6},{6,7},{8,9},{9,10},{10,11},{12,13},{... | collective-permute-start | bytes 786440 | tf_op jit(solution)/shard_map/ppermute | solution.py:24
  36.3 3.7 %convolution_convert_fusion = bf16[512,2048]{1,0:T(8,128)(2,1)S(1)} fusion(bf16[512,768]{1,0:T(8,128)(2,1)S(1)} %bitcast.89, bf16[2048,768]{1,0:T(8,128)(2,1)} %bitcast.87), kind=kOutput, calls=%fused_computation.8 | convolution fusion | flops 1611661312 | bytes 6029312 | tf_op jit(solution)/shard_map/tf,hf->th/dot_general | solution.py:108
  40.2 2.2 %collective-permute-start.6 = (bf16[512,1024]{1,0:T(8,128)(2,1)S(1)}, bf16[512,1024]{1,0:T(8,128)(2,1)}, u32[]{:S(2)}, u32[]{:S(2)}) collective-permute-start(bf16[512,1024]{1,0:T(8,128)(2,1)S(1)} %constant_dynamic-slice_fusion.4), channel_id=1, source_target_pairs={{0,4},{4,0},{1,5},{5,1},{2,6},{6,2},{3,7},{7,3},{8,12},{12,8},{9,1... | collective-permute-start | bytes 3145736 | tf_op jit(solution)/shard_map/ppermute | solution.py:20
  42.4 5.6 %collective-permute-done = bf16[512,256]{1,0:T(8,128)(2,1)S(1)} collective-permute-done((bf16[512,256]{1,0:T(8,128)(2,1)S(1)}, bf16[512,256]{1,0:T(8,128)(2,1)S(1)}, u32[]{:S(2)}, u32[]{:S(2)}) %collective-permute-start) | collective-permute-done | bytes 262176 | tf_op jit(solution)/shard_map/ppermute | solution.py:24
  48.1 1.6 fusion
  49.7 1.7 fusion.26
  51.4 2.0 %copy-done = f32[512,2048]{1,0:T(8,128)} copy-done((f32[512,2048]{1,0:T(8,128)}, f32[512,2048]{1,0:T(8,128)S(1)}, u32[]{:S(2)}) %copy-start) | copy-done | bytes 4194328
  54.8 1.9 %add_convert_fusion = bf16[512,1024]{1,0:T(8,128)(2,1)S(1)} fusion(bf16[512,1024]{1,0:T(8,128)(2,1)} %collective-permute-done.6, bf16[512,2048]{1,0:T(8,128)(2,1)} %copy-done.3, s32[]{:T(128)S(6)} %select_n.99), kind=kLoop, calls=%fused_computation.20 | loop fusion | flops 2097152 | bytes 3145732 | tf_op jit(solution)/shard_map/convert_element_type | solution.py:111
  59.0 1.5 collective-permute-start.15
  60.5 1.5 collective-permute-start.14
  62.0 2.4 %collective-permute-done.13 = bf16[512,256]{1,0:T(8,128)(2,1)S(1)} collective-permute-done((bf16[512,256]{1,0:T(8,128)(2,1)}, bf16[512,256]{1,0:T(8,128)(2,1)S(1)}, u32[]{:S(2)}, u32[]{:S(2)}) %collective-permute-start.13) | collective-permute-done | bytes 262176 | tf_op jit(solution)/shard_map/ppermute | solution.py:20
  64.7 6.3 %collective-permute-done.14 = bf16[512,256]{1,0:T(8,128)(2,1)} collective-permute-done((bf16[512,256]{1,0:T(8,128)(2,1)S(1)}, bf16[512,256]{1,0:T(8,128)(2,1)}, u32[]{:S(2)}, u32[]{:S(2)}) %collective-permute-start.14) | collective-permute-done | bytes 262176 | tf_op jit(solution)/shard_map/ppermute | solution.py:20
  72.2 5.2 %collective-permute-start.16 = (bf16[512,128]{1,0:T(8,128)(2,1)S(1)}, bf16[512,128]{1,0:T(8,128)(2,1)S(1)}, u32[]{:S(2)}, u32[]{:S(2)}) collective-permute-start(bf16[512,128]{1,0:T(8,128)(2,1)S(1)} %constant_dynamic-slice_fusion), channel_id=1, source_target_pairs={{0,32},{32,0},{1,33},{33,1},{2,34},{34,2},{3,35},{35,3},{4,36},{36... | collective-permute-start | bytes 393224 | tf_op jit(solution)/shard_map/ppermute | solution.py:20
  77.4 2.6 %collective-permute-done.16 = bf16[512,128]{1,0:T(8,128)(2,1)S(1)} collective-permute-done((bf16[512,128]{1,0:T(8,128)(2,1)S(1)}, bf16[512,128]{1,0:T(8,128)(2,1)S(1)}, u32[]{:S(2)}, u32[]{:S(2)}) %collective-permute-start.16) | collective-permute-done | bytes 131104 | tf_op jit(solution)/shard_map/ppermute | solution.py:20
  80.0 3.0 %multiply_reduce_fusion = (f32[512]{0:T(512)S(1)}, f32[512,2048]{1,0:T(8,128)S(1)}) fusion(f32[512,2048]{1,0:T(8,128)} %copy-done, f32[512]{0:T(512)S(1)} %broadcast_divide_fusion, bf16[2048,256]{1,0:T(8,128)(2,1)S(1)} %bitcast.80, bf16[512,128]{1,0:T(8,128)(2,1)S(1)} %collective-permute-done.16, bf16[512,256]{1,0:T(8,128)(2,1)S(1)} %add_convert_fusion.2, ...), kind=kOutput, calls=%fused_computation.1 | convolution fusion | flops 271842816 | bytes 9179140 | tf_op jit(solution)/shard_map/dot_general | solution.py:121
  87.7 2.7 %collective-permute-start.10 = (bf16[4,128,768]{2,1,0:T(8,128)(2,1)}, bf16[4,128,768]{2,1,0:T(8,128)(2,1)S(1)}, u32[]{:S(2)}, u32[]{:S(2)}) collective-permute-start(bf16[4,128,768]{2,1,0:T(8,128)(2,1)} %fusion.8), channel_id=1, source_target_pairs={{0,192},{64,0},{128,64},{192,128},{1,193},{65,1},{129,65},{193,129... | collective-permute-start | bytes 2359304 | tf_op jit(solution)/shard_map/ppermute | solution.py:20
  93.0 13.5 %collective-permute-done.17 = bf16[512,256]{0,1:T(8,128)(2,1)S(1)} collective-permute-done((bf16[512,256]{0,1:T(8,128)(2,1)S(1)}, bf16[512,256]{0,1:T(8,128)(2,1)S(1)}, u32[]{:S(2)}, u32[]{:S(2)}) %collective-permute-start.17) | collective-permute-done | bytes 262176 | tf_op jit(solution)/shard_map/ppermute | solution.py:24
  106.5 1.5 collective-permute-start.18
  109.9 3.1 %collective-permute-done.19 = bf16[512,256]{0,1:T(8,128)(2,1)S(1)} collective-permute-done((bf16[512,256]{0,1:T(8,128)(2,1)S(1)}, bf16[512,256]{0,1:T(8,128)(2,1)S(1)}, u32[]{:S(2)}, u32[]{:S(2)}) %collective-permute-start.19) | collective-permute-done | bytes 262176 | tf_op jit(solution)/shard_map/ppermute | solution.py:24
  113.0 19.4 %collective-permute-done.18 = bf16[512,256]{0,1:T(8,128)(2,1)S(1)} collective-permute-done((bf16[512,256]{0,1:T(8,128)(2,1)S(1)}, bf16[512,256]{0,1:T(8,128)(2,1)S(1)}, u32[]{:S(2)}, u32[]{:S(2)}) %collective-permute-start.18) | collective-permute-done | bytes 262176 | tf_op jit(solution)/shard_map/ppermute | solution.py:24
  134.1 1.6 pad_maximum_fusion
  136.0 18.1 %all-gather.3.cloned.1.call-done = bf16[32768,128]{1,0:T(8,128)(2,1)} async-done(((bf16[512,128]{1,0:T(8,128)(2,1)}), bf16[32768,128]{1,0:T(8,128)(2,1)}) %all-gather.3.cloned.1.call-update) | async-done | bytes 8388624 | tf_op jit(solution)/shard_map/all_gather | solution.py:115
  154.1 3.6 %fusion.2 = f32[2,4,2,128,768]{4,3,2,1,0:T(8,128)S(1)} fusion(bf16[512,768,1,1,1]{1,0,4,3,2:T(8,128)(2,1)S(1)} %bitcast.85, bf16[2,4,4,2,512,128]{5,4,3,2,1,0:T(8,128)(2,1)} %bitcast.73), kind=kOutput, calls=%fused_computation.19 | convolution fusion | flops 1610612736 | bytes 9175040 | tf_op jit(solution)/shard_map/zxcth,tf->zxchf/dot_general | solution.py:145
  158.1 1.8 %convolution_add_fusion.2 = f32[2,4,2,128,768]{4,3,2,1,0:T(8,128)S(1)} fusion(f32[2,4,2,128,768]{4,3,2,1,0:T(8,128)S(1)} %fusion.2, bf16[512,768,1,1,1]{1,0,4,3,2:T(8,128)(2,1)S(1)} %bitcast.84, bf16[2,4,4,2,512,128]{5,4,3,2,1,0:T(8,128)(2,1)S(1)} %bitcast.74), kind=kOutput, calls=%fused_computation.11 | convolution fusion | flops 1612185600 | bytes 15466496 | tf_op jit(solution)/shard_map/zxcth,tf->zxchf/dot_general | solution.py:145
  159.9 1.8 %convolution_add_fusion.1 = f32[2,4,2,128,768]{4,3,2,1,0:T(8,128)S(1)} fusion(f32[2,4,2,128,768]{4,3,2,1,0:T(8,128)S(1)} %convolution_add_fusion.2, bf16[512,768,1,1,1]{1,0,4,3,2:T(8,128)(2,1)S(1)} %bitcast.83, bf16[2,4,4,2,512,128]{5,4,3,2,1,0:T(8,128)(2,1)S(1)} %bitcast.75), kind=kOutput, calls=%fused_computation.10 | convolution fusion | flops 1612185600 | bytes 15466496 | tf_op jit(solution)/shard_map/zxcth,tf->zxchf/dot_general | solution.py:145
  161.7 4.5 %convolution_add_fusion = f32[2,4,2,128,768]{4,3,2,1,0:T(8,128)} fusion(f32[2,4,2,128,768]{4,3,2,1,0:T(8,128)S(1)} %convolution_add_fusion.1, bf16[512,768,1,1,1]{1,0,4,3,2:T(8,128)(2,1)S(1)} %bitcast.82, bf16[2,4,4,2,512,128]{5,4,3,2,1,0:T(8,128)(2,1)S(1)} %bitcast.76), kind=kOutput, calls=%fused_computation.9 | convolution fusion | flops 1612185600 | bytes 15466496 | tf_op jit(solution)/shard_map/zxcth,tf->zxchf/dot_general | solution.py:145
  (68 shorter events, 22.7 us)
Async XLA Ops:
  7.2 15.2 %copy-start.4 = (bf16[1,128,768]{2,1,0:T(8,128)(2,1)S(1)}, bf16[1,128,768]{2,1,0:T(8,128)(2,1)}, u32[]{:S(2)}) copy-start(bf16[1,128,768]{2,1,0:T(8,128)(2,1)} %param.6) | copy-start | bytes 589828
  7.2 15.1 %copy-start.5 = (bf16[512,128]{1,0:T(8,128)(2,1)S(1)}, bf16[512,128]{1,0:T(8,128)(2,1)}, u32[]{:S(2)}) copy-start(bf16[512,128]{1,0:T(8,128)(2,1)} %param.9) | copy-start | bytes 393220
  7.2 16.4 %copy-start.6 = (bf16[512,128]{1,0:T(8,128)(2,1)S(1)}, bf16[512,128]{1,0:T(8,128)(2,1)}, u32[]{:S(2)}) copy-start(bf16[512,128]{1,0:T(8,128)(2,1)} %param.10) | copy-start | bytes 393220
  7.2 146.9 %all-gather.3.cloned.1.call-start = ((), (), s32[]{:S(2)}) async-start(), calls=%async_computation | async-start | bytes 8519680 | tf_op jit(solution)/shard_map/all_gather | solution.py:115
  7.2 15.1 %collective-permute-start.9 = (bf16[128,768]{1,0:T(8,128)(2,1)}, bf16[128,768]{1,0:T(8,128)(2,1)S(1)}, u32[]{:S(2)}, u32[]{:S(2)}) collective-permute-start(bf16[128,768]{1,0:T(8,128)(2,1)} %bitcast.94), channel_id=1, source_target_pairs={{0,1},{1,2},{2,3},{3,0},{4,5},{5,6},{6,7},{7,4},{8,9},{9,10},{10,1... | collective-permute-start | bytes 589832 | tf_op jit(solution)/shard_map/ppermute | solution.py:20
  9.8 16.7 %collective-permute-start.8 = (bf16[128,768]{1,0:T(8,128)(2,1)}, bf16[128,768]{1,0:T(8,128)(2,1)S(1)}, u32[]{:S(2)}, u32[]{:S(2)}) collective-permute-start(bf16[128,768]{1,0:T(8,128)(2,1)} %bitcast.95), channel_id=1, source_target_pairs={{0,2},{1,3},{2,0},{3,1},{4,6},{5,7},{6,4},{7,5},{8,10},{9,11},{10,... | collective-permute-start | bytes 589832 | tf_op jit(solution)/shard_map/ppermute | solution.py:20
  12.8 19.8 %collective-permute-start.7 = (bf16[128,768]{1,0:T(8,128)(2,1)}, bf16[128,768]{1,0:T(8,128)(2,1)S(1)}, u32[]{:S(2)}, u32[]{:S(2)}) collective-permute-start(bf16[128,768]{1,0:T(8,128)(2,1)} %bitcast.96), channel_id=1, source_target_pairs={{0,3},{1,0},{2,1},{3,2},{4,7},{5,4},{6,5},{7,6},{8,11},{9,8},{10,9... | collective-permute-start | bytes 589832 | tf_op jit(solution)/shard_map/ppermute | solution.py:20
  13.5 20.4 %collective-permute-start.5 = (bf16[128,768]{1,0:T(8,128)(2,1)}, bf16[128,768]{1,0:T(8,128)(2,1)S(1)}, u32[]{:S(2)}, u32[]{:S(2)}) collective-permute-start(bf16[128,768]{1,0:T(8,128)(2,1)} %bitcast.97), channel_id=1, source_target_pairs={{0,64},{64,128},{128,192},{192,0},{1,65},{65,129},{129,193},{193,1... | collective-permute-start | bytes 589832 | tf_op jit(solution)/shard_map/ppermute | solution.py:20
  14.8 21.3 %collective-permute-start.4 = (bf16[128,768]{1,0:T(8,128)(2,1)}, bf16[128,768]{1,0:T(8,128)(2,1)S(1)}, u32[]{:S(2)}, u32[]{:S(2)}) collective-permute-start(bf16[128,768]{1,0:T(8,128)(2,1)} %bitcast.98), channel_id=1, source_target_pairs={{0,128},{64,192},{128,0},{192,64},{1,129},{65,193},{129,1},{193,65... | collective-permute-start | bytes 589832 | tf_op jit(solution)/shard_map/ppermute | solution.py:20
  22.3 13.8 %collective-permute-start.3 = (bf16[128,768]{1,0:T(8,128)(2,1)S(1)}, bf16[128,768]{1,0:T(8,128)(2,1)S(1)}, u32[]{:S(2)}, u32[]{:S(2)}) collective-permute-start(bf16[128,768]{1,0:T(8,128)(2,1)S(1)} %bitcast.99), channel_id=1, source_target_pairs={{0,192},{64,0},{128,64},{192,128},{1,193},{65,1},{129,65},{193,129... | collective-permute-start | bytes 589832 | tf_op jit(solution)/shard_map/ppermute | solution.py:20
  26.5 15.9 %collective-permute-start.2 = (bf16[512,256]{1,0:T(8,128)(2,1)S(1)}, bf16[512,256]{1,0:T(8,128)(2,1)S(1)}, u32[]{:S(2)}, u32[]{:S(2)}) collective-permute-start(bf16[512,256]{1,0:T(8,128)(2,1)S(1)} %constant_dynamic-update-slice_fusion), channel_id=1, source_target_pairs={{0,3},{4,7},{8,11},{12,15},{16,19},{20,23},{24,27},{28,31},{32,35}... | collective-permute-start | bytes 786440 | tf_op jit(solution)/shard_map/ppermute | solution.py:24
  32.6 9.8 %collective-permute-start.1 = (bf16[512,256]{1,0:T(8,128)(2,1)S(1)}, bf16[512,256]{1,0:T(8,128)(2,1)S(1)}, u32[]{:S(2)}, u32[]{:S(2)}) collective-permute-start(bf16[512,256]{1,0:T(8,128)(2,1)S(1)} %constant_dynamic-update-slice_fusion), channel_id=1, source_target_pairs={{0,2},{1,3},{4,6},{5,7},{8,10},{9,11},{12,14},{13,15},{16,18},{17,... | collective-permute-start | bytes 786440 | tf_op jit(solution)/shard_map/ppermute | solution.py:24
  33.9 14.0 %collective-permute-start = (bf16[512,256]{1,0:T(8,128)(2,1)S(1)}, bf16[512,256]{1,0:T(8,128)(2,1)S(1)}, u32[]{:S(2)}, u32[]{:S(2)}) collective-permute-start(bf16[512,256]{1,0:T(8,128)(2,1)S(1)} %constant_dynamic-update-slice_fusion), channel_id=1, source_target_pairs={{0,1},{1,2},{2,3},{4,5},{5,6},{6,7},{8,9},{9,10},{10,11},{12,13},{... | collective-permute-start | bytes 786440 | tf_op jit(solution)/shard_map/ppermute | solution.py:24
  40.0 8.0 %copy-start.3 = (bf16[512,2048]{1,0:T(8,128)(2,1)}, bf16[512,2048]{1,0:T(8,128)(2,1)S(1)}, u32[]{:S(2)}) copy-start(bf16[512,2048]{1,0:T(8,128)(2,1)S(1)} %convolution_convert_fusion) | copy-start | bytes 6291460
  40.0 8.0 %copy-start.7 = (bf16[512,128]{1,0:T(8,128)(2,1)S(1)}, bf16[512,128]{1,0:T(8,128)(2,1)}, u32[]{:S(2)}) copy-start(bf16[512,128]{1,0:T(8,128)(2,1)} %param.8) | copy-start | bytes 393220
  40.2 14.7 %collective-permute-start.6 = (bf16[512,1024]{1,0:T(8,128)(2,1)S(1)}, bf16[512,1024]{1,0:T(8,128)(2,1)}, u32[]{:S(2)}, u32[]{:S(2)}) collective-permute-start(bf16[512,1024]{1,0:T(8,128)(2,1)S(1)} %constant_dynamic-slice_fusion.4), channel_id=1, source_target_pairs={{0,4},{4,0},{1,5},{5,1},{2,6},{6,2},{3,7},{7,3},{8,12},{12,8},{9,1... | collective-permute-start | bytes 3145736 | tf_op jit(solution)/shard_map/ppermute | solution.py:20
  51.4 2.0 %copy-start = (f32[512,2048]{1,0:T(8,128)}, f32[512,2048]{1,0:T(8,128)S(1)}, u32[]{:S(2)}) copy-start(f32[512,2048]{1,0:T(8,128)S(1)} %get-tuple-element.27) | copy-start | bytes 12582916
  57.8 6.6 %collective-permute-start.13 = (bf16[512,256]{1,0:T(8,128)(2,1)}, bf16[512,256]{1,0:T(8,128)(2,1)S(1)}, u32[]{:S(2)}, u32[]{:S(2)}) collective-permute-start(bf16[512,256]{1,0:T(8,128)(2,1)} %get-tuple-element.35), channel_id=1, source_target_pairs={{0,8},{8,16},{16,24},{24,0},{1,9},{9,17},{17,25},{25,1},{2,10},{10... | collective-permute-start | bytes 786440 | tf_op jit(solution)/shard_map/ppermute | solution.py:20
  59.0 5.6 %collective-permute-start.15 = (bf16[512,256]{1,0:T(8,128)(2,1)}, bf16[512,256]{1,0:T(8,128)(2,1)}, u32[]{:S(2)}, u32[]{:S(2)}) collective-permute-start(bf16[512,256]{1,0:T(8,128)(2,1)} %get-tuple-element.36), channel_id=1, source_target_pairs={{0,24},{8,0},{16,8},{24,16},{1,25},{9,1},{17,9},{25,17},{2,26},{10... | collective-permute-start | bytes 786440 | tf_op jit(solution)/shard_map/ppermute | solution.py:20
  60.5 10.5 %collective-permute-start.14 = (bf16[512,256]{1,0:T(8,128)(2,1)S(1)}, bf16[512,256]{1,0:T(8,128)(2,1)}, u32[]{:S(2)}, u32[]{:S(2)}) collective-permute-start(bf16[512,256]{1,0:T(8,128)(2,1)S(1)} %get-tuple-element.37), channel_id=1, source_target_pairs={{0,16},{8,24},{16,0},{24,8},{1,17},{9,25},{17,1},{25,9},{2,18},{10... | collective-permute-start | bytes 786440 | tf_op jit(solution)/shard_map/ppermute | solution.py:20
  72.2 7.8 %collective-permute-start.16 = (bf16[512,128]{1,0:T(8,128)(2,1)S(1)}, bf16[512,128]{1,0:T(8,128)(2,1)S(1)}, u32[]{:S(2)}, u32[]{:S(2)}) collective-permute-start(bf16[512,128]{1,0:T(8,128)(2,1)S(1)} %constant_dynamic-slice_fusion), channel_id=1, source_target_pairs={{0,32},{32,0},{1,33},{33,1},{2,34},{34,2},{3,35},{35,3},{4,36},{36... | collective-permute-start | bytes 393224 | tf_op jit(solution)/shard_map/ppermute | solution.py:20
  77.4 5.6 %copy-start.1 = (f32[512,2048]{1,0:T(8,128)S(1)}, f32[512,2048]{1,0:T(8,128)}, u32[]{:S(2)}) copy-start(f32[512,2048]{1,0:T(8,128)} %copy-done) | copy-start | bytes 12582916
  85.2 21.3 %collective-permute-start.17 = (bf16[512,256]{0,1:T(8,128)(2,1)S(1)}, bf16[512,256]{0,1:T(8,128)(2,1)S(1)}, u32[]{:S(2)}, u32[]{:S(2)}) collective-permute-start(bf16[512,256]{0,1:T(8,128)(2,1)S(1)} %get-tuple-element.32), channel_id=1, source_target_pairs={{1,0},{2,1},{3,2},{5,4},{6,5},{7,6},{9,8},{10,9},{11,10},{13,12},{... | collective-permute-start | bytes 786440 | tf_op jit(solution)/shard_map/ppermute | solution.py:24
  87.7 46.4 %collective-permute-start.10 = (bf16[4,128,768]{2,1,0:T(8,128)(2,1)}, bf16[4,128,768]{2,1,0:T(8,128)(2,1)S(1)}, u32[]{:S(2)}, u32[]{:S(2)}) collective-permute-start(bf16[4,128,768]{2,1,0:T(8,128)(2,1)} %fusion.8), channel_id=1, source_target_pairs={{0,192},{64,0},{128,64},{192,128},{1,193},{65,1},{129,65},{193,129... | collective-permute-start | bytes 2359304 | tf_op jit(solution)/shard_map/ppermute | solution.py:20
  90.4 43.7 %collective-permute-start.11 = (bf16[4,128,768]{2,1,0:T(8,128)(2,1)}, bf16[4,128,768]{2,1,0:T(8,128)(2,1)}, u32[]{:S(2)}, u32[]{:S(2)}) collective-permute-start(bf16[4,128,768]{2,1,0:T(8,128)(2,1)} %fusion.8), channel_id=1, source_target_pairs={{0,128},{64,192},{128,0},{192,64},{1,129},{65,193},{129,1},{193,65... | collective-permute-start | bytes 2359304 | tf_op jit(solution)/shard_map/ppermute | solution.py:20
  90.8 43.3 %collective-permute-start.12 = (bf16[4,128,768]{2,1,0:T(8,128)(2,1)}, bf16[4,128,768]{2,1,0:T(8,128)(2,1)}, u32[]{:S(2)}, u32[]{:S(2)}) collective-permute-start(bf16[4,128,768]{2,1,0:T(8,128)(2,1)} %fusion.8), channel_id=1, source_target_pairs={{0,64},{64,128},{128,192},{192,0},{1,65},{65,129},{129,193},{193,1... | collective-permute-start | bytes 2359304 | tf_op jit(solution)/shard_map/ppermute | solution.py:20
  91.7 21.3 %collective-permute-start.19 = (bf16[512,256]{0,1:T(8,128)(2,1)S(1)}, bf16[512,256]{0,1:T(8,128)(2,1)S(1)}, u32[]{:S(2)}, u32[]{:S(2)}) collective-permute-start(bf16[512,256]{0,1:T(8,128)(2,1)S(1)} %get-tuple-element.33), channel_id=1, source_target_pairs={{3,0},{7,4},{11,8},{15,12},{19,16},{23,20},{27,24},{31,28},{35,32}... | collective-permute-start | bytes 786440 | tf_op jit(solution)/shard_map/ppermute | solution.py:24
  106.5 25.9 %collective-permute-start.18 = (bf16[512,256]{0,1:T(8,128)(2,1)S(1)}, bf16[512,256]{0,1:T(8,128)(2,1)S(1)}, u32[]{:S(2)}, u32[]{:S(2)}) collective-permute-start(bf16[512,256]{0,1:T(8,128)(2,1)S(1)} %get-tuple-element.34), channel_id=1, source_target_pairs={{2,0},{3,1},{6,4},{7,5},{10,8},{11,9},{14,12},{15,13},{18,16},{19,... | collective-permute-start | bytes 786440 | tf_op jit(solution)/shard_map/ppermute | solution.py:24
  154.0 4.0 %copy-start.2 = (bf16[32768,128]{1,0:T(8,128)(2,1)S(1)}, bf16[32768,128]{1,0:T(8,128)(2,1)}, u32[]{:S(2)}) copy-start(bf16[32768,128]{1,0:T(8,128)(2,1)} %all-gather.3.cloned.1.call-done) | copy-start | bytes 25165828
Sparse Core Ops, SparseCore 0:
  56.9 97.0 all-gather.2
